TPU v7x, 32 devices: a whole 2x2x4 slice. The times are simulated.
32 devices in a mesh: shift: 4 (over y, x), rows: 8 (over z, core).
Axes of the slice: x: 2, y: 2, z: 4, core: 2. Of those that a mesh axis runs over, the one named last changes fastest.
Arguments:
- filtered: bfloat16 [4, 131072, 256], P('shift', 'rows'), as said below
- weights: float32 [4, 256], P('shift'), may hold values from 0.25 to 2
Outputs:
- basis: float32 [131072, 256], P(('rows', 'shift'))
- r_factor: float32 [256, 256], replicated
Inputs may be any that keep to these rules, and one draw needn't show every extreme that they name: Each filtered block is of full rank.
All inputs are finite; a program needn't handle non-finite values.
Results may differ from a plain program's by a relative error of at most 0.0003.
Values sent between devices are 32-bit elements; how exact they have to be, the bound alone decides.
No kernel may reach another device: no remote copies, remote signals or barrier semaphores. Data moves between devices by JAX's collectives and lax.ppermute only.
A program may use at most 128 MiB of HBM per device.

v0:
```python
import jax
import jax.numpy as jnp
from jax import lax
from jax.sharding import PartitionSpec as P


def cross_products(left, right):
    return jnp.dot(
        left.T, right, precision=lax.Precision.HIGHEST, preferred_element_type=jnp.float32
    )


def shards(filtered, weights):
    weighted = filtered[0].astype(jnp.float32) * weights[0][None, :]
    mixed = lax.psum_scatter(weighted, "shift", scatter_dimension=0, tiled=True)
    devices_all = lax.axis_size(("shift", "rows"))
    total_rows = mixed.shape[0] * devices_all
    gram = cross_products(mixed, mixed) / total_rows
    lower = jnp.linalg.cholesky(lax.psum(gram, ("shift", "rows")))
    basis = jax.scipy.linalg.solve_triangular(lower, mixed.T, lower=True).T
    return (basis, lower.T)


def solution(mesh):
    in_specs = (P("shift", "rows", None), P("shift", None))
    out_specs = (P(("rows", "shift"), None), P())
    return jax.shard_map(shards, mesh=mesh, in_specs=in_specs, out_specs=out_specs, check_vma=False)
```

profile of v0, /device:TPU:0, one launch (start us, length us, event | category | flops | bytes accessed | tf_op | source)
XLA Modules:
  0.0 396.4 jit_solution(7916319687444031821)
XLA Ops:
  7.2 0.0 reduce-scatter.2.cloned.1.call-start
  7.2 9.6 %convert_multiply_fusion = f32[16384,256]{1,0:T(8,128)} fusion(bf16[1,16384,256]{2,1,0:T(8,128)(2,1)} %param.2, f32[256]{0:T(256)} %bitcast.44), kind=kLoop, calls=%fused_computation.2 | loop fusion | flops 8388608 | bytes 25166848 | tf_op jit(solution)/shard_map/mul | solution.py:14
  16.8 0.0 reduce-scatter.2.cloned.1.call-update
  16.8 0.0 all-reduce.3.cloned.1.call-start
  16.9 156.7 %reduce-scatter.2.cloned.1.call-done = f32[4096,256]{1,0:T(8,128)} async-done(((f32[16384,256]{1,0:T(8,128)}), f32[4096,256]{1,0:T(8,128)}) %reduce-scatter.2.cloned.1.call-update) | async-done | bytes 4194320 | tf_op jit(solution)/shard_map/reduce_scatter | solution.py:15
  173.5 10.9 %convolution_multiply_fusion = f32[256,256]{0,1:T(8,128)} fusion(f32[4096,256]{1,0:T(8,128)} %reduce-scatter.2.cloned.1.call-done), kind=kOutput, calls=%fused_computation.7 | convolution fusion | flops 3221291008 | bytes 4456448 | tf_op jit(solution)/shard_map/dot_general | solution.py:8
  184.4 0.0 all-reduce.3.cloned.1.call-update
  184.5 125.1 %all-reduce.3.cloned.1.call-done = f32[256,256]{0,1:T(8,128)} async-done(((f32[256,256]{0,1:T(8,128)}), f32[256,256]{0,1:T(8,128)}) %all-reduce.3.cloned.1.call-update) | async-done | bytes 262160 | tf_op jit(solution)/shard_map/psum | solution.py:19
  309.6 1.1 copy.5
  310.7 1.0 fusion.2
  311.7 11.7 %cholesky.50 = f32[128,128]{1,0:T(8,128)S(1)} custom-call(f32[128,128]{1,0:T(8,128)S(1)} %cholesky.118), custom_call_target="Cholesky" | custom-call | tf_op jit(solution)/shard_map/jit(cholesky)/cholesky | solution.py:19
  323.4 10.0 %custom-call.15 = f32[1,128,128]{1,2,0:T(8,128)S(1)} custom-call(f32[1,128,128]{2,1,0:T(8,128)S(1)} %get-tuple-element.27), custom_call_target="InvertDiagBlocksLowerTriangular" | custom-call | tf_op jit(solution)/shard_map/jit(cholesky)/cholesky | solution.py:19
  333.4 0.2 constant_dynamic-update-slice_fusion.1
  333.7 0.3 convolution_subtract_fusion.1
  333.9 11.7 %cholesky.105 = f32[128,128]{1,0:T(8,128)S(1)} custom-call(f32[128,128]{1,0:T(8,128)S(1)} %convolution_subtract_fusion.1), custom_call_target="Cholesky" | custom-call | tf_op jit(solution)/shard_map/jit(cholesky)/cholesky | solution.py:19
  345.7 0.7 compare_reduce_fusion
  347.8 0.1 triangular_solve.57
  347.9 4.1 %while.1 = (s32[]{:T(128)}, f32[256,256]{1,0:T(8,128)S(1)}, s32[2,2]{1,0:T(2,128)S(1)}, f32[2,128,128]{2,1,0:T(8,128)S(1)}, s32[]{:T(128)}) while((s32[]{:T(128)}, f32[256,256]{1,0:T(8,128)S(1)}, s32[2,2]{1,0:T(2,128)S(1)}, f32[2,128,128]{2,1,0:T(8,128)S(1)}, s32[]{:T(128)}) %tuple.29), condition=%wide.while_cond, body=%wide.while_body.sunk | while | flops 2 | bytes 131181 | solution.py:20
  347.9 0.6 fusion.18
  348.5 1.4 bitcast_dynamic-update-slice_fusion.2
  349.9 0.6 fusion.18
  350.5 1.4 bitcast_dynamic-update-slice_fusion.2
  352.0 19.7 %custom-call.16 = f32[2,128,128]{1,2,0:T(8,128)S(1)} custom-call(f32[2,128,128]{2,1,0:T(8,128)S(1)} %get-tuple-element.9), custom_call_target="InvertDiagBlocksLowerTriangular" | custom-call | tf_op jit(solution)/shard_map/jit(_solve_triangular)/triangular_solve | solution.py:20
  371.6 0.0 copy-start
  371.6 3.7 fusion
  375.3 0.0 copy-done
  375.3 3.4 convolution_subtract_fusion
  378.8 2.0 fusion.6
  380.8 2.4 maximum_bitcast_fusion
  383.2 5.6 %copy.6 = f32[4096,256]{1,0:T(8,128)} copy(f32[4096,256]{0,1:T(8,128)} %maximum_bitcast_fusion) | data formatting | bytes 8388608
  388.8 0.8 copy.7
  (9 shorter events, 0.2 us)
Async XLA Ops:
  7.2 166.4 %reduce-scatter.2.cloned.1.call-start = ((), (), s32[]{:S(2)}) async-start(), calls=%async_computation.1 | async-start | bytes 20971520 | tf_op jit(solution)/shard_map/reduce_scatter | solution.py:15
  16.8 292.8 %all-reduce.3.cloned.1.call-start = ((), (), s32[]{:S(2)}) async-start(), calls=%async_computation.2 | async-start | bytes 524288 | tf_op jit(solution)/shard_map/psum | solution.py:19
  371.6 3.7 copy-start
Sparse Core Ops, SparseCore 0:
  17.0 156.5 reduce-scatter.1
  184.6 124.9 all-reduce.2
where the time goes:
time: 397 us; the launch traced here: 396 us
  waiting for transfers between devices  282 us (71%)
  other arithmetic  66.9 us (17%)
  matrix products  20.5 us (5%)
  between operations  15.5 us (4%)
  local copies, waits for them, and re-layouts  11.7 us (3%)
    reduce_scatter x1, waiting for transfers between devices, shards(): mixed = lax.psum_scatter(weighted, 'shift', scatter_dimension=0, tiled=True)  157 us
    psum x1, waiting for transfers between devices, shards(): lower = jnp.linalg.cholesky(lax.psum(gram, ('shift', 'rows')))  125 us
    another operation x6, other arithmetic, shards(): lower = jnp.linalg.cholesky(lax.psum(gram, ('shift', 'rows')))  34.2 us
    another operation x2, other arithmetic, shards(): basis = jax.scipy.linalg.solve_triangular(lower, mixed.T, lower=True).T  19.7 us
    dot_general x1, matrix products, cross_products(): jnp.dot(left.T, right, precision=lax.Precision.HIGHEST, preferred_element...  10.9 us
    mul x1, other arithmetic, shards(): weighted = filtered[0].astype(jnp.float32) * weights[0][None, :]  9.6 us
    another operation x3, matrix products, shards(): basis = jax.scipy.linalg.solve_triangular(lower, mixed.T, lower=True).T  9.09 us
  transfers between devices with their start and end apart: 2, of which 2 were waited for; matrix products, arithmetic and copies ran while one was open for 0% of the time, Pallas kernels for 0%

commit v1 on v0

--- a/solution.py
+++ b/solution.py
@@ -10,13 +10,23 @@
     )
 
 
+def butterfly_sum(x, axes):
+    size = lax.axis_size(axes)
+    bit = 1
+    while bit < size:
+        pairs = [(i, i ^ bit) for i in range(size)]
+        x = x + lax.ppermute(x, axes, pairs)
+        bit *= 2
+    return x
+
+
 def shards(filtered, weights):
     weighted = filtered[0].astype(jnp.float32) * weights[0][None, :]
     mixed = lax.psum_scatter(weighted, "shift", scatter_dimension=0, tiled=True)
     devices_all = lax.axis_size(("shift", "rows"))
     total_rows = mixed.shape[0] * devices_all
     gram = cross_products(mixed, mixed) / total_rows
-    lower = jnp.linalg.cholesky(lax.psum(gram, ("shift", "rows")))
+    lower = jnp.linalg.cholesky(butterfly_sum(gram, ("shift", "rows")))
     basis = jax.scipy.linalg.solve_triangular(lower, mixed.T, lower=True).T
     return (basis, lower.T)
 

time: 397 us -> 307 us (0.77)
  waiting for transfers between devices: 282 us -> 188 us
  starting transfers between devices: 0.08 us -> 6.94 us
    psum x1 -> x0, waiting for transfers between devices: 125 us -> none  [shards(): lower = jnp.linalg.cholesky(lax.psum(gram, ('shift', 'rows')))]
    ppermute x0 -> x5, waiting for transfers between devices: none -> 30.9 us  [butterfly_sum(): x = x + lax.ppermute(x, axes, pairs)]
    ppermute x0 -> x5, starting transfers between devices: none -> 6.9 us  [butterfly_sum(): x = x + lax.ppermute(x, axes, pairs)]
  transfers between devices with their start and end apart: 2 -> 6, of which waited for: 2 -> 6; matrix products, arithmetic and copies ran while one was open for 0% -> 0% of each run, Pallas kernels for 0% -> 0%
where the time goes in v1:
time: 307 us
  waiting for transfers between devices  188 us (61%)
  other arithmetic  66.1 us (22%)
  matrix products  20 us (7%)
  between operations  15.5 us (5%)
  local copies, waits for them, and re-layouts  10.6 us (3%)
  starting transfers between devices  6.94 us (2%)
    reduce_scatter x1, waiting for transfers between devices, shards(): mixed = lax.psum_scatter(weighted, 'shift', scatter_dimension=0, tiled=True)  157 us
    another operation x6, other arithmetic, shards(): lower = jnp.linalg.cholesky(butterfly_sum(gram, ('shift', 'rows')))  34 us
    ppermute x5, waiting for transfers between devices, butterfly_sum(): x = x + lax.ppermute(x, axes, pairs)  30.9 us
    another operation x2, other arithmetic, shards(): basis = jax.scipy.linalg.solve_triangular(lower, mixed.T, lower=True).T  19.9 us
    dot_general x1, matrix products, cross_products(): jnp.dot(left.T, right, precision=lax.Precision.HIGHEST, preferred_element...  10.4 us
    mul x1, other arithmetic, shards(): weighted = filtered[0].astype(jnp.float32) * weights[0][None, :]  9.59 us
    another operation x3, matrix products, shards(): basis = jax.scipy.linalg.solve_triangular(lower, mixed.T, lower=True).T  9.09 us
    ppermute x5, starting transfers between devices, butterfly_sum(): x = x + lax.ppermute(x, axes, pairs)  6.9 us
  transfers between devices with their start and end apart: 6, of which 6 were waited for; matrix products, arithmetic and copies ran while one was open for 0% of the time, Pallas kernels for 0%

profile of v1, /device:TPU:0, one launch (start us, length us, event | category | flops | bytes accessed | tf_op | source)
XLA Modules:
  0.0 306.8 jit_solution(10274207014774629932)
XLA Ops:
  7.2 0.0 reduce-scatter.2.cloned.1.call-start
  7.2 9.6 %convert_multiply_fusion = f32[16384,256]{1,0:T(8,128)} fusion(bf16[1,16384,256]{2,1,0:T(8,128)(2,1)} %param.2, f32[256]{0:T(256)} %bitcast.44), kind=kLoop, calls=%fused_computation.2 | loop fusion | flops 8388608 | bytes 25166848 | tf_op jit(solution)/shard_map/mul | solution.py:24
  16.8 0.0 reduce-scatter.2.cloned.1.call-update
  16.8 156.7 %reduce-scatter.2.cloned.1.call-done = f32[4096,256]{1,0:T(8,128)} async-done(((f32[16384,256]{1,0:T(8,128)}), f32[4096,256]{1,0:T(8,128)}) %reduce-scatter.2.cloned.1.call-update) | async-done | bytes 4194320 | tf_op jit(solution)/shard_map/reduce_scatter | solution.py:25
  173.5 10.4 %convolution_multiply_fusion = f32[256,256]{0,1:T(8,128)S(1)} fusion(f32[4096,256]{1,0:T(8,128)} %reduce-scatter.2.cloned.1.call-done), kind=kOutput, calls=%fused_computation.7 | convolution fusion | flops 3221291008 | bytes 4456448 | tf_op jit(solution)/shard_map/dot_general | solution.py:8
  183.9 0.1 collective-permute-start
  184.0 1.5 collective-permute-done
  185.6 1.6 collective-permute-start.1
  187.1 6.9 %collective-permute-done.1 = f32[256,256]{0,1:T(8,128)S(1)} collective-permute-done((f32[256,256]{0,1:T(8,128)S(1)}, f32[256,256]{0,1:T(8,128)S(1)}, u32[]{:S(2)}, u32[]{:S(2)}) %collective-permute-start.1) | collective-permute-done | bytes 262176 | tf_op jit(solution)/shard_map/ppermute | solution.py:18
  194.0 2.5 collective-permute-start.2
  196.5 11.7 %collective-permute-done.2 = f32[256,256]{0,1:T(8,128)S(1)} collective-permute-done((f32[256,256]{0,1:T(8,128)S(1)}, f32[256,256]{0,1:T(8,128)S(1)}, u32[]{:S(2)}, u32[]{:S(2)}) %collective-permute-start.2) | collective-permute-done | bytes 262176 | tf_op jit(solution)/shard_map/ppermute | solution.py:18
  208.2 1.4 collective-permute-start.3
  209.6 5.9 %collective-permute-done.3 = f32[256,256]{0,1:T(8,128)S(1)} collective-permute-done((f32[256,256]{0,1:T(8,128)S(1)}, f32[256,256]{0,1:T(8,128)S(1)}, u32[]{:S(2)}, u32[]{:S(2)}) %collective-permute-start.3) | collective-permute-done | bytes 262176 | tf_op jit(solution)/shard_map/ppermute | solution.py:18
  215.5 1.4 collective-permute-start.4
  216.9 5.0 %collective-permute-done.4 = f32[256,256]{0,1:T(8,128)S(1)} collective-permute-done((f32[256,256]{0,1:T(8,128)S(1)}, f32[256,256]{0,1:T(8,128)S(1)}, u32[]{:S(2)}, u32[]{:S(2)}) %collective-permute-start.4) | collective-permute-done | bytes 262176 | tf_op jit(solution)/shard_map/ppermute | solution.py:18
  222.0 0.1 copy.5
  222.2 11.7 %cholesky.50 = f32[128,128]{1,0:T(8,128)S(1)} custom-call(f32[128,128]{1,0:T(8,128)S(1)} %cholesky.118), custom_call_target="Cholesky" | custom-call | tf_op jit(solution)/shard_map/jit(cholesky)/cholesky | solution.py:29
  234.0 9.8 %custom-call.15 = f32[1,128,128]{1,2,0:T(8,128)S(1)} custom-call(f32[1,128,128]{2,1,0:T(8,128)S(1)} %get-tuple-element.27), custom_call_target="InvertDiagBlocksLowerTriangular" | custom-call | tf_op jit(solution)/shard_map/jit(cholesky)/cholesky | solution.py:29
  243.8 0.2 constant_dynamic-update-slice_fusion.1
  244.0 0.3 slice_subtract_fusion
  244.2 11.7 %cholesky.105 = f32[128,128]{1,0:T(8,128)S(1)} custom-call(f32[128,128]{1,0:T(8,128)S(1)} %slice_subtract_fusion), custom_call_target="Cholesky" | custom-call | tf_op jit(solution)/shard_map/jit(cholesky)/cholesky | solution.py:29
  256.0 0.7 compare_reduce_fusion
  258.0 0.1 triangular_solve.57
  258.1 4.0 %while.1 = (s32[]{:T(128)}, f32[256,256]{1,0:T(8,128)S(1)}, s32[2,2]{1,0:T(2,128)S(1)}, f32[2,128,128]{2,1,0:T(8,128)S(1)}, s32[]{:T(128)}) while((s32[]{:T(128)}, f32[256,256]{1,0:T(8,128)S(1)}, s32[2,2]{1,0:T(2,128)S(1)}, f32[2,128,128]{2,1,0:T(8,128)S(1)}, s32[]{:T(128)}) %tuple.29), condition=%wide.while_cond, body=%wide.while_body.sunk | while | flops 2 | bytes 131181 | solution.py:30
  258.1 0.6 fusion.18
  258.7 1.4 bitcast_dynamic-update-slice_fusion.2
  260.1 0.6 fusion.18
  260.7 1.4 bitcast_dynamic-update-slice_fusion.2
  262.0 19.9 %custom-call.16 = f32[2,128,128]{1,2,0:T(8,128)S(1)} custom-call(f32[2,128,128]{2,1,0:T(8,128)S(1)} %get-tuple-element.9), custom_call_target="InvertDiagBlocksLowerTriangular" | custom-call | tf_op jit(solution)/shard_map/jit(_solve_triangular)/triangular_solve | solution.py:30
  281.9 0.0 copy-start
  282.0 3.7 %fusion = f32[128,4096]{1,0:T(8,128)S(1)} fusion(f32[256,4096]{0,1:T(8,128)} %bitcast.42, f32[2,128,128]{1,2,0:T(8,128)S(1)} %custom-call.16), kind=kOutput, calls=%fused_computation.5 | convolution fusion | flops 805306368 | bytes 4259840 | tf_op jit(solution)/shard_map/jit(_solve_triangular)/triangular_solve | solution.py:30
  285.6 0.0 copy-done
  285.7 3.4 %convolution_subtract_fusion = f32[128,4096]{0,1:T(8,128)S(1)} fusion(f32[128,4096]{1,0:T(8,128)S(1)} %fusion, f32[256,4096]{0,1:T(8,128)S(1)} %bitcast.43, f32[256,256]{1,0:T(8,128)S(1)} %get-tuple-element.80), kind=kOutput, calls=%fused_computation.3 | convolution fusion | flops 805830656 | bytes 6356992 | tf_op jit(solution)/shard_map/jit(_solve_triangular)/triangular_solve | solution.py:30
  289.1 2.0 fusion.6
  291.1 2.4 maximum_bitcast_fusion
  293.5 5.6 %copy.6 = f32[4096,256]{1,0:T(8,128)} copy(f32[4096,256]{0,1:T(8,128)} %maximum_bitcast_fusion) | data formatting | bytes 8388608
  299.1 0.8 copy.7
  (15 shorter events, 0.4 us)
Async XLA Ops:
  7.2 166.4 %reduce-scatter.2.cloned.1.call-start = ((), (), s32[]{:S(2)}) async-start(), calls=%async_computation.1 | async-start | bytes 20971520 | tf_op jit(solution)/shard_map/reduce_scatter | solution.py:25
  183.9 1.6 collective-permute-start
  185.6 8.4 %collective-permute-start.1 = (f32[256,256]{0,1:T(8,128)S(1)}, f32[256,256]{0,1:T(8,128)S(1)}, u32[]{:S(2)}, u32[]{:S(2)}) collective-permute-start(f32[256,256]{0,1:T(8,128)S(1)} %add.40), channel_id=1, source_target_pairs={{0,2},{1,3},{2,0},{3,1},{4,6},{5,7},{6,4},{7,5},{8,10},{9,11},{10,... | collective-permute-start | bytes 786440 | tf_op jit(solution)/shard_map/ppermute | solution.py:18
  194.0 14.1 %collective-permute-start.2 = (f32[256,256]{0,1:T(8,128)S(1)}, f32[256,256]{0,1:T(8,128)S(1)}, u32[]{:S(2)}, u32[]{:S(2)}) collective-permute-start(f32[256,256]{0,1:T(8,128)S(1)} %add.41), channel_id=1, source_target_pairs={{0,4},{1,5},{2,6},{3,7},{4,0},{5,1},{6,2},{7,3},{8,12},{9,13},{10,... | collective-permute-start | bytes 786440 | tf_op jit(solution)/shard_map/ppermute | solution.py:18
  208.2 7.3 %collective-permute-start.3 = (f32[256,256]{0,1:T(8,128)S(1)}, f32[256,256]{0,1:T(8,128)S(1)}, u32[]{:S(2)}, u32[]{:S(2)}) collective-permute-start(f32[256,256]{0,1:T(8,128)S(1)} %add.42), channel_id=1, source_target_pairs={{0,8},{1,9},{2,10},{3,11},{4,12},{5,13},{6,14},{7,15},{8,0},{9,1},... | collective-permute-start | bytes 786440 | tf_op jit(solution)/shard_map/ppermute | solution.py:18
  215.5 6.4 %collective-permute-start.4 = (f32[256,256]{0,1:T(8,128)S(1)}, f32[256,256]{0,1:T(8,128)S(1)}, u32[]{:S(2)}, u32[]{:S(2)}) collective-permute-start(f32[256,256]{0,1:T(8,128)S(1)} %add.43), channel_id=1, source_target_pairs={{0,16},{1,17},{2,18},{3,19},{4,20},{5,21},{6,22},{7,23},{8,24},{9,... | collective-permute-start | bytes 786440 | tf_op jit(solution)/shard_map/ppermute | solution.py:18
  281.9 3.7 %copy-start = (f32[4096,256]{1,0:T(8,128)S(1)}, f32[4096,256]{1,0:T(8,128)}, u32[]{:S(2)}) copy-start(f32[4096,256]{1,0:T(8,128)} %reduce-scatter.2.cloned.1.call-done) | copy-start | bytes 12582916
Sparse Core Ops, SparseCore 0:
  16.9 156.5 reduce-scatter.1

commit v2 on v1

v2 whole, which is shorter than its diff:
```python
import jax
import jax.numpy as jnp
from jax import lax
from jax.experimental import pallas as pl
from jax.experimental.pallas import tpu as pltpu
from jax.sharding import PartitionSpec as P

HIGHEST = lax.Precision.HIGHEST


def cross_products(left, right):
    return jnp.dot(left.T, right, precision=HIGHEST, preferred_element_type=jnp.float32)


def butterfly_sum(x, axes):
    size = lax.axis_size(axes)
    bit = 1
    while bit < size:
        pairs = [(i, i ^ bit) for i in range(size)]
        x = x + lax.ppermute(x, axes, pairs)
        bit *= 2
    return x


def dot(a, b):
    return jnp.dot(a, b, precision=HIGHEST, preferred_element_type=jnp.float32)


def leaf_factor(a, work):
    n = a.shape[0]
    rows = lax.broadcasted_iota(jnp.int32, (n, 2 * n), 0)
    cols = lax.broadcasted_iota(jnp.int32, (n, 2 * n), 1)
    work[...] = jnp.where(cols < n, jnp.concatenate([a, a], axis=1), (cols - n == rows).astype(jnp.float32))
    row_index = lax.broadcasted_iota(jnp.int32, (n, 1), 0)
    lane_index = lax.broadcasted_iota(jnp.int32, (1, n), 1)

    def step(j, carry):
        row = work[pl.ds(j, 1), :]
        pivot = jnp.sum(jnp.where(lane_index == j, row[:, :n], 0.0), axis=1, keepdims=True)
        scale = 1.0 / jnp.sqrt(pivot)
        scaled = row * scale
        current = work[...]
        column = jnp.sum(jnp.where(lane_index == j, current[:, :n], 0.0), axis=1, keepdims=True)
        coef = jnp.where(row_index > j, column * scale, 0.0)
        work[...] = current - coef * scaled
        work[pl.ds(j, 1), :] = scaled
        return carry

    lax.fori_loop(0, n, step, 0)
    result = work[...]
    upper = jnp.where(cols[:, :n] >= rows[:, :n], result[:, :n], 0.0)
    return upper, result[:, n:]


def factor_kernel(gram_ref, r_ref, rinv_ref, work):
    n = gram_ref.shape[0]
    h = n // 2
    g = gram_ref[...]
    r11, l11i = leaf_factor(g[:h, :h], work)
    r12 = dot(l11i, g[:h, h:])
    schur = g[h:, h:] - dot(r12.T, r12)
    r22, l22i = leaf_factor(schur, work)
    r11i = l11i.T
    r22i = l22i.T
    rinv12 = -dot(dot(r11i, r12), r22i)
    zero = jnp.zeros((h, h), jnp.float32)
    r_ref[:h, :h] = r11
    r_ref[:h, h:] = r12
    r_ref[h:, :h] = zero
    r_ref[h:, h:] = r22
    rinv_ref[:h, :h] = r11i
    rinv_ref[:h, h:] = rinv12
    rinv_ref[h:, :h] = zero
    rinv_ref[h:, h:] = r22i


def factor(gram):
    n = gram.shape[0]
    vmem = pl.BlockSpec(memory_space=pltpu.VMEM)
    return pl.pallas_call(
        factor_kernel,
        out_shape=(jax.ShapeDtypeStruct((n, n), jnp.float32), jax.ShapeDtypeStruct((n, n), jnp.float32)),
        in_specs=[vmem],
        out_specs=(vmem, vmem),
        scratch_shapes=[pltpu.VMEM((n // 2, n), jnp.float32)],
    )(gram)


def shards(filtered, weights):
    weighted = filtered[0].astype(jnp.float32) * weights[0][None, :]
    mixed = lax.psum_scatter(weighted, "shift", scatter_dimension=0, tiled=True)
    devices_all = lax.axis_size(("shift", "rows"))
    total_rows = mixed.shape[0] * devices_all
    gram = cross_products(mixed, mixed) / total_rows
    upper, upper_inv = factor(butterfly_sum(gram, ("shift", "rows")))
    basis = dot(mixed, upper_inv)
    return (basis, upper)


def solution(mesh):
    in_specs = (P("shift", "rows", None), P("shift", None))
    out_specs = (P(("rows", "shift"), None), P())
    return jax.shard_map(shards, mesh=mesh, in_specs=in_specs, out_specs=out_specs, check_vma=False)
```

time: 307 us -> 269 us (0.88)
  other arithmetic: 66.1 us -> 10.5 us
  Pallas kernels: 0 us -> 32.1 us
  local copies, waits for them, and re-layouts: 10.6 us -> 0 us
    another operation x8 -> x0, other arithmetic: 53.9 us -> none  [the longest x6 34 us: shards(): lower = jnp.linalg.cholesky(butterfly_sum(gram, ('shift', 'rows')))]
    pallas_call x0 -> x1, Pallas kernels: none -> 32.1 us  [factor(): pl.pallas_call(factor_kernel, out_shape=(jax.ShapeDtypeStruct((n, n), jnp...]
    another operation x5 -> x0, matrix products: 9.56 us -> none  [the longest x3 9.09 us: shards(): basis = jax.scipy.linalg.solve_triangular(lower, mixed.T, lower=True).T]
    dot_general x1 -> x2, matrix products: 10.4 us -> 17.5 us  [the longest x1 9.88 us: cross_products(): jnp.dot(left.T, right, precision=HIGHEST, preferred_element_type=jnp.floa...]
    unnamed x4 -> x0, local copies, waits for them, and re-layouts: 6.43 us -> none
    another operation x9 -> x0, local copies, waits for them, and re-layouts: 4.03 us -> none
where the time goes in v2:
time: 269 us
  waiting for transfers between devices  188 us (70%)
  Pallas kernels  32.1 us (12%)
  matrix products  17.5 us (7%)
  between operations  14.1 us (5%)
  other arithmetic  10.5 us (4%)
  starting transfers between devices  6.94 us (3%)
    reduce_scatter x1, waiting for transfers between devices, shards(): mixed = lax.psum_scatter(weighted, 'shift', scatter_dimension=0, tiled=True)  157 us
    pallas_call x1, Pallas kernels, factor(): pl.pallas_call(factor_kernel, out_shape=(jax.ShapeDtypeStruct((n, n), jnp...  32.1 us
    ppermute x5, waiting for transfers between devices, butterfly_sum(): x = x + lax.ppermute(x, axes, pairs)  30.9 us
    dot_general x1, matrix products, cross_products(): jnp.dot(left.T, right, precision=HIGHEST, preferred_element_type=jnp.floa...  9.88 us
    mul x1, other arithmetic, shards(): weighted = filtered[0].astype(jnp.float32) * weights[0][None, :]  9.59 us
    dot_general x1, matrix products, dot(): return jnp.dot(a, b, precision=HIGHEST, preferred_element_type=jnp.float32)  7.65 us
    ppermute x5, starting transfers between devices, butterfly_sum(): x = x + lax.ppermute(x, axes, pairs)  6.9 us
  transfers between devices with their start and end apart: 6, of which 6 were waited for; matrix products, arithmetic and copies ran while one was open for 0% of the time, Pallas kernels for 0%

profile of v2, /device:TPU:0, one launch (start us, length us, event | category | flops | bytes accessed | tf_op | source)
XLA Modules:
  0.0 268.8 jit_solution(6094478851898482909)
XLA Ops:
  7.2 0.0 reduce-scatter.2.cloned.1.call-start
  7.2 9.6 %convert_multiply_fusion = f32[16384,256]{1,0:T(8,128)} fusion(bf16[1,16384,256]{2,1,0:T(8,128)(2,1)} %param.2, f32[256]{0:T(256)} %bitcast.8), kind=kLoop, calls=%fused_computation | loop fusion | flops 8388608 | bytes 25166848 | tf_op jit(solution)/shard_map/mul | solution.py:90
  16.8 0.0 reduce-scatter.2.cloned.1.call-update
  16.8 156.7 %reduce-scatter.2.cloned.1.call-done = f32[4096,256]{1,0:T(8,128)} async-done(((f32[16384,256]{1,0:T(8,128)}), f32[4096,256]{1,0:T(8,128)}) %reduce-scatter.2.cloned.1.call-update) | async-done | bytes 4194320 | tf_op jit(solution)/shard_map/reduce_scatter | solution.py:91
  173.5 9.9 %convolution_multiply_fusion = f32[256,256]{1,0:T(8,128)S(1)} fusion(f32[4096,256]{1,0:T(8,128)} %reduce-scatter.2.cloned.1.call-done), kind=kOutput, calls=%fused_computation.1 | convolution fusion | flops 3221291008 | bytes 4456448 | tf_op jit(solution)/shard_map/dot_general | solution.py:12
  183.4 0.1 collective-permute-start
  183.5 1.5 collective-permute-done
  185.1 1.6 collective-permute-start.1
  186.6 6.9 %collective-permute-done.1 = f32[256,256]{1,0:T(8,128)S(1)} collective-permute-done((f32[256,256]{1,0:T(8,128)S(1)}, f32[256,256]{1,0:T(8,128)S(1)}, u32[]{:S(2)}, u32[]{:S(2)}) %collective-permute-start.1) | collective-permute-done | bytes 262176 | tf_op jit(solution)/shard_map/ppermute | solution.py:20
  193.5 2.4 collective-permute-start.2
  196.0 11.7 %collective-permute-done.2 = f32[256,256]{1,0:T(8,128)S(1)} collective-permute-done((f32[256,256]{1,0:T(8,128)S(1)}, f32[256,256]{1,0:T(8,128)S(1)}, u32[]{:S(2)}, u32[]{:S(2)}) %collective-permute-start.2) | collective-permute-done | bytes 262176 | tf_op jit(solution)/shard_map/ppermute | solution.py:20
  207.6 1.4 collective-permute-start.3
  209.1 5.9 %collective-permute-done.3 = f32[256,256]{1,0:T(8,128)S(1)} collective-permute-done((f32[256,256]{1,0:T(8,128)S(1)}, f32[256,256]{1,0:T(8,128)S(1)}, u32[]{:S(2)}, u32[]{:S(2)}) %collective-permute-start.3) | collective-permute-done | bytes 262176 | tf_op jit(solution)/shard_map/ppermute | solution.py:20
  215.0 1.4 collective-permute-start.4
  216.4 5.0 %collective-permute-done.4 = f32[256,256]{1,0:T(8,128)S(1)} collective-permute-done((f32[256,256]{1,0:T(8,128)S(1)}, f32[256,256]{1,0:T(8,128)S(1)}, u32[]{:S(2)}, u32[]{:S(2)}) %collective-permute-start.4) | collective-permute-done | bytes 262176 | tf_op jit(solution)/shard_map/ppermute | solution.py:20
  221.4 0.7 add.21.gram_ref
  222.2 32.1 %shard_map.41 = (f32[256,256]{1,0:T(8,128)}, f32[256,256]{1,0:T(8,128)}) custom-call(f32[256,256]{1,0:T(8,128)} %add.21.gram_ref), custom_call_target="tpu_custom_call" | custom-call | tf_op jit(solution)/shard_map/pallas_call | solution.py:80
  254.3 7.6 %fusion = f32[4096,256]{1,0:T(8,128)} fusion(f32[4096,256]{1,0:T(8,128)} %reduce-scatter.2.cloned.1.call-done, f32[256,256]{1,0:T(8,128)} %get-tuple-element.4), kind=kOutput, calls=%fused_computation.2 | convolution fusion | flops 3221225472 | bytes 8650752 | tf_op jit(solution)/shard_map/dot_general | solution.py:26
  (4 shorter events, 0.1 us)
Async XLA Ops:
  7.2 166.4 %reduce-scatter.2.cloned.1.call-start = ((), (), s32[]{:S(2)}) async-start(), calls=%async_computation.1 | async-start | bytes 20971520 | tf_op jit(solution)/shard_map/reduce_scatter | solution.py:91
  183.4 1.6 collective-permute-start
  185.1 8.4 %collective-permute-start.1 = (f32[256,256]{1,0:T(8,128)S(1)}, f32[256,256]{1,0:T(8,128)S(1)}, u32[]{:S(2)}, u32[]{:S(2)}) collective-permute-start(f32[256,256]{1,0:T(8,128)S(1)} %add.17), channel_id=1, source_target_pairs={{0,2},{1,3},{2,0},{3,1},{4,6},{5,7},{6,4},{7,5},{8,10},{9,11},{10,... | collective-permute-start | bytes 786440 | tf_op jit(solution)/shard_map/ppermute | solution.py:20
  193.5 14.1 %collective-permute-start.2 = (f32[256,256]{1,0:T(8,128)S(1)}, f32[256,256]{1,0:T(8,128)S(1)}, u32[]{:S(2)}, u32[]{:S(2)}) collective-permute-start(f32[256,256]{1,0:T(8,128)S(1)} %add.18), channel_id=1, source_target_pairs={{0,4},{1,5},{2,6},{3,7},{4,0},{5,1},{6,2},{7,3},{8,12},{9,13},{10,... | collective-permute-start | bytes 786440 | tf_op jit(solution)/shard_map/ppermute | solution.py:20
  207.6 7.3 %collective-permute-start.3 = (f32[256,256]{1,0:T(8,128)S(1)}, f32[256,256]{1,0:T(8,128)S(1)}, u32[]{:S(2)}, u32[]{:S(2)}) collective-permute-start(f32[256,256]{1,0:T(8,128)S(1)} %add.19), channel_id=1, source_target_pairs={{0,8},{1,9},{2,10},{3,11},{4,12},{5,13},{6,14},{7,15},{8,0},{9,1},... | collective-permute-start | bytes 786440 | tf_op jit(solution)/shard_map/ppermute | solution.py:20
  215.0 6.4 %collective-permute-start.4 = (f32[256,256]{1,0:T(8,128)S(1)}, f32[256,256]{1,0:T(8,128)S(1)}, u32[]{:S(2)}, u32[]{:S(2)}) collective-permute-start(f32[256,256]{1,0:T(8,128)S(1)} %add.20), channel_id=1, source_target_pairs={{0,16},{1,17},{2,18},{3,19},{4,20},{5,21},{6,22},{7,23},{8,24},{9,... | collective-permute-start | bytes 786440 | tf_op jit(solution)/shard_map/ppermute | solution.py:20
Sparse Core Ops, SparseCore 0:
  16.9 156.5 reduce-scatter.1

commit v3 on v2

--- a/solution.py
+++ b/solution.py
@@ -9,7 +9,11 @@
 
 
 def cross_products(left, right):
-    return jnp.dot(left.T, right, precision=HIGHEST, preferred_element_type=jnp.float32)
+    return jnp.dot(left.T, right, precision=lax.Precision.HIGH, preferred_element_type=jnp.float32)
+
+
+def dot_high(a, b):
+    return jnp.dot(a, b, precision=lax.Precision.HIGH, preferred_element_type=jnp.float32)
 
 
 def butterfly_sum(x, axes):
@@ -86,14 +90,27 @@
     )(gram)
 
 
+PIECES = 2
+
+
 def shards(filtered, weights):
-    weighted = filtered[0].astype(jnp.float32) * weights[0][None, :]
-    mixed = lax.psum_scatter(weighted, "shift", scatter_dimension=0, tiled=True)
+    shifts = lax.axis_size("shift")
+    rows, width = filtered.shape[1], filtered.shape[2]
+    block = rows // shifts
+    blocks = filtered[0].reshape(shifts, PIECES, block // PIECES, width)
+    mixed_pieces = []
+    gram = None
+    for piece in range(PIECES):
+        weighted = blocks[:, piece].reshape(rows // PIECES, width).astype(jnp.float32) * weights[0][None, :]
+        mixed_piece = lax.psum_scatter(weighted, "shift", scatter_dimension=0, tiled=True)
+        mixed_pieces.append(mixed_piece)
+        part = cross_products(mixed_piece, mixed_piece)
+        gram = part if gram is None else gram + part
+    mixed = jnp.concatenate(mixed_pieces, axis=0)
     devices_all = lax.axis_size(("shift", "rows"))
     total_rows = mixed.shape[0] * devices_all
-    gram = cross_products(mixed, mixed) / total_rows
-    upper, upper_inv = factor(butterfly_sum(gram, ("shift", "rows")))
-    basis = dot(mixed, upper_inv)
+    upper, upper_inv = factor(butterfly_sum(gram / total_rows, ("shift", "rows")))
+    basis = dot_high(mixed, upper_inv)
     return (basis, upper)
 
 

time: 269 us -> 289 us (1.074)
  waiting for transfers between devices: 188 us -> 206 us
  local copies, waits for them, and re-layouts: 0 us -> 5.09 us
  matrix products: 17.5 us -> 13.5 us
    reduce_scatter x1 -> x2, waiting for transfers between devices: 157 us -> 174 us  [shards(): lax.psum_scatter(weighted, 'shift', scatter_dimension=0, tiled=True)]
    slice x0 -> x1, local copies, waits for them, and re-layouts: none -> 5.08 us  [shards(): blocks[:, piece].reshape(rows // PIECES, width).astype(jnp.float32)]
    dot_general x2 -> x3, matrix products: 17.5 us -> 13.5 us  [the longest x2 8.05 us: cross_products(): jnp.dot(left.T, right, precision=lax.Precision.HIGH, preferred_element_ty...]
  transfers between devices with their start and end apart: 6 -> 7, of which waited for: 6 -> 7; matrix products, arithmetic and copies ran while one was open for 0% -> 1% of each run, Pallas kernels for 0% -> 0%
where the time goes in v3:
time: 289 us; the launch traced here: 288 us
  waiting for transfers between devices  206 us (71%)
  Pallas kernels  32.1 us (11%)
  between operations  14.1 us (5%)
  matrix products  13.5 us (5%)
  other arithmetic  10.5 us (4%)
  starting transfers between devices  7.04 us (2%)
  local copies, waits for them, and re-layouts  5.09 us (2%)
    reduce_scatter x2, waiting for transfers between devices, shards(): lax.psum_scatter(weighted, 'shift', scatter_dimension=0, tiled=True)  174 us
    pallas_call x1, Pallas kernels, factor(): pl.pallas_call(factor_kernel, out_shape=(jax.ShapeDtypeStruct((n, n), jnp...  32.1 us
    ppermute x5, waiting for transfers between devices, butterfly_sum(): x = x + lax.ppermute(x, axes, pairs)  30.9 us
    mul x1, other arithmetic, shards(): blocks[:, piece].reshape(rows // PIECES, width).astype(jnp.float32)  9.58 us
    dot_general x2, matrix products, cross_products(): jnp.dot(left.T, right, precision=lax.Precision.HIGH, preferred_element_ty...  8.05 us
    ppermute x5, starting transfers between devices, butterfly_sum(): x = x + lax.ppermute(x, axes, pairs)  6.96 us
  transfers between devices with their start and end apart: 7, of which 7 were waited for; matrix products, arithmetic and copies ran while one was open for 1% of the time, Pallas kernels for 0%

profile of v3, /device:TPU:0, one launch (start us, length us, event | category | flops | bytes accessed | tf_op | source)
XLA Modules:
  0.0 288.1 jit_solution(8936709201730217360)
XLA Ops:
  7.2 0.0 reduce-scatter.3.cloned.1.call-start
  7.2 0.0 copy-start.1
  7.2 5.1 %fusion.6 = (bf16[4,1,2048,256]{3,2,1,0:T(8,128)(2,1)S(1)}, bf16[4,1,2048,256]{3,2,1,0:T(8,128)(2,1)}) fusion(bf16[4,2,2048,256]{3,2,1,0:T(8,128)(2,1)} %bitcast.13), kind=kLoop, calls=%fused_computation.9 | loop fusion | bytes 16777216 | tf_op jit(solution)/shard_map/slice | solution.py:104
  12.3 0.0 copy-done.1
  12.3 9.6 %convert_multiply_fusion = (f32[8192,256]{1,0:T(8,128)}, f32[8192,256]{1,0:T(8,128)}) fusion(bf16[4,1,2048,256]{3,2,1,0:T(8,128)(2,1)S(1)} %get-tuple-element.6, f32[256]{0:T(256)S(1)} %bitcast.14, bf16[4,1,2048,256]{3,2,1,0:T(8,128)(2,1)} %get-tuple-element.7), kind=kLoop, calls=%fused_computation | loop fusion | flops 8388608 | bytes 25166848 | tf_op jit(solution)/shard_map/mul | solution.py:104
  21.9 0.0 reduce-scatter.3.cloned.1.call-update
  21.9 0.0 reduce-scatter.5.cloned.1.call-start
  22.0 0.7 reduce-scatter.5.cloned.1.call-update
  22.7 88.5 %reduce-scatter.3.cloned.1.call-done = f32[2048,256]{1,0:T(8,128)} async-done(((f32[8192,256]{1,0:T(8,128)}), f32[2048,256]{1,0:T(8,128)}) %reduce-scatter.3.cloned.1.call-update) | async-done | bytes 2097168 | tf_op jit(solution)/shard_map/reduce_scatter | solution.py:105
  111.2 4.0 %fusion.7 = f32[256,256]{1,0:T(8,128)S(1)} fusion(f32[2048,256]{1,0:T(8,128)} %reduce-scatter.3.cloned.1.call-done), kind=kOutput, calls=%fused_computation.10 | convolution fusion | flops 805306368 | bytes 2359296 | tf_op jit(solution)/shard_map/dot_general | solution.py:12
  115.2 0.0 copy-start
  115.2 85.7 %reduce-scatter.5.cloned.1.call-done = f32[2048,256]{1,0:T(8,128)} async-done(((f32[8192,256]{1,0:T(8,128)}), f32[2048,256]{1,0:T(8,128)}) %reduce-scatter.5.cloned.1.call-update) | async-done | bytes 2097168 | tf_op jit(solution)/shard_map/reduce_scatter | solution.py:105
  201.0 4.0 %fusion.4 = f32[256,256]{1,0:T(8,128)S(1)} fusion(f32[256,256]{1,0:T(8,128)S(1)} %fusion.7, f32[2048,256]{1,0:T(8,128)} %reduce-scatter.5.cloned.1.call-done), kind=kOutput, calls=%fused_computation.7 | convolution fusion | flops 805437440 | bytes 2621440 | tf_op jit(solution)/shard_map/dot_general | solution.py:12
  205.0 0.1 collective-permute-start
  205.1 1.5 collective-permute-done
  206.6 1.5 collective-permute-start.1
  208.2 6.9 %collective-permute-done.1 = f32[256,256]{1,0:T(8,128)S(1)} collective-permute-done((f32[256,256]{1,0:T(8,128)S(1)}, f32[256,256]{1,0:T(8,128)S(1)}, u32[]{:S(2)}, u32[]{:S(2)}) %collective-permute-start.1) | collective-permute-done | bytes 262176 | tf_op jit(solution)/shard_map/ppermute | solution.py:24
  215.1 2.5 collective-permute-start.2
  217.6 11.6 %collective-permute-done.2 = f32[256,256]{1,0:T(8,128)S(1)} collective-permute-done((f32[256,256]{1,0:T(8,128)S(1)}, f32[256,256]{1,0:T(8,128)S(1)}, u32[]{:S(2)}, u32[]{:S(2)}) %collective-permute-start.2) | collective-permute-done | bytes 262176 | tf_op jit(solution)/shard_map/ppermute | solution.py:24
  229.2 1.4 collective-permute-start.3
  230.7 5.9 %collective-permute-done.3 = f32[256,256]{1,0:T(8,128)S(1)} collective-permute-done((f32[256,256]{1,0:T(8,128)S(1)}, f32[256,256]{1,0:T(8,128)S(1)}, u32[]{:S(2)}, u32[]{:S(2)}) %collective-permute-start.3) | collective-permute-done | bytes 262176 | tf_op jit(solution)/shard_map/ppermute | solution.py:24
  236.6 1.4 collective-permute-start.4
  238.0 5.0 %collective-permute-done.4 = f32[256,256]{1,0:T(8,128)S(1)} collective-permute-done((f32[256,256]{1,0:T(8,128)S(1)}, f32[256,256]{1,0:T(8,128)S(1)}, u32[]{:S(2)}, u32[]{:S(2)}) %collective-permute-start.4) | collective-permute-done | bytes 262176 | tf_op jit(solution)/shard_map/ppermute | solution.py:24
  243.0 0.7 add.27.gram_ref
  243.7 32.1 %shard_map.41 = (f32[256,256]{1,0:T(8,128)}, f32[256,256]{1,0:T(8,128)}) custom-call(f32[256,256]{1,0:T(8,128)} %add.27.gram_ref), custom_call_target="tpu_custom_call" | custom-call | tf_op jit(solution)/shard_map/pallas_call | solution.py:84
  275.9 0.0 copy-done
  275.9 5.4 %fusion = f32[4096,256]{1,0:T(8,128)} fusion(f32[256,256]{1,0:T(8,128)} %get-tuple-element.4, f32[2048,256]{1,0:T(8,128)} %reduce-scatter.5.cloned.1.call-done, f32[2048,256]{1,0:T(8,128)S(1)} %copy-done), kind=kOutput, calls=%fused_computation.2 | convolution fusion | flops 1611661312 | bytes 8650752 | tf_op jit(solution)/shard_map/dot_general | solution.py:16
  (4 shorter events, 0.1 us)
Async XLA Ops:
  7.2 104.0 %reduce-scatter.3.cloned.1.call-start = ((), (), s32[]{:S(2)}) async-start(), calls=%async_computation.2 | async-start | bytes 10485760 | tf_op jit(solution)/shard_map/reduce_scatter | solution.py:105
  7.2 5.1 %copy-start.1 = (f32[1,256]{1,0:T(1,128)S(1)}, f32[1,256]{1,0:T(1,128)}, u32[]{:S(2)}) copy-start(f32[1,256]{1,0:T(1,128)} %param.3) | copy-start | bytes 3076
  21.9 179.0 %reduce-scatter.5.cloned.1.call-start = ((), (), s32[]{:S(2)}) async-start(), calls=%async_computation.3 | async-start | bytes 10485760 | tf_op jit(solution)/shard_map/reduce_scatter | solution.py:105
  115.2 160.7 %copy-start = (f32[2048,256]{1,0:T(8,128)S(1)}, f32[2048,256]{1,0:T(8,128)}, u32[]{:S(2)}) copy-start(f32[2048,256]{1,0:T(8,128)} %reduce-scatter.3.cloned.1.call-done) | copy-start | bytes 6291460
  205.0 1.6 collective-permute-start
  206.6 8.4 %collective-permute-start.1 = (f32[256,256]{1,0:T(8,128)S(1)}, f32[256,256]{1,0:T(8,128)S(1)}, u32[]{:S(2)}, u32[]{:S(2)}) collective-permute-start(f32[256,256]{1,0:T(8,128)S(1)} %add.23), channel_id=1, source_target_pairs={{0,2},{1,3},{2,0},{3,1},{4,6},{5,7},{6,4},{7,5},{8,10},{9,11},{10,... | collective-permute-start | bytes 786440 | tf_op jit(solution)/shard_map/ppermute | solution.py:24
  215.1 14.1 %collective-permute-start.2 = (f32[256,256]{1,0:T(8,128)S(1)}, f32[256,256]{1,0:T(8,128)S(1)}, u32[]{:S(2)}, u32[]{:S(2)}) collective-permute-start(f32[256,256]{1,0:T(8,128)S(1)} %add.24), channel_id=1, source_target_pairs={{0,4},{1,5},{2,6},{3,7},{4,0},{5,1},{6,2},{7,3},{8,12},{9,13},{10,... | collective-permute-start | bytes 786440 | tf_op jit(solution)/shard_map/ppermute | solution.py:24
  229.2 7.3 %collective-permute-start.3 = (f32[256,256]{1,0:T(8,128)S(1)}, f32[256,256]{1,0:T(8,128)S(1)}, u32[]{:S(2)}, u32[]{:S(2)}) collective-permute-start(f32[256,256]{1,0:T(8,128)S(1)} %add.25), channel_id=1, source_target_pairs={{0,8},{1,9},{2,10},{3,11},{4,12},{5,13},{6,14},{7,15},{8,0},{9,1},... | collective-permute-start | bytes 786440 | tf_op jit(solution)/shard_map/ppermute | solution.py:24
  236.6 6.4 %collective-permute-start.4 = (f32[256,256]{1,0:T(8,128)S(1)}, f32[256,256]{1,0:T(8,128)S(1)}, u32[]{:S(2)}, u32[]{:S(2)}) collective-permute-start(f32[256,256]{1,0:T(8,128)S(1)} %add.26), channel_id=1, source_target_pairs={{0,16},{1,17},{2,18},{3,19},{4,20},{5,21},{6,22},{7,23},{8,24},{9,... | collective-permute-start | bytes 786440 | tf_op jit(solution)/shard_map/ppermute | solution.py:24
Sparse Core Ops, SparseCore 0:
  22.0 89.0 reduce-scatter.2
  114.5 86.3 reduce-scatter.4

commit v4 on v2

--- a/solution.py
+++ b/solution.py
@@ -9,7 +9,11 @@
 
 
 def cross_products(left, right):
-    return jnp.dot(left.T, right, precision=HIGHEST, preferred_element_type=jnp.float32)
+    return jnp.dot(left.T, right, precision=lax.Precision.HIGH, preferred_element_type=jnp.float32)
+
+
+def dot_high(a, b):
+    return jnp.dot(a, b, precision=lax.Precision.HIGH, preferred_element_type=jnp.float32)
 
 
 def butterfly_sum(x, axes):
@@ -93,7 +97,7 @@
     total_rows = mixed.shape[0] * devices_all
     gram = cross_products(mixed, mixed) / total_rows
     upper, upper_inv = factor(butterfly_sum(gram, ("shift", "rows")))
-    basis = dot(mixed, upper_inv)
+    basis = dot_high(mixed, upper_inv)
     return (basis, upper)
 
 

time: 269 us -> 265 us (0.985)
  matrix products: 17.5 us -> 12.9 us
    dot_general x2, matrix products: 17.5 us -> 12.9 us  [the longest x1 6.88 us: cross_products(): jnp.dot(left.T, right, precision=lax.Precision.HIGH, preferred_element_ty...]
where the time goes in v4:
time: 265 us; the launch traced here: 264 us
  waiting for transfers between devices  188 us (71%)
  Pallas kernels  32.1 us (12%)
  between operations  14.1 us (5%)
  matrix products  12.9 us (5%)
  other arithmetic  10.5 us (4%)
  starting transfers between devices  6.94 us (3%)
    reduce_scatter x1, waiting for transfers between devices, shards(): mixed = lax.psum_scatter(weighted, 'shift', scatter_dimension=0, tiled=True)  157 us
    pallas_call x1, Pallas kernels, factor(): pl.pallas_call(factor_kernel, out_shape=(jax.ShapeDtypeStruct((n, n), jnp...  32.1 us
    ppermute x5, waiting for transfers between devices, butterfly_sum(): x = x + lax.ppermute(x, axes, pairs)  30.9 us
    mul x1, other arithmetic, shards(): weighted = filtered[0].astype(jnp.float32) * weights[0][None, :]  9.59 us
    ppermute x5, starting transfers between devices, butterfly_sum(): x = x + lax.ppermute(x, axes, pairs)  6.9 us
    dot_general x1, matrix products, cross_products(): jnp.dot(left.T, right, precision=lax.Precision.HIGH, preferred_element_ty...  6.88 us
    dot_general x1, matrix products, dot_high(): jnp.dot(a, b, precision=lax.Precision.HIGH, preferred_element_type=jnp.fl...  6.03 us
  transfers between devices with their start and end apart: 6, of which 6 were waited for; matrix products, arithmetic and copies ran while one was open for 0% of the time, Pallas kernels for 0%

profile of v4, /device:TPU:0, one launch (start us, length us, event | category | flops | bytes accessed | tf_op | source)
XLA Modules:
  0.0 264.2 jit_solution(12342906776185926398)
XLA Ops:
  7.2 0.0 reduce-scatter.2.cloned.1.call-start
  7.2 9.6 %convert_multiply_fusion = f32[16384,256]{1,0:T(8,128)} fusion(bf16[1,16384,256]{2,1,0:T(8,128)(2,1)} %param.2, f32[256]{0:T(256)} %bitcast.8), kind=kLoop, calls=%fused_computation | loop fusion | flops 8388608 | bytes 25166848 | tf_op jit(solution)/shard_map/mul | solution.py:94
  16.8 0.0 reduce-scatter.2.cloned.1.call-update
  16.8 156.7 %reduce-scatter.2.cloned.1.call-done = f32[4096,256]{1,0:T(8,128)} async-done(((f32[16384,256]{1,0:T(8,128)}), f32[4096,256]{1,0:T(8,128)}) %reduce-scatter.2.cloned.1.call-update) | async-done | bytes 4194320 | tf_op jit(solution)/shard_map/reduce_scatter | solution.py:95
  173.5 6.9 %convolution_multiply_fusion = f32[256,256]{1,0:T(8,128)S(1)} fusion(f32[4096,256]{1,0:T(8,128)} %reduce-scatter.2.cloned.1.call-done), kind=kOutput, calls=%fused_computation.1 | convolution fusion | flops 1610678272 | bytes 4456448 | tf_op jit(solution)/shard_map/dot_general | solution.py:12
  180.4 0.1 collective-permute-start
  180.5 1.5 collective-permute-done
  182.1 1.6 collective-permute-start.1
  183.6 6.9 %collective-permute-done.1 = f32[256,256]{1,0:T(8,128)S(1)} collective-permute-done((f32[256,256]{1,0:T(8,128)S(1)}, f32[256,256]{1,0:T(8,128)S(1)}, u32[]{:S(2)}, u32[]{:S(2)}) %collective-permute-start.1) | collective-permute-done | bytes 262176 | tf_op jit(solution)/shard_map/ppermute | solution.py:24
  190.5 2.5 collective-permute-start.2
  193.0 11.7 %collective-permute-done.2 = f32[256,256]{1,0:T(8,128)S(1)} collective-permute-done((f32[256,256]{1,0:T(8,128)S(1)}, f32[256,256]{1,0:T(8,128)S(1)}, u32[]{:S(2)}, u32[]{:S(2)}) %collective-permute-start.2) | collective-permute-done | bytes 262176 | tf_op jit(solution)/shard_map/ppermute | solution.py:24
  204.6 1.4 collective-permute-start.3
  206.1 5.9 %collective-permute-done.3 = f32[256,256]{1,0:T(8,128)S(1)} collective-permute-done((f32[256,256]{1,0:T(8,128)S(1)}, f32[256,256]{1,0:T(8,128)S(1)}, u32[]{:S(2)}, u32[]{:S(2)}) %collective-permute-start.3) | collective-permute-done | bytes 262176 | tf_op jit(solution)/shard_map/ppermute | solution.py:24
  212.0 1.4 collective-permute-start.4
  213.4 5.0 %collective-permute-done.4 = f32[256,256]{1,0:T(8,128)S(1)} collective-permute-done((f32[256,256]{1,0:T(8,128)S(1)}, f32[256,256]{1,0:T(8,128)S(1)}, u32[]{:S(2)}, u32[]{:S(2)}) %collective-permute-start.4) | collective-permute-done | bytes 262176 | tf_op jit(solution)/shard_map/ppermute | solution.py:24
  218.4 0.7 add.21.gram_ref
  219.2 32.1 %shard_map.41 = (f32[256,256]{1,0:T(8,128)}, f32[256,256]{1,0:T(8,128)}) custom-call(f32[256,256]{1,0:T(8,128)} %add.21.gram_ref), custom_call_target="tpu_custom_call" | custom-call | tf_op jit(solution)/shard_map/pallas_call | solution.py:84
  251.3 6.0 %fusion = f32[4096,256]{1,0:T(8,128)} fusion(f32[4096,256]{1,0:T(8,128)} %reduce-scatter.2.cloned.1.call-done, f32[256,256]{1,0:T(8,128)} %get-tuple-element.4), kind=kOutput, calls=%fused_computation.2 | convolution fusion | flops 1610612736 | bytes 8650752 | tf_op jit(solution)/shard_map/dot_general | solution.py:16
  (4 shorter events, 0.1 us)
Async XLA Ops:
  7.2 166.4 %reduce-scatter.2.cloned.1.call-start = ((), (), s32[]{:S(2)}) async-start(), calls=%async_computation.1 | async-start | bytes 20971520 | tf_op jit(solution)/shard_map/reduce_scatter | solution.py:95
  180.4 1.6 collective-permute-start
  182.1 8.4 %collective-permute-start.1 = (f32[256,256]{1,0:T(8,128)S(1)}, f32[256,256]{1,0:T(8,128)S(1)}, u32[]{:S(2)}, u32[]{:S(2)}) collective-permute-start(f32[256,256]{1,0:T(8,128)S(1)} %add.17), channel_id=1, source_target_pairs={{0,2},{1,3},{2,0},{3,1},{4,6},{5,7},{6,4},{7,5},{8,10},{9,11},{10,... | collective-permute-start | bytes 786440 | tf_op jit(solution)/shard_map/ppermute | solution.py:24
  190.5 14.1 %collective-permute-start.2 = (f32[256,256]{1,0:T(8,128)S(1)}, f32[256,256]{1,0:T(8,128)S(1)}, u32[]{:S(2)}, u32[]{:S(2)}) collective-permute-start(f32[256,256]{1,0:T(8,128)S(1)} %add.18), channel_id=1, source_target_pairs={{0,4},{1,5},{2,6},{3,7},{4,0},{5,1},{6,2},{7,3},{8,12},{9,13},{10,... | collective-permute-start | bytes 786440 | tf_op jit(solution)/shard_map/ppermute | solution.py:24
  204.6 7.3 %collective-permute-start.3 = (f32[256,256]{1,0:T(8,128)S(1)}, f32[256,256]{1,0:T(8,128)S(1)}, u32[]{:S(2)}, u32[]{:S(2)}) collective-permute-start(f32[256,256]{1,0:T(8,128)S(1)} %add.19), channel_id=1, source_target_pairs={{0,8},{1,9},{2,10},{3,11},{4,12},{5,13},{6,14},{7,15},{8,0},{9,1},... | collective-permute-start | bytes 786440 | tf_op jit(solution)/shard_map/ppermute | solution.py:24
  212.0 6.4 %collective-permute-start.4 = (f32[256,256]{1,0:T(8,128)S(1)}, f32[256,256]{1,0:T(8,128)S(1)}, u32[]{:S(2)}, u32[]{:S(2)}) collective-permute-start(f32[256,256]{1,0:T(8,128)S(1)} %add.20), channel_id=1, source_target_pairs={{0,16},{1,17},{2,18},{3,19},{4,20},{5,21},{6,22},{7,23},{8,24},{9,... | collective-permute-start | bytes 786440 | tf_op jit(solution)/shard_map/ppermute | solution.py:24
Sparse Core Ops, SparseCore 0:
  16.9 156.5 reduce-scatter.1

commit v5 on v4

--- a/solution.py
+++ b/solution.py
@@ -31,39 +31,58 @@
 
 
 def leaf_factor(a, work):
-    n = a.shape[0]
-    rows = lax.broadcasted_iota(jnp.int32, (n, 2 * n), 0)
-    cols = lax.broadcasted_iota(jnp.int32, (n, 2 * n), 1)
-    work[...] = jnp.where(cols < n, jnp.concatenate([a, a], axis=1), (cols - n == rows).astype(jnp.float32))
-    row_index = lax.broadcasted_iota(jnp.int32, (n, 1), 0)
-    lane_index = lax.broadcasted_iota(jnp.int32, (1, n), 1)
+    m, width = a.shape
+    rows = lax.broadcasted_iota(jnp.int32, (m, width), 0)
+    cols = lax.broadcasted_iota(jnp.int32, (m, width), 1)
+    work[...] = jnp.where(cols < m, a, (cols - m == rows).astype(jnp.float32))
+    row_index = lax.broadcasted_iota(jnp.int32, (m, 1), 0)
+    lane_index = lax.broadcasted_iota(jnp.int32, (1, width), 1)
 
     def step(j, carry):
         row = work[pl.ds(j, 1), :]
-        pivot = jnp.sum(jnp.where(lane_index == j, row[:, :n], 0.0), axis=1, keepdims=True)
+        pivot = jnp.sum(jnp.where(lane_index == j, row, 0.0), axis=1, keepdims=True)
         scale = 1.0 / jnp.sqrt(pivot)
         scaled = row * scale
         current = work[...]
-        column = jnp.sum(jnp.where(lane_index == j, current[:, :n], 0.0), axis=1, keepdims=True)
+        column = jnp.sum(jnp.where(lane_index == j, current, 0.0), axis=1, keepdims=True)
         coef = jnp.where(row_index > j, column * scale, 0.0)
         work[...] = current - coef * scaled
         work[pl.ds(j, 1), :] = scaled
         return carry
 
-    lax.fori_loop(0, n, step, 0)
+    lax.fori_loop(0, m, step, 0)
     result = work[...]
-    upper = jnp.where(cols[:, :n] >= rows[:, :n], result[:, :n], 0.0)
-    return upper, result[:, n:]
+    upper = jnp.where((cols >= rows) & (cols < m), result, 0.0)
+    inverse = jnp.where(cols >= m, result, 0.0)
+    return upper, inverse
+
+
+def factor_half(x, work):
+    n = x.shape[0]
+    m = n // 2
+    cols = lax.broadcasted_iota(jnp.int32, (m, n), 1)
+    zeros = jnp.zeros((m, n), jnp.float32)
+    r11, l11i_high = leaf_factor(x[:m, :], work)
+    l11i = pltpu.roll(l11i_high, m, 1)
+    r12 = jnp.where(cols >= m, dot(l11i, x), 0.0)
+    r12_full = jnp.concatenate([r12, zeros], axis=0)
+    schur_rows = (x - dot(r12_full.T, r12_full))[m:, :]
+    r22, l22i_high = leaf_factor(pltpu.roll(schur_rows, m, 1), work)
+    upper = jnp.concatenate([r11 + r12, pltpu.roll(r22, m, 1)], axis=0)
+    first = jnp.concatenate([l11i, zeros], axis=0)
+    second = jnp.concatenate([zeros, l22i_high], axis=0)
+    inverse = first + second - dot(dot(second, r12_full.T), first)
+    return upper, inverse
 
 
 def factor_kernel(gram_ref, r_ref, rinv_ref, work):
     n = gram_ref.shape[0]
     h = n // 2
     g = gram_ref[...]
-    r11, l11i = leaf_factor(g[:h, :h], work)
+    r11, l11i = factor_half(g[:h, :h], work)
     r12 = dot(l11i, g[:h, h:])
     schur = g[h:, h:] - dot(r12.T, r12)
-    r22, l22i = leaf_factor(schur, work)
+    r22, l22i = factor_half(schur, work)
     r11i = l11i.T
     r22i = l22i.T
     rinv12 = -dot(dot(r11i, r12), r22i)
@@ -86,7 +105,7 @@
         out_shape=(jax.ShapeDtypeStruct((n, n), jnp.float32), jax.ShapeDtypeStruct((n, n), jnp.float32)),
         in_specs=[vmem],
         out_specs=(vmem, vmem),
-        scratch_shapes=[pltpu.VMEM((n // 2, n), jnp.float32)],
+        scratch_shapes=[pltpu.VMEM((n // 4, n // 2), jnp.float32)],
     )(gram)
 
 

time: 265 us -> 264 us (level)
  no operation moved by 1% of the time
where the time goes in v5:
time: 264 us; the launch traced here: 263 us
  waiting for transfers between devices  188 us (71%)
  Pallas kernels  31.4 us (12%)
  between operations  14.1 us (5%)
  matrix products  12.9 us (5%)
  other arithmetic  10.5 us (4%)
  starting transfers between devices  6.94 us (3%)
    reduce_scatter x1, waiting for transfers between devices, shards(): mixed = lax.psum_scatter(weighted, 'shift', scatter_dimension=0, tiled=True)  157 us
    pallas_call x1, Pallas kernels, factor(): pl.pallas_call(factor_kernel, out_shape=(jax.ShapeDtypeStruct((n, n), jnp...  31.4 us
    ppermute x5, waiting for transfers between devices, butterfly_sum(): x = x + lax.ppermute(x, axes, pairs)  30.9 us
    mul x1, other arithmetic, shards(): weighted = filtered[0].astype(jnp.float32) * weights[0][None, :]  9.59 us
    ppermute x5, starting transfers between devices, butterfly_sum(): x = x + lax.ppermute(x, axes, pairs)  6.9 us
    dot_general x1, matrix products, cross_products(): jnp.dot(left.T, right, precision=lax.Precision.HIGH, preferred_element_ty...  6.88 us
    dot_general x1, matrix products, dot_high(): jnp.dot(a, b, precision=lax.Precision.HIGH, preferred_element_type=jnp.fl...  6.03 us
  transfers between devices with their start and end apart: 6, of which 6 were waited for; matrix products, arithmetic and copies ran while one was open for 0% of the time, Pallas kernels for 0%

profile of v5, /device:TPU:0, one launch (start us, length us, event | category | flops | bytes accessed | tf_op | source)
XLA Modules:
  0.0 263.4 jit_solution(3106162447498265168)
XLA Ops:
  7.2 0.0 reduce-scatter.2.cloned.1.call-start
  7.2 9.6 %convert_multiply_fusion = f32[16384,256]{1,0:T(8,128)} fusion(bf16[1,16384,256]{2,1,0:T(8,128)(2,1)} %param.2, f32[256]{0:T(256)} %bitcast.8), kind=kLoop, calls=%fused_computation | loop fusion | flops 8388608 | bytes 25166848 | tf_op jit(solution)/shard_map/mul | solution.py:113
  16.8 0.0 reduce-scatter.2.cloned.1.call-update
  16.8 156.7 %reduce-scatter.2.cloned.1.call-done = f32[4096,256]{1,0:T(8,128)} async-done(((f32[16384,256]{1,0:T(8,128)}), f32[4096,256]{1,0:T(8,128)}) %reduce-scatter.2.cloned.1.call-update) | async-done | bytes 4194320 | tf_op jit(solution)/shard_map/reduce_scatter | solution.py:114
  173.5 6.9 %convolution_multiply_fusion = f32[256,256]{1,0:T(8,128)S(1)} fusion(f32[4096,256]{1,0:T(8,128)} %reduce-scatter.2.cloned.1.call-done), kind=kOutput, calls=%fused_computation.1 | convolution fusion | flops 1610678272 | bytes 4456448 | tf_op jit(solution)/shard_map/dot_general | solution.py:12
  180.4 0.1 collective-permute-start
  180.5 1.5 collective-permute-done
  182.1 1.6 collective-permute-start.1
  183.6 6.9 %collective-permute-done.1 = f32[256,256]{1,0:T(8,128)S(1)} collective-permute-done((f32[256,256]{1,0:T(8,128)S(1)}, f32[256,256]{1,0:T(8,128)S(1)}, u32[]{:S(2)}, u32[]{:S(2)}) %collective-permute-start.1) | collective-permute-done | bytes 262176 | tf_op jit(solution)/shard_map/ppermute | solution.py:24
  190.5 2.5 collective-permute-start.2
  193.0 11.7 %collective-permute-done.2 = f32[256,256]{1,0:T(8,128)S(1)} collective-permute-done((f32[256,256]{1,0:T(8,128)S(1)}, f32[256,256]{1,0:T(8,128)S(1)}, u32[]{:S(2)}, u32[]{:S(2)}) %collective-permute-start.2) | collective-permute-done | bytes 262176 | tf_op jit(solution)/shard_map/ppermute | solution.py:24
  204.6 1.4 collective-permute-start.3
  206.1 5.9 %collective-permute-done.3 = f32[256,256]{1,0:T(8,128)S(1)} collective-permute-done((f32[256,256]{1,0:T(8,128)S(1)}, f32[256,256]{1,0:T(8,128)S(1)}, u32[]{:S(2)}, u32[]{:S(2)}) %collective-permute-start.3) | collective-permute-done | bytes 262176 | tf_op jit(solution)/shard_map/ppermute | solution.py:24
  212.0 1.4 collective-permute-start.4
  213.4 5.0 %collective-permute-done.4 = f32[256,256]{1,0:T(8,128)S(1)} collective-permute-done((f32[256,256]{1,0:T(8,128)S(1)}, f32[256,256]{1,0:T(8,128)S(1)}, u32[]{:S(2)}, u32[]{:S(2)}) %collective-permute-start.4) | collective-permute-done | bytes 262176 | tf_op jit(solution)/shard_map/ppermute | solution.py:24
  218.4 0.7 add.21.gram_ref
  219.2 31.4 %shard_map.41 = (f32[256,256]{1,0:T(8,128)}, f32[256,256]{1,0:T(8,128)}) custom-call(f32[256,256]{1,0:T(8,128)} %add.21.gram_ref), custom_call_target="tpu_custom_call" | custom-call | tf_op jit(solution)/shard_map/pallas_call | solution.py:103
  250.6 6.0 %fusion = f32[4096,256]{1,0:T(8,128)} fusion(f32[4096,256]{1,0:T(8,128)} %reduce-scatter.2.cloned.1.call-done, f32[256,256]{1,0:T(8,128)} %get-tuple-element.4), kind=kOutput, calls=%fused_computation.2 | convolution fusion | flops 1610612736 | bytes 8650752 | tf_op jit(solution)/shard_map/dot_general | solution.py:16
  (4 shorter events, 0.1 us)
Async XLA Ops:
  7.2 166.4 %reduce-scatter.2.cloned.1.call-start = ((), (), s32[]{:S(2)}) async-start(), calls=%async_computation.1 | async-start | bytes 20971520 | tf_op jit(solution)/shard_map/reduce_scatter | solution.py:114
  180.4 1.6 collective-permute-start
  182.1 8.4 %collective-permute-start.1 = (f32[256,256]{1,0:T(8,128)S(1)}, f32[256,256]{1,0:T(8,128)S(1)}, u32[]{:S(2)}, u32[]{:S(2)}) collective-permute-start(f32[256,256]{1,0:T(8,128)S(1)} %add.17), channel_id=1, source_target_pairs={{0,2},{1,3},{2,0},{3,1},{4,6},{5,7},{6,4},{7,5},{8,10},{9,11},{10,... | collective-permute-start | bytes 786440 | tf_op jit(solution)/shard_map/ppermute | solution.py:24
  190.5 14.1 %collective-permute-start.2 = (f32[256,256]{1,0:T(8,128)S(1)}, f32[256,256]{1,0:T(8,128)S(1)}, u32[]{:S(2)}, u32[]{:S(2)}) collective-permute-start(f32[256,256]{1,0:T(8,128)S(1)} %add.18), channel_id=1, source_target_pairs={{0,4},{1,5},{2,6},{3,7},{4,0},{5,1},{6,2},{7,3},{8,12},{9,13},{10,... | collective-permute-start | bytes 786440 | tf_op jit(solution)/shard_map/ppermute | solution.py:24
  204.6 7.3 %collective-permute-start.3 = (f32[256,256]{1,0:T(8,128)S(1)}, f32[256,256]{1,0:T(8,128)S(1)}, u32[]{:S(2)}, u32[]{:S(2)}) collective-permute-start(f32[256,256]{1,0:T(8,128)S(1)} %add.19), channel_id=1, source_target_pairs={{0,8},{1,9},{2,10},{3,11},{4,12},{5,13},{6,14},{7,15},{8,0},{9,1},... | collective-permute-start | bytes 786440 | tf_op jit(solution)/shard_map/ppermute | solution.py:24
  212.0 6.4 %collective-permute-start.4 = (f32[256,256]{1,0:T(8,128)S(1)}, f32[256,256]{1,0:T(8,128)S(1)}, u32[]{:S(2)}, u32[]{:S(2)}) collective-permute-start(f32[256,256]{1,0:T(8,128)S(1)} %add.20), channel_id=1, source_target_pairs={{0,16},{1,17},{2,18},{3,19},{4,20},{5,21},{6,22},{7,23},{8,24},{9,... | collective-permute-start | bytes 786440 | tf_op jit(solution)/shard_map/ppermute | solution.py:24
Sparse Core Ops, SparseCore 0:
  16.9 156.5 reduce-scatter.1

commit v6 on v5

--- a/solution.py
+++ b/solution.py
@@ -31,29 +31,20 @@
 
 
 def leaf_factor(a, work):
+    del work
     m, width = a.shape
     rows = lax.broadcasted_iota(jnp.int32, (m, width), 0)
     cols = lax.broadcasted_iota(jnp.int32, (m, width), 1)
-    work[...] = jnp.where(cols < m, a, (cols - m == rows).astype(jnp.float32))
+    current = jnp.where(cols < m, a, (cols - m == rows).astype(jnp.float32))
     row_index = lax.broadcasted_iota(jnp.int32, (m, 1), 0)
-    lane_index = lax.broadcasted_iota(jnp.int32, (1, width), 1)
-
-    def step(j, carry):
-        row = work[pl.ds(j, 1), :]
-        pivot = jnp.sum(jnp.where(lane_index == j, row, 0.0), axis=1, keepdims=True)
-        scale = 1.0 / jnp.sqrt(pivot)
+    for j in range(m):
+        row = current[j:j + 1, :]
+        scale = 1.0 / jnp.sqrt(row[:, j:j + 1])
         scaled = row * scale
-        current = work[...]
-        column = jnp.sum(jnp.where(lane_index == j, current, 0.0), axis=1, keepdims=True)
-        coef = jnp.where(row_index > j, column * scale, 0.0)
-        work[...] = current - coef * scaled
-        work[pl.ds(j, 1), :] = scaled
-        return carry
-
-    lax.fori_loop(0, m, step, 0)
-    result = work[...]
-    upper = jnp.where((cols >= rows) & (cols < m), result, 0.0)
-    inverse = jnp.where(cols >= m, result, 0.0)
+        coef = jnp.where(row_index > j, current[:, j:j + 1] * scale, 0.0)
+        current = jnp.where(row_index == j, scaled, current - coef * scaled)
+    upper = jnp.where((cols >= rows) & (cols < m), current, 0.0)
+    inverse = jnp.where(cols >= m, current, 0.0)
     return upper, inverse
 
 

time: 264 us -> 262 us (level)
  no operation moved by 1% of the time
where the time goes in v6:
time: 262 us; the launch traced here: 261 us
  waiting for transfers between devices  188 us (72%)
  Pallas kernels  29.4 us (11%)
  between operations  14.1 us (5%)
  matrix products  12.9 us (5%)
  other arithmetic  10.5 us (4%)
  starting transfers between devices  6.94 us (3%)
    reduce_scatter x1, waiting for transfers between devices, shards(): mixed = lax.psum_scatter(weighted, 'shift', scatter_dimension=0, tiled=True)  157 us
    ppermute x5, waiting for transfers between devices, butterfly_sum(): x = x + lax.ppermute(x, axes, pairs)  30.9 us
    pallas_call x1, Pallas kernels, factor(): pl.pallas_call(factor_kernel, out_shape=(jax.ShapeDtypeStruct((n, n), jnp...  29.4 us
    mul x1, other arithmetic, shards(): weighted = filtered[0].astype(jnp.float32) * weights[0][None, :]  9.59 us
    ppermute x5, starting transfers between devices, butterfly_sum(): x = x + lax.ppermute(x, axes, pairs)  6.9 us
    dot_general x1, matrix products, cross_products(): jnp.dot(left.T, right, precision=lax.Precision.HIGH, preferred_element_ty...  6.88 us
    dot_general x1, matrix products, dot_high(): jnp.dot(a, b, precision=lax.Precision.HIGH, preferred_element_type=jnp.fl...  6.03 us
  transfers between devices with their start and end apart: 6, of which 6 were waited for; matrix products, arithmetic and copies ran while one was open for 0% of the time, Pallas kernels for 0%

profile of v6, /device:TPU:0, one launch (start us, length us, event | category | flops | bytes accessed | tf_op | source)
XLA Modules:
  0.0 261.4 jit_solution(13640194973106391335)
XLA Ops:
  7.2 0.0 reduce-scatter.2.cloned.1.call-start
  7.2 9.6 %convert_multiply_fusion = f32[16384,256]{1,0:T(8,128)} fusion(bf16[1,16384,256]{2,1,0:T(8,128)(2,1)} %param.2, f32[256]{0:T(256)} %bitcast.8), kind=kLoop, calls=%fused_computation | loop fusion | flops 8388608 | bytes 25166848 | tf_op jit(solution)/shard_map/mul | solution.py:104
  16.8 0.0 reduce-scatter.2.cloned.1.call-update
  16.8 156.7 %reduce-scatter.2.cloned.1.call-done = f32[4096,256]{1,0:T(8,128)} async-done(((f32[16384,256]{1,0:T(8,128)}), f32[4096,256]{1,0:T(8,128)}) %reduce-scatter.2.cloned.1.call-update) | async-done | bytes 4194320 | tf_op jit(solution)/shard_map/reduce_scatter | solution.py:105
  173.5 6.9 %convolution_multiply_fusion = f32[256,256]{1,0:T(8,128)S(1)} fusion(f32[4096,256]{1,0:T(8,128)} %reduce-scatter.2.cloned.1.call-done), kind=kOutput, calls=%fused_computation.1 | convolution fusion | flops 1610678272 | bytes 4456448 | tf_op jit(solution)/shard_map/dot_general | solution.py:12
  180.4 0.1 collective-permute-start
  180.5 1.5 collective-permute-done
  182.1 1.6 collective-permute-start.1
  183.6 6.9 %collective-permute-done.1 = f32[256,256]{1,0:T(8,128)S(1)} collective-permute-done((f32[256,256]{1,0:T(8,128)S(1)}, f32[256,256]{1,0:T(8,128)S(1)}, u32[]{:S(2)}, u32[]{:S(2)}) %collective-permute-start.1) | collective-permute-done | bytes 262176 | tf_op jit(solution)/shard_map/ppermute | solution.py:24
  190.5 2.5 collective-permute-start.2
  193.0 11.7 %collective-permute-done.2 = f32[256,256]{1,0:T(8,128)S(1)} collective-permute-done((f32[256,256]{1,0:T(8,128)S(1)}, f32[256,256]{1,0:T(8,128)S(1)}, u32[]{:S(2)}, u32[]{:S(2)}) %collective-permute-start.2) | collective-permute-done | bytes 262176 | tf_op jit(solution)/shard_map/ppermute | solution.py:24
  204.6 1.4 collective-permute-start.3
  206.1 5.9 %collective-permute-done.3 = f32[256,256]{1,0:T(8,128)S(1)} collective-permute-done((f32[256,256]{1,0:T(8,128)S(1)}, f32[256,256]{1,0:T(8,128)S(1)}, u32[]{:S(2)}, u32[]{:S(2)}) %collective-permute-start.3) | collective-permute-done | bytes 262176 | tf_op jit(solution)/shard_map/ppermute | solution.py:24
  212.0 1.4 collective-permute-start.4
  213.4 5.0 %collective-permute-done.4 = f32[256,256]{1,0:T(8,128)S(1)} collective-permute-done((f32[256,256]{1,0:T(8,128)S(1)}, f32[256,256]{1,0:T(8,128)S(1)}, u32[]{:S(2)}, u32[]{:S(2)}) %collective-permute-start.4) | collective-permute-done | bytes 262176 | tf_op jit(solution)/shard_map/ppermute | solution.py:24
  218.4 0.7 add.21.gram_ref
  219.2 29.4 %shard_map.41 = (f32[256,256]{1,0:T(8,128)}, f32[256,256]{1,0:T(8,128)}) custom-call(f32[256,256]{1,0:T(8,128)} %add.21.gram_ref), custom_call_target="tpu_custom_call" | custom-call | tf_op jit(solution)/shard_map/pallas_call | solution.py:94
  248.5 6.0 %fusion = f32[4096,256]{1,0:T(8,128)} fusion(f32[4096,256]{1,0:T(8,128)} %reduce-scatter.2.cloned.1.call-done, f32[256,256]{1,0:T(8,128)} %get-tuple-element.4), kind=kOutput, calls=%fused_computation.2 | convolution fusion | flops 1610612736 | bytes 8650752 | tf_op jit(solution)/shard_map/dot_general | solution.py:16
  (4 shorter events, 0.1 us)
Async XLA Ops:
  7.2 166.4 %reduce-scatter.2.cloned.1.call-start = ((), (), s32[]{:S(2)}) async-start(), calls=%async_computation.1 | async-start | bytes 20971520 | tf_op jit(solution)/shard_map/reduce_scatter | solution.py:105
  180.4 1.6 collective-permute-start
  182.1 8.4 %collective-permute-start.1 = (f32[256,256]{1,0:T(8,128)S(1)}, f32[256,256]{1,0:T(8,128)S(1)}, u32[]{:S(2)}, u32[]{:S(2)}) collective-permute-start(f32[256,256]{1,0:T(8,128)S(1)} %add.17), channel_id=1, source_target_pairs={{0,2},{1,3},{2,0},{3,1},{4,6},{5,7},{6,4},{7,5},{8,10},{9,11},{10,... | collective-permute-start | bytes 786440 | tf_op jit(solution)/shard_map/ppermute | solution.py:24
  190.5 14.1 %collective-permute-start.2 = (f32[256,256]{1,0:T(8,128)S(1)}, f32[256,256]{1,0:T(8,128)S(1)}, u32[]{:S(2)}, u32[]{:S(2)}) collective-permute-start(f32[256,256]{1,0:T(8,128)S(1)} %add.18), channel_id=1, source_target_pairs={{0,4},{1,5},{2,6},{3,7},{4,0},{5,1},{6,2},{7,3},{8,12},{9,13},{10,... | collective-permute-start | bytes 786440 | tf_op jit(solution)/shard_map/ppermute | solution.py:24
  204.6 7.3 %collective-permute-start.3 = (f32[256,256]{1,0:T(8,128)S(1)}, f32[256,256]{1,0:T(8,128)S(1)}, u32[]{:S(2)}, u32[]{:S(2)}) collective-permute-start(f32[256,256]{1,0:T(8,128)S(1)} %add.19), channel_id=1, source_target_pairs={{0,8},{1,9},{2,10},{3,11},{4,12},{5,13},{6,14},{7,15},{8,0},{9,1},... | collective-permute-start | bytes 786440 | tf_op jit(solution)/shard_map/ppermute | solution.py:24
  212.0 6.4 %collective-permute-start.4 = (f32[256,256]{1,0:T(8,128)S(1)}, f32[256,256]{1,0:T(8,128)S(1)}, u32[]{:S(2)}, u32[]{:S(2)}) collective-permute-start(f32[256,256]{1,0:T(8,128)S(1)} %add.20), channel_id=1, source_target_pairs={{0,16},{1,17},{2,18},{3,19},{4,20},{5,21},{6,22},{7,23},{8,24},{9,... | collective-permute-start | bytes 786440 | tf_op jit(solution)/shard_map/ppermute | solution.py:24
Sparse Core Ops, SparseCore 0:
  16.9 156.5 reduce-scatter.1

commit v7 on v6

--- a/solution.py
+++ b/solution.py
@@ -67,12 +67,11 @@
 
 
 def factor_kernel(gram_ref, r_ref, rinv_ref, work):
-    n = gram_ref.shape[0]
-    h = n // 2
+    h = gram_ref.shape[1]
     g = gram_ref[...]
-    r11, l11i = factor_half(g[:h, :h], work)
-    r12 = dot(l11i, g[:h, h:])
-    schur = g[h:, h:] - dot(r12.T, r12)
+    r11, l11i = factor_half(g[:h], work)
+    r12 = dot(l11i, g[h:2 * h])
+    schur = g[2 * h:] - dot(r12.T, r12)
     r22, l22i = factor_half(schur, work)
     r11i = l11i.T
     r22i = l22i.T
@@ -89,7 +88,7 @@
 
 
 def factor(gram):
-    n = gram.shape[0]
+    n = 2 * gram.shape[1]
     vmem = pl.BlockSpec(memory_space=pltpu.VMEM)
     return pl.pallas_call(
         factor_kernel,
@@ -105,8 +104,11 @@
     mixed = lax.psum_scatter(weighted, "shift", scatter_dimension=0, tiled=True)
     devices_all = lax.axis_size(("shift", "rows"))
     total_rows = mixed.shape[0] * devices_all
-    gram = cross_products(mixed, mixed) / total_rows
-    upper, upper_inv = factor(butterfly_sum(gram, ("shift", "rows")))
+    half = mixed.shape[1] // 2
+    top = cross_products(mixed[:, :half], mixed)
+    bottom = cross_products(mixed[:, half:], mixed[:, half:])
+    blocks = jnp.concatenate([top[:, :half], top[:, half:], bottom], axis=0) / total_rows
+    upper, upper_inv = factor(butterfly_sum(blocks, ("shift", "rows")))
     basis = dot_high(mixed, upper_inv)
     return (basis, upper)
 

time: 262 us -> 255 us (0.973)
  waiting for transfers between devices: 188 us -> 181 us
    ppermute x5, waiting for transfers between devices: 30.9 us -> 24.5 us  [butterfly_sum(): x = x + lax.ppermute(x, axes, pairs)]
    dot_general x1 -> x2, matrix products: 6.88 us -> 6.65 us  [cross_products(): jnp.dot(left.T, right, precision=lax.Precision.HIGH, preferred_element_ty...]
where the time goes in v7:
time: 255 us
  waiting for transfers between devices  181 us (71%)
  Pallas kernels  29.3 us (11%)
  between operations  14.1 us (6%)
  matrix products  12.7 us (5%)
  other arithmetic  10.4 us (4%)
  starting transfers between devices  6.94 us (3%)
    reduce_scatter x1, waiting for transfers between devices, shards(): mixed = lax.psum_scatter(weighted, 'shift', scatter_dimension=0, tiled=True)  157 us
    pallas_call x1, Pallas kernels, factor(): pl.pallas_call(factor_kernel, out_shape=(jax.ShapeDtypeStruct((n, n), jnp...  29.3 us
    ppermute x5, waiting for transfers between devices, butterfly_sum(): x = x + lax.ppermute(x, axes, pairs)  24.5 us
    mul x1, other arithmetic, shards(): weighted = filtered[0].astype(jnp.float32) * weights[0][None, :]  9.58 us
    ppermute x5, starting transfers between devices, butterfly_sum(): x = x + lax.ppermute(x, axes, pairs)  6.9 us
    dot_general x2, matrix products, cross_products(): jnp.dot(left.T, right, precision=lax.Precision.HIGH, preferred_element_ty...  6.65 us
    dot_general x1, matrix products, dot_high(): jnp.dot(a, b, precision=lax.Precision.HIGH, preferred_element_type=jnp.fl...  6.03 us
  transfers between devices with their start and end apart: 6, of which 6 were waited for; matrix products, arithmetic and copies ran while one was open for 0% of the time, Pallas kernels for 0%

profile of v7, /device:TPU:0, one launch (start us, length us, event | category | flops | bytes accessed | tf_op | source)
XLA Modules:
  0.0 254.7 jit_solution(14470175305485466854)
XLA Ops:
  7.2 0.0 reduce-scatter.2.cloned.1.call-start
  7.2 9.6 %convert_multiply_fusion = f32[16384,256]{1,0:T(8,128)} fusion(bf16[1,16384,256]{2,1,0:T(8,128)(2,1)} %param.2, f32[256]{0:T(256)} %bitcast.7), kind=kLoop, calls=%fused_computation | loop fusion | flops 8388608 | bytes 25166848 | tf_op jit(solution)/shard_map/mul | solution.py:103
  16.8 0.0 reduce-scatter.2.cloned.1.call-update
  16.8 156.7 %reduce-scatter.2.cloned.1.call-done = f32[4096,256]{1,0:T(8,128)} async-done(((f32[16384,256]{1,0:T(8,128)}), f32[4096,256]{1,0:T(8,128)}) %reduce-scatter.2.cloned.1.call-update) | async-done | bytes 4194320 | tf_op jit(solution)/shard_map/reduce_scatter | solution.py:104
  173.5 0.0 copy-start
  173.5 4.8 %fusion.2 = f32[128,256]{1,0:T(8,128)S(1)} fusion(f32[4096,256]{1,0:T(8,128)} %reduce-scatter.2.cloned.1.call-done), kind=kOutput, calls=%fused_computation.3 | convolution fusion | flops 805306368 | bytes 6422528 | tf_op jit(solution)/shard_map/dot_general | solution.py:12
  178.3 0.0 copy-done
  178.3 1.9 fusion
  180.2 0.1 collective-permute-start
  180.3 1.4 collective-permute-done
  181.8 1.5 collective-permute-start.1
  183.3 5.5 %collective-permute-done.1 = f32[384,128]{1,0:T(8,128)S(1)} collective-permute-done((f32[384,128]{1,0:T(8,128)S(1)}, f32[384,128]{1,0:T(8,128)S(1)}, u32[]{:S(2)}, u32[]{:S(2)}) %collective-permute-start.1) | collective-permute-done | bytes 196640 | tf_op jit(solution)/shard_map/ppermute | solution.py:24
  188.8 2.5 collective-permute-start.2
  191.3 8.8 %collective-permute-done.2 = f32[384,128]{1,0:T(8,128)S(1)} collective-permute-done((f32[384,128]{1,0:T(8,128)S(1)}, f32[384,128]{1,0:T(8,128)S(1)}, u32[]{:S(2)}, u32[]{:S(2)}) %collective-permute-start.2) | collective-permute-done | bytes 196640 | tf_op jit(solution)/shard_map/ppermute | solution.py:24
  200.1 1.4 collective-permute-start.3
  201.6 4.5 %collective-permute-done.3 = f32[384,128]{1,0:T(8,128)S(1)} collective-permute-done((f32[384,128]{1,0:T(8,128)S(1)}, f32[384,128]{1,0:T(8,128)S(1)}, u32[]{:S(2)}, u32[]{:S(2)}) %collective-permute-start.3) | collective-permute-done | bytes 196640 | tf_op jit(solution)/shard_map/ppermute | solution.py:24
  206.1 1.4 collective-permute-start.4
  207.5 4.3 %collective-permute-done.4 = f32[384,128]{1,0:T(8,128)S(1)} collective-permute-done((f32[384,128]{1,0:T(8,128)S(1)}, f32[384,128]{1,0:T(8,128)S(1)}, u32[]{:S(2)}, u32[]{:S(2)}) %collective-permute-start.4) | collective-permute-done | bytes 196640 | tf_op jit(solution)/shard_map/ppermute | solution.py:24
  211.8 0.7 add.21.gram_ref
  212.5 29.3 %shard_map.41 = (f32[256,256]{1,0:T(8,128)}, f32[256,256]{1,0:T(8,128)}) custom-call(f32[384,128]{1,0:T(8,128)} %add.21.gram_ref), custom_call_target="tpu_custom_call" | custom-call | tf_op jit(solution)/shard_map/pallas_call | solution.py:93
  241.8 6.0 %fusion.6 = f32[4096,256]{1,0:T(8,128)} fusion(f32[4096,256]{1,0:T(8,128)} %reduce-scatter.2.cloned.1.call-done, f32[256,256]{1,0:T(8,128)} %get-tuple-element.4), kind=kOutput, calls=%fused_computation.8 | convolution fusion | flops 1610612736 | bytes 8650752 | tf_op jit(solution)/shard_map/dot_general | solution.py:16
  (6 shorter events, 0.1 us)
Async XLA Ops:
  7.2 166.4 %reduce-scatter.2.cloned.1.call-start = ((), (), s32[]{:S(2)}) async-start(), calls=%async_computation.1 | async-start | bytes 20971520 | tf_op jit(solution)/shard_map/reduce_scatter | solution.py:104
  173.5 4.8 %copy-start = (f32[4096,256]{1,0:T(8,128)S(1)}, f32[4096,256]{1,0:T(8,128)}, u32[]{:S(2)}) copy-start(f32[4096,256]{1,0:T(8,128)} %reduce-scatter.2.cloned.1.call-done) | copy-start | bytes 12582916
  180.2 1.5 collective-permute-start
  181.8 7.0 %collective-permute-start.1 = (f32[384,128]{1,0:T(8,128)S(1)}, f32[384,128]{1,0:T(8,128)S(1)}, u32[]{:S(2)}, u32[]{:S(2)}) collective-permute-start(f32[384,128]{1,0:T(8,128)S(1)} %fusion.4), channel_id=1, source_target_pairs={{0,2},{1,3},{2,0},{3,1},{4,6},{5,7},{6,4},{7,5},{8,10},{9,11},{10,... | collective-permute-start | bytes 589832 | tf_op jit(solution)/shard_map/ppermute | solution.py:24
  188.8 11.3 %collective-permute-start.2 = (f32[384,128]{1,0:T(8,128)S(1)}, f32[384,128]{1,0:T(8,128)S(1)}, u32[]{:S(2)}, u32[]{:S(2)}) collective-permute-start(f32[384,128]{1,0:T(8,128)S(1)} %add.18), channel_id=1, source_target_pairs={{0,4},{1,5},{2,6},{3,7},{4,0},{5,1},{6,2},{7,3},{8,12},{9,13},{10,... | collective-permute-start | bytes 589832 | tf_op jit(solution)/shard_map/ppermute | solution.py:24
  200.1 5.9 %collective-permute-start.3 = (f32[384,128]{1,0:T(8,128)S(1)}, f32[384,128]{1,0:T(8,128)S(1)}, u32[]{:S(2)}, u32[]{:S(2)}) collective-permute-start(f32[384,128]{1,0:T(8,128)S(1)} %add.19), channel_id=1, source_target_pairs={{0,8},{1,9},{2,10},{3,11},{4,12},{5,13},{6,14},{7,15},{8,0},{9,1},... | collective-permute-start | bytes 589832 | tf_op jit(solution)/shard_map/ppermute | solution.py:24
  206.1 5.7 %collective-permute-start.4 = (f32[384,128]{1,0:T(8,128)S(1)}, f32[384,128]{1,0:T(8,128)S(1)}, u32[]{:S(2)}, u32[]{:S(2)}) collective-permute-start(f32[384,128]{1,0:T(8,128)S(1)} %add.20), channel_id=1, source_target_pairs={{0,16},{1,17},{2,18},{3,19},{4,20},{5,21},{6,22},{7,23},{8,24},{9,... | collective-permute-start | bytes 589832 | tf_op jit(solution)/shard_map/ppermute | solution.py:24
Sparse Core Ops, SparseCore 0:
  16.9 156.5 reduce-scatter.1

commit v8 on v7

--- a/solution.py
+++ b/solution.py
@@ -99,9 +99,46 @@
     )(gram)
 
 
+def swap(x, bit):
+    size = lax.axis_size("shift")
+    return lax.ppermute(x, "shift", [(i, i ^ bit) for i in range(size)])
+
+
+def take(x, index, axis):
+    return lax.dynamic_index_in_dim(x, index, axis=axis, keepdims=False)
+
+
+def mix_rows(filtered, weights):
+    shift = lax.axis_index("shift")
+    low, high = shift % 2, shift // 2
+    rows, width = filtered.shape[1], filtered.shape[2]
+    piece = rows // 8
+    blocks = filtered[0].reshape(2, 2, 2, piece, width)
+    scale = weights[0][None, None, :]
+
+    def weighted(x):
+        return x.astype(jnp.float32) * scale
+
+    send_first = weighted(take(blocks[:, :, 0], 1 - low, 1))
+    send_second = weighted(take(blocks[:, :, 1], 1 - high, 0))
+    send_first, send_second = lax.optimization_barrier((send_first, send_second))
+    got_first, got_second = swap(send_first, 1), swap(send_second, 2)
+    first = weighted(take(blocks[:, :, 0], low, 1)) + got_first
+    second = weighted(take(blocks[:, :, 1], high, 0)) + got_second
+    send_first, send_second = take(first, 1 - high, 0), take(second, 1 - low, 0)
+    send_first, send_second = lax.optimization_barrier((send_first, send_second))
+    got_first, got_second = swap(send_first, 2), swap(send_second, 1)
+    first = take(first, high, 0) + got_first
+    second = take(second, low, 0) + got_second
+    return jnp.concatenate([first, second], axis=0)
+
+
 def shards(filtered, weights):
-    weighted = filtered[0].astype(jnp.float32) * weights[0][None, :]
-    mixed = lax.psum_scatter(weighted, "shift", scatter_dimension=0, tiled=True)
+    if lax.axis_size("shift") == 4:
+        mixed = mix_rows(filtered, weights)
+    else:
+        weighted = filtered[0].astype(jnp.float32) * weights[0][None, :]
+        mixed = lax.psum_scatter(weighted, "shift", scatter_dimension=0, tiled=True)
     devices_all = lax.axis_size(("shift", "rows"))
     total_rows = mixed.shape[0] * devices_all
     half = mixed.shape[1] // 2

time: 255 us -> 234 us (0.918)
  waiting for transfers between devices: 181 us -> 162 us
  between operations: 14.1 us -> 0.76 us
  local copies, waits for them, and re-layouts: 0.01 us -> 7.48 us
  starting transfers between devices: 6.94 us -> 12.2 us
  matrix products: 12.7 us -> 9.07 us
  other arithmetic: 10.4 us -> 13.2 us
    reduce_scatter x1 -> x0, waiting for transfers between devices: 157 us -> none  [shards(): mixed = lax.psum_scatter(weighted, 'shift', scatter_dimension=0, tiled=True)]
    ppermute x0 -> x4, waiting for transfers between devices: none -> 136 us  [swap(): return lax.ppermute(x, 'shift', [(i, i ^ bit) for i in range(size)])]
    slice x0 -> x1, local copies, waits for them, and re-layouts: none -> 7.12 us  [mix_rows(): send_second = weighted(take(blocks[:, :, 1], 1 - high, 0))]
    ppermute x0 -> x4, starting transfers between devices: none -> 6.58 us  [swap(): return lax.ppermute(x, 'shift', [(i, i ^ bit) for i in range(size)])]
    add x0 -> x3, other arithmetic: none -> 6.18 us  [the longest x1 5.63 us: mix_rows(): second = weighted(take(blocks[:, :, 1], high, 0)) + got_second]
    mul x1, other arithmetic: 9.58 us -> 6.21 us  [weighted(): return x.astype(jnp.float32) * scale]
    dot_general x2, matrix products: 6.65 us -> 3.65 us  [cross_products(): jnp.dot(left.T, right, precision=lax.Precision.HIGH, preferred_element_ty...]
  transfers between devices with their start and end apart: 6 -> 9, of which waited for: 6 -> 9; matrix products, arithmetic and copies ran while one was open for 0% -> 0% of each run, Pallas kernels for 0% -> 0%
where the time goes in v8:
time: 234 us
  waiting for transfers between devices  162 us (69%)
  Pallas kernels  29.5 us (13%)
  other arithmetic  13.2 us (6%)
  starting transfers between devices  12.2 us (5%)
  matrix products  9.07 us (4%)
  local copies, waits for them, and re-layouts  7.48 us (3%)
    ppermute x4, waiting for transfers between devices, swap(): return lax.ppermute(x, 'shift', [(i, i ^ bit) for i in range(size)])  136 us
    pallas_call x1, Pallas kernels, factor(): pl.pallas_call(factor_kernel, out_shape=(jax.ShapeDtypeStruct((n, n), jnp...  29.5 us
    ppermute x5, waiting for transfers between devices, butterfly_sum(): x = x + lax.ppermute(x, axes, pairs)  25.7 us
    slice x1, local copies, waits for them, and re-layouts, mix_rows(): send_second = weighted(take(blocks[:, :, 1], 1 - high, 0))  7.12 us
    ppermute x4, starting transfers between devices, swap(): return lax.ppermute(x, 'shift', [(i, i ^ bit) for i in range(size)])  6.58 us
    mul x1, other arithmetic, weighted(): return x.astype(jnp.float32) * scale  6.21 us
    ppermute x5, starting transfers between devices, butterfly_sum(): x = x + lax.ppermute(x, axes, pairs)  5.67 us
    add x1, other arithmetic, mix_rows(): second = weighted(take(blocks[:, :, 1], high, 0)) + got_second  5.63 us
  transfers between devices with their start and end apart: 9, of which 9 were waited for; matrix products, arithmetic and copies ran while one was open for 0% of the time, Pallas kernels for 0%

profile of v8, /device:TPU:0, one launch (start us, length us, event | category | flops | bytes accessed | tf_op | source)
XLA Modules:
  0.0 233.9 jit_solution(14373871724882329447)
XLA Ops:
  0.7 0.0 copy-start.1
  0.7 7.1 %fusion.13 = (bf16[2,2,1,2048,256]{4,3,2,1,0:T(8,128)(2,1)}, bf16[2,2,1,2048,256]{4,3,1,2,0:T(8,128)(2,1)}, bf16[2,2,1,2048,256]{4,3,2,1,0:T(8,128)(2,1)}) fusion(bf16[2,2,2,2048,256]{4,3,2,1,0:T(8,128)(2,1)} %bitcast.29), kind=kLoop, calls=%fused_computation.26 | loop fusion | bytes 20971520 | tf_op jit(solution)/shard_map/slice | solution.py:123
  7.8 0.0 copy-done.1
  7.8 6.2 %convert_multiply_fusion.1 = (f32[2,2048,256]{2,1,0:T(8,128)}, f32[2,2048,256]{2,1,0:T(8,128)}) fusion(bf16[2,2,1,2048,256]{4,3,1,2,0:T(8,128)(2,1)} %get-tuple-element.15, s32[]{:T(128)S(6)} %select_n.34, f32[256]{0:T(256)S(1)} %bitcast.30, bf16[2,2,1,2048,256]{4,3,2,1,0:T(8,128)(2,1)} %get-tuple-element.16, s32[]{:T(128)S(6)} %select_n.32), kind=kLoop, calls=%fused_computation.7 | loop fusion | flops 4194304 | bytes 12583944 | tf_op jit(solution)/shard_map/mul | solution.py:120
  14.0 2.9 %collective-permute-start = (f32[2,2048,256]{2,1,0:T(8,128)}, f32[2,2048,256]{2,1,0:T(8,128)}, u32[]{:S(2)}, u32[]{:S(2)}) collective-permute-start(f32[2,2048,256]{2,1,0:T(8,128)} %get-tuple-element.8), channel_id=1, source_target_pairs={{0,8},{8,0},{16,24},{24,16},{1,9},{9,1},{17,25},{25,17},{2,10},{10... | collective-permute-start | bytes 12582920 | tf_op jit(solution)/shard_map/ppermute | solution.py:104
  16.9 1.5 collective-permute-start.1
  18.5 89.4 %collective-permute-done = f32[2,2048,256]{2,1,0:T(8,128)} collective-permute-done((f32[2,2048,256]{2,1,0:T(8,128)}, f32[2,2048,256]{2,1,0:T(8,128)}, u32[]{:S(2)}, u32[]{:S(2)}) %collective-permute-start) | collective-permute-done | bytes 4194336 | tf_op jit(solution)/shard_map/ppermute | solution.py:104
  107.8 1.5 collective-permute-done.1
  109.3 5.6 %fusion = (f32[2,2048,256]{2,1,0:T(8,128)S(1)}, f32[2,2048,256]{2,1,0:T(8,128)S(1)}) fusion(f32[2,2048,256]{2,1,0:T(8,128)} %collective-permute-done.1, bf16[2,2,1,2048,256]{4,3,2,1,0:T(8,128)(2,1)} %get-tuple-element.14, s32[]{:T(128)S(6)} %select_n.35, f32[256]{0:T(256)S(1)} %bitcast.31, f32[2,2048,256]{2,1,0:T(8,128)} %collective-permute-done, ...), kind=kLoop, calls=%fused_computation.6 | loop fusion | flops 6291456 | bytes 20972552 | tf_op jit(solution)/shard_map/add | solution.py:127
  114.9 0.3 dynamic-slice_bitcast_fusion
  115.3 1.6 collective-permute-start.2
  116.8 0.5 collective-permute-start.3
  117.4 44.1 %collective-permute-done.2 = f32[2048,256]{1,0:T(8,128)S(1)} collective-permute-done((f32[2048,256]{1,0:T(8,128)S(1)}, f32[2048,256]{1,0:T(8,128)S(1)}, u32[]{:S(2)}, u32[]{:S(2)}) %collective-permute-start.2) | collective-permute-done | bytes 2097184 | tf_op jit(solution)/shard_map/ppermute | solution.py:104
  161.5 0.3 bitcast_add_fusion.1
  161.8 1.0 collective-permute-done.3
  162.8 0.3 bitcast_add_fusion
  163.0 0.0 copy-start
  163.0 1.8 fusion.7
  164.9 1.8 fusion.2
  166.7 0.0 copy-done
  166.8 0.1 collective-permute-start.4
  166.8 1.4 collective-permute-done.4
  168.3 1.6 collective-permute-start.5
  169.9 5.4 %collective-permute-done.5 = f32[384,128]{1,0:T(8,128)S(1)} collective-permute-done((f32[384,128]{1,0:T(8,128)S(1)}, f32[384,128]{1,0:T(8,128)S(1)}, u32[]{:S(2)}, u32[]{:S(2)}) %collective-permute-start.5) | collective-permute-done | bytes 196640 | tf_op jit(solution)/shard_map/ppermute | solution.py:24
  175.3 2.7 %collective-permute-start.6 = (f32[384,128]{1,0:T(8,128)S(1)}, f32[384,128]{1,0:T(8,128)S(1)}, u32[]{:S(2)}, u32[]{:S(2)}) collective-permute-start(f32[384,128]{1,0:T(8,128)S(1)} %add.63), channel_id=1, source_target_pairs={{0,4},{1,5},{2,6},{3,7},{4,0},{5,1},{6,2},{7,3},{8,12},{9,13},{10,... | collective-permute-start | bytes 589832 | tf_op jit(solution)/shard_map/ppermute | solution.py:24
  178.0 8.6 %collective-permute-done.6 = f32[384,128]{1,0:T(8,128)S(1)} collective-permute-done((f32[384,128]{1,0:T(8,128)S(1)}, f32[384,128]{1,0:T(8,128)S(1)}, u32[]{:S(2)}, u32[]{:S(2)}) %collective-permute-start.6) | collective-permute-done | bytes 196640 | tf_op jit(solution)/shard_map/ppermute | solution.py:24
  186.6 0.7 collective-permute-start.7
  187.3 5.1 %collective-permute-done.7 = f32[384,128]{1,0:T(8,128)S(1)} collective-permute-done((f32[384,128]{1,0:T(8,128)S(1)}, f32[384,128]{1,0:T(8,128)S(1)}, u32[]{:S(2)}, u32[]{:S(2)}) %collective-permute-start.7) | collective-permute-done | bytes 196640 | tf_op jit(solution)/shard_map/ppermute | solution.py:24
  192.5 0.6 collective-permute-start.8
  193.1 5.1 %collective-permute-done.8 = f32[384,128]{1,0:T(8,128)S(1)} collective-permute-done((f32[384,128]{1,0:T(8,128)S(1)}, f32[384,128]{1,0:T(8,128)S(1)}, u32[]{:S(2)}, u32[]{:S(2)}) %collective-permute-start.8) | collective-permute-done | bytes 196640 | tf_op jit(solution)/shard_map/ppermute | solution.py:24
  198.2 0.7 add.66.gram_ref
  198.9 29.5 %shard_map.41 = (f32[256,256]{1,0:T(8,128)}, f32[256,256]{1,0:T(8,128)}) custom-call(f32[384,128]{1,0:T(8,128)} %add.66.gram_ref), custom_call_target="tpu_custom_call" | custom-call | tf_op jit(solution)/shard_map/pallas_call | solution.py:93
  228.4 5.4 %fusion.3 = f32[4096,256]{1,0:T(8,128)} fusion(f32[256,256]{1,0:T(8,128)} %get-tuple-element.12, f32[2048,256]{1,0:T(8,128)} %copy-done, f32[2048,256]{1,0:T(8,128)S(1)} %bitcast_add_fusion.1), kind=kOutput, calls=%fused_computation.12 | convolution fusion | flops 1611661312 | bytes 8650752 | tf_op jit(solution)/shard_map/dot_general | solution.py:16
  (6 shorter events, 0.1 us)
Async XLA Ops:
  0.7 7.1 %copy-start.1 = (f32[1,256]{1,0:T(1,128)S(1)}, f32[1,256]{1,0:T(1,128)}, u32[]{:S(2)}) copy-start(f32[1,256]{1,0:T(1,128)} %param.3) | copy-start | bytes 3076
  14.0 93.8 %collective-permute-start = (f32[2,2048,256]{2,1,0:T(8,128)}, f32[2,2048,256]{2,1,0:T(8,128)}, u32[]{:S(2)}, u32[]{:S(2)}) collective-permute-start(f32[2,2048,256]{2,1,0:T(8,128)} %get-tuple-element.8), channel_id=1, source_target_pairs={{0,8},{8,0},{16,24},{24,16},{1,9},{9,1},{17,25},{25,17},{2,10},{10... | collective-permute-start | bytes 12582920 | tf_op jit(solution)/shard_map/ppermute | solution.py:104
  16.9 92.3 %collective-permute-start.1 = (f32[2,2048,256]{2,1,0:T(8,128)}, f32[2,2048,256]{2,1,0:T(8,128)}, u32[]{:S(2)}, u32[]{:S(2)}) collective-permute-start(f32[2,2048,256]{2,1,0:T(8,128)} %get-tuple-element.9), channel_id=1, source_target_pairs={{0,16},{8,24},{16,0},{24,8},{1,17},{9,25},{17,1},{25,9},{2,18},{10... | collective-permute-start | bytes 12582920 | tf_op jit(solution)/shard_map/ppermute | solution.py:104
  115.3 46.2 %collective-permute-start.2 = (f32[2048,256]{1,0:T(8,128)S(1)}, f32[2048,256]{1,0:T(8,128)S(1)}, u32[]{:S(2)}, u32[]{:S(2)}) collective-permute-start(f32[2048,256]{1,0:T(8,128)S(1)} %get-tuple-element.10), channel_id=1, source_target_pairs={{0,16},{8,24},{16,0},{24,8},{1,17},{9,25},{17,1},{25,9},{2,18},{10... | collective-permute-start | bytes 6291464 | tf_op jit(solution)/shard_map/ppermute | solution.py:104
  116.8 45.9 %collective-permute-start.3 = (f32[2048,256]{1,0:T(8,128)S(1)}, f32[2048,256]{1,0:T(8,128)S(1)}, u32[]{:S(2)}, u32[]{:S(2)}) collective-permute-start(f32[2048,256]{1,0:T(8,128)S(1)} %get-tuple-element.11), channel_id=1, source_target_pairs={{0,8},{8,0},{16,24},{24,16},{1,9},{9,1},{17,25},{25,17},{2,10},{10... | collective-permute-start | bytes 6291464 | tf_op jit(solution)/shard_map/ppermute | solution.py:104
  163.0 3.7 %copy-start = (f32[2048,256]{1,0:T(8,128)}, f32[2048,256]{1,0:T(8,128)S(1)}, u32[]{:S(2)}) copy-start(f32[2048,256]{1,0:T(8,128)S(1)} %bitcast_add_fusion) | copy-start | bytes 6291460
  166.8 1.5 collective-permute-start.4
  168.3 7.0 %collective-permute-start.5 = (f32[384,128]{1,0:T(8,128)S(1)}, f32[384,128]{1,0:T(8,128)S(1)}, u32[]{:S(2)}, u32[]{:S(2)}) collective-permute-start(f32[384,128]{1,0:T(8,128)S(1)} %fusion.12), channel_id=1, source_target_pairs={{0,2},{1,3},{2,0},{3,1},{4,6},{5,7},{6,4},{7,5},{8,10},{9,11},{10,... | collective-permute-start | bytes 589832 | tf_op jit(solution)/shard_map/ppermute | solution.py:24
  175.3 11.3 %collective-permute-start.6 = (f32[384,128]{1,0:T(8,128)S(1)}, f32[384,128]{1,0:T(8,128)S(1)}, u32[]{:S(2)}, u32[]{:S(2)}) collective-permute-start(f32[384,128]{1,0:T(8,128)S(1)} %add.63), channel_id=1, source_target_pairs={{0,4},{1,5},{2,6},{3,7},{4,0},{5,1},{6,2},{7,3},{8,12},{9,13},{10,... | collective-permute-start | bytes 589832 | tf_op jit(solution)/shard_map/ppermute | solution.py:24
  186.6 5.8 %collective-permute-start.7 = (f32[384,128]{1,0:T(8,128)S(1)}, f32[384,128]{1,0:T(8,128)S(1)}, u32[]{:S(2)}, u32[]{:S(2)}) collective-permute-start(f32[384,128]{1,0:T(8,128)S(1)} %add.64), channel_id=1, source_target_pairs={{0,8},{1,9},{2,10},{3,11},{4,12},{5,13},{6,14},{7,15},{8,0},{9,1},... | collective-permute-start | bytes 589832 | tf_op jit(solution)/shard_map/ppermute | solution.py:24
  192.5 5.7 %collective-permute-start.8 = (f32[384,128]{1,0:T(8,128)S(1)}, f32[384,128]{1,0:T(8,128)S(1)}, u32[]{:S(2)}, u32[]{:S(2)}) collective-permute-start(f32[384,128]{1,0:T(8,128)S(1)} %add.65), channel_id=1, source_target_pairs={{0,16},{1,17},{2,18},{3,19},{4,20},{5,21},{6,22},{7,23},{8,24},{9,... | collective-permute-start | bytes 589832 | tf_op jit(solution)/shard_map/ppermute | solution.py:24

commit v9 on v8

--- a/solution.py
+++ b/solution.py
@@ -112,24 +112,25 @@
     shift = lax.axis_index("shift")
     low, high = shift % 2, shift // 2
     rows, width = filtered.shape[1], filtered.shape[2]
-    piece = rows // 8
-    blocks = filtered[0].reshape(2, 2, 2, piece, width)
-    scale = weights[0][None, None, :]
+    block, piece = rows // 4, rows // 8
+    scale = weights[0][None, :]
 
-    def weighted(x):
-        return x.astype(jnp.float32) * scale
+    def part(chunk, half):
+        start = chunk * block + half * piece
+        values = lax.dynamic_slice_in_dim(filtered[0], start, piece, axis=0)
+        return values.astype(jnp.float32) * scale
 
-    send_first = weighted(take(blocks[:, :, 0], 1 - low, 1))
-    send_second = weighted(take(blocks[:, :, 1], 1 - high, 0))
-    send_first, send_second = lax.optimization_barrier((send_first, send_second))
-    got_first, got_second = swap(send_first, 1), swap(send_second, 2)
-    first = weighted(take(blocks[:, :, 0], low, 1)) + got_first
-    second = weighted(take(blocks[:, :, 1], high, 0)) + got_second
-    send_first, send_second = take(first, 1 - high, 0), take(second, 1 - low, 0)
+    sends = [part(2 * hi + 1 - low, 0) for hi in range(2)] + [part(2 * (1 - high) + lo, 1) for lo in range(2)]
+    sends = lax.optimization_barrier(sends)
+    got = [swap(sends[0], 1), swap(sends[1], 1), swap(sends[2], 2), swap(sends[3], 2)]
+    first = [part(2 * hi + low, 0) + got[hi] for hi in range(2)]
+    second = [part(2 * high + lo, 1) + got[2 + lo] for lo in range(2)]
+    send_first = jnp.where(high == 0, first[1], first[0])
+    send_second = jnp.where(low == 0, second[1], second[0])
     send_first, send_second = lax.optimization_barrier((send_first, send_second))
     got_first, got_second = swap(send_first, 2), swap(send_second, 1)
-    first = take(first, high, 0) + got_first
-    second = take(second, low, 0) + got_second
+    first = jnp.where(high == 0, first[0], first[1]) + got_first
+    second = jnp.where(low == 0, second[0], second[1]) + got_second
     return jnp.concatenate([first, second], axis=0)
 
 

time: 234 us -> 231 us (0.987)
  local copies, waits for them, and re-layouts: 7.48 us -> 0.02 us
  other arithmetic: 13.2 us -> 17.2 us
  waiting for transfers between devices: 162 us -> 159 us
  starting transfers between devices: 12.2 us -> 15 us
    slice x1 -> x0, local copies, waits for them, and re-layouts: 7.12 us -> none  [mix_rows(): send_second = weighted(take(blocks[:, :, 1], 1 - high, 0))]
    select_n x0 -> x1, other arithmetic: none -> 5.01 us  [mix_rows(): send_second = jnp.where(low == 0, second[1], second[0])]
    ppermute x4 -> x6, starting transfers between devices: 6.58 us -> 8.32 us  [swap(): return lax.ppermute(x, 'shift', [(i, i ^ bit) for i in range(size)])]
    ppermute x4 -> x6, waiting for transfers between devices: 136 us -> 134 us  [swap(): return lax.ppermute(x, 'shift', [(i, i ^ bit) for i in range(size)])]
    add x3 -> x1, other arithmetic: 6.18 us -> 5.75 us  [mix_rows(): second = jnp.where(low == 0, second[0], second[1]) + got_second]
  transfers between devices with their start and end apart: 9 -> 11, of which waited for: 9 -> 10; matrix products, arithmetic and copies ran while one was open for 0% -> 0% of each run, Pallas kernels for 0% -> 0%
where the time goes in v9:
time: 231 us
  waiting for transfers between devices  159 us (69%)
  Pallas kernels  29.5 us (13%)
  other arithmetic  17.2 us (7%)
  starting transfers between devices  15 us (6%)
  matrix products  9.07 us (4%)
    ppermute x6, waiting for transfers between devices, swap(): return lax.ppermute(x, 'shift', [(i, i ^ bit) for i in range(size)])  134 us
    pallas_call x1, Pallas kernels, factor(): pl.pallas_call(factor_kernel, out_shape=(jax.ShapeDtypeStruct((n, n), jnp...  29.5 us
    ppermute x5, waiting for transfers between devices, butterfly_sum(): x = x + lax.ppermute(x, axes, pairs)  24.7 us
    ppermute x6, starting transfers between devices, swap(): return lax.ppermute(x, 'shift', [(i, i ^ bit) for i in range(size)])  8.32 us
    ppermute x5, starting transfers between devices, butterfly_sum(): x = x + lax.ppermute(x, axes, pairs)  6.65 us
    add x1, other arithmetic, mix_rows(): second = jnp.where(low == 0, second[0], second[1]) + got_second  5.75 us
    mul x1, other arithmetic, part(): return values.astype(jnp.float32) * scale  5.66 us
    dot_general x1, matrix products, dot_high(): jnp.dot(a, b, precision=lax.Precision.HIGH, preferred_element_type=jnp.fl...  5.41 us
  transfers between devices with their start and end apart: 11, of which 10 were waited for; matrix products, arithmetic and copies ran while one was open for 0% of the time, Pallas kernels for 0%

profile of v9, /device:TPU:0, one launch (start us, length us, event | category | flops | bytes accessed | tf_op | source)
XLA Modules:
  0.0 230.7 jit_solution(13150215859093778036)
XLA Ops:
  0.7 0.0 copy-start.2
  0.7 5.7 %convert_multiply_fusion.3 = (f32[2048,256]{1,0:T(8,128)}, f32[2048,256]{1,0:T(8,128)}, f32[2048,256]{1,0:T(8,128)}, f32[2048,256]{1,0:T(8,128)}) fusion(bf16[1,16384,256]{2,1,0:T(8,128)(2,1)} %param.2, s32[]{:T(128)S(6)} %select_n.64, f32[256]{0:T(256)} %bitcast.30, s32[]{:T(128)S(6)} %select_n.63, s32[]{:T(128)S(6)} %select_n.62, s32[]{:T(128)S(6)} %select_n.61), kind=kLoop, calls=%fused_computation.16 | loop fusion | flops 4194304 | bytes 12583952 | tf_op jit(solution)/shard_map/mul | solution.py:121
  6.3 2.9 %collective-permute-start = (f32[2048,256]{1,0:T(8,128)}, f32[2048,256]{1,0:T(8,128)S(1)}, u32[]{:S(2)}, u32[]{:S(2)}) collective-permute-start(f32[2048,256]{1,0:T(8,128)} %get-tuple-element.10), channel_id=1, source_target_pairs={{0,8},{8,0},{16,24},{24,16},{1,9},{9,1},{17,25},{25,17},{2,10},{10... | collective-permute-start | bytes 6291464 | tf_op jit(solution)/shard_map/ppermute | solution.py:104
  9.3 0.0 collective-permute-start.1
  9.3 2.0 collective-permute-start.2
  11.3 0.0 collective-permute-start.3
  11.4 44.6 %collective-permute-done = f32[2048,256]{1,0:T(8,128)S(1)} collective-permute-done((f32[2048,256]{1,0:T(8,128)}, f32[2048,256]{1,0:T(8,128)S(1)}, u32[]{:S(2)}, u32[]{:S(2)}) %collective-permute-start) | collective-permute-done | bytes 2097184 | tf_op jit(solution)/shard_map/ppermute | solution.py:104
  55.9 0.0 copy-start.1
  55.9 44.2 %collective-permute-done.1 = f32[2048,256]{1,0:T(8,128)} collective-permute-done((f32[2048,256]{1,0:T(8,128)}, f32[2048,256]{1,0:T(8,128)}, u32[]{:S(2)}, u32[]{:S(2)}) %collective-permute-start.1) | collective-permute-done | bytes 2097184 | tf_op jit(solution)/shard_map/ppermute | solution.py:104
  100.2 0.0 collective-permute-done.2
  100.2 1.5 collective-permute-done.3
  101.7 0.0 copy-done.2
  101.7 5.0 %fusion.12 = (f32[2048,256]{1,0:T(8,128)S(1)}, f32[2048,256]{1,0:T(8,128)S(1)}) fusion(f32[2048,256]{1,0:T(8,128)} %collective-permute-done.2, f32[2048,256]{1,0:T(8,128)} %collective-permute-done.3, f32[256]{0:T(256)S(1)} %bitcast.31, pred[]{:T(512)S(6)} %eq.11, bf16[1,16384,256]{2,1,0:T(8,128)(2,1)} %param.2, s32[]{:T(128)S(6)} %select_n.70, ...), kind=kLoop, calls=%fused_computation.25 | loop fusion | flops 7340032 | bytes 16778258 | tf_op jit(solution)/shard_map/jit(_where)/select_n | solution.py:129
  106.7 0.0 copy-done.1
  106.7 1.8 collective-permute-start.4
  108.5 1.5 collective-permute-start.5
  110.0 42.9 %collective-permute-done.4 = f32[2048,256]{1,0:T(8,128)S(1)} collective-permute-done((f32[2048,256]{1,0:T(8,128)S(1)}, f32[2048,256]{1,0:T(8,128)S(1)}, u32[]{:S(2)}, u32[]{:S(2)}) %collective-permute-start.4) | collective-permute-done | bytes 2097184 | tf_op jit(solution)/shard_map/ppermute | solution.py:104
  152.9 1.2 collective-permute-done.5
  154.1 5.8 %select_add_fusion = (f32[2048,256]{1,0:T(8,128)S(1)}, f32[2048,256]{1,0:T(8,128)S(1)}) fusion(f32[2048,256]{1,0:T(8,128)S(1)} %collective-permute-done.5, f32[2048,256]{1,0:T(8,128)} %collective-permute-done.2, f32[2048,256]{1,0:T(8,128)} %collective-permute-done.3, f32[256]{0:T(256)S(1)} %bitcast.32, pred[]{:T(512)S(6)} %eq.11, ...), kind=kLoop, calls=%fused_computation.22 | loop fusion | flops 8388608 | bytes 20972562 | tf_op jit(solution)/shard_map/add | solution.py:133
  159.9 0.0 copy-start
  159.9 1.8 fusion.5
  161.7 0.0 copy-done
  161.7 1.8 fusion
  163.6 0.1 collective-permute-start.6
  163.7 1.4 collective-permute-done.6
  165.1 1.6 collective-permute-start.7
  166.8 5.4 %collective-permute-done.7 = f32[384,128]{1,0:T(8,128)S(1)} collective-permute-done((f32[384,128]{1,0:T(8,128)S(1)}, f32[384,128]{1,0:T(8,128)S(1)}, u32[]{:S(2)}, u32[]{:S(2)}) %collective-permute-start.7) | collective-permute-done | bytes 196640 | tf_op jit(solution)/shard_map/ppermute | solution.py:24
  172.2 2.7 %collective-permute-start.8 = (f32[384,128]{1,0:T(8,128)S(1)}, f32[384,128]{1,0:T(8,128)S(1)}, u32[]{:S(2)}, u32[]{:S(2)}) collective-permute-start(f32[384,128]{1,0:T(8,128)S(1)} %add.114), channel_id=1, source_target_pairs={{0,4},{1,5},{2,6},{3,7},{4,0},{5,1},{6,2},{7,3},{8,12},{9,13},{10,... | collective-permute-start | bytes 589832 | tf_op jit(solution)/shard_map/ppermute | solution.py:24
  174.8 8.6 %collective-permute-done.8 = f32[384,128]{1,0:T(8,128)S(1)} collective-permute-done((f32[384,128]{1,0:T(8,128)S(1)}, f32[384,128]{1,0:T(8,128)S(1)}, u32[]{:S(2)}, u32[]{:S(2)}) %collective-permute-start.8) | collective-permute-done | bytes 196640 | tf_op jit(solution)/shard_map/ppermute | solution.py:24
  183.5 1.6 collective-permute-start.9
  185.0 4.3 %collective-permute-done.9 = f32[384,128]{1,0:T(8,128)S(1)} collective-permute-done((f32[384,128]{1,0:T(8,128)S(1)}, f32[384,128]{1,0:T(8,128)S(1)}, u32[]{:S(2)}, u32[]{:S(2)}) %collective-permute-start.9) | collective-permute-done | bytes 196640 | tf_op jit(solution)/shard_map/ppermute | solution.py:24
  189.3 0.7 collective-permute-start.10
  190.0 5.0 %collective-permute-done.10 = f32[384,128]{1,0:T(8,128)S(1)} collective-permute-done((f32[384,128]{1,0:T(8,128)S(1)}, f32[384,128]{1,0:T(8,128)S(1)}, u32[]{:S(2)}, u32[]{:S(2)}) %collective-permute-start.10) | collective-permute-done | bytes 196640 | tf_op jit(solution)/shard_map/ppermute | solution.py:24
  195.0 0.7 add.117.gram_ref
  195.7 29.5 %shard_map.41 = (f32[256,256]{1,0:T(8,128)}, f32[256,256]{1,0:T(8,128)}) custom-call(f32[384,128]{1,0:T(8,128)} %add.117.gram_ref), custom_call_target="tpu_custom_call" | custom-call | tf_op jit(solution)/shard_map/pallas_call | solution.py:93
  225.3 5.4 %fusion.1 = f32[4096,256]{1,0:T(8,128)} fusion(f32[256,256]{1,0:T(8,128)} %get-tuple-element.16, f32[2048,256]{1,0:T(8,128)S(1)} %get-tuple-element.18, f32[2048,256]{1,0:T(8,128)} %copy-done), kind=kOutput, calls=%fused_computation.6 | convolution fusion | flops 1611661312 | bytes 8650752 | tf_op jit(solution)/shard_map/dot_general | solution.py:16
  (6 shorter events, 0.1 us)
Async XLA Ops:
  0.7 101.0 %copy-start.2 = (f32[1,256]{1,0:T(1,128)S(1)}, f32[1,256]{1,0:T(1,128)}, u32[]{:S(2)}) copy-start(f32[1,256]{1,0:T(1,128)} %param.3) | copy-start | bytes 3076
  6.3 49.6 %collective-permute-start = (f32[2048,256]{1,0:T(8,128)}, f32[2048,256]{1,0:T(8,128)S(1)}, u32[]{:S(2)}, u32[]{:S(2)}) collective-permute-start(f32[2048,256]{1,0:T(8,128)} %get-tuple-element.10), channel_id=1, source_target_pairs={{0,8},{8,0},{16,24},{24,16},{1,9},{9,1},{17,25},{25,17},{2,10},{10... | collective-permute-start | bytes 6291464 | tf_op jit(solution)/shard_map/ppermute | solution.py:104
  9.3 90.9 %collective-permute-start.1 = (f32[2048,256]{1,0:T(8,128)}, f32[2048,256]{1,0:T(8,128)}, u32[]{:S(2)}, u32[]{:S(2)}) collective-permute-start(f32[2048,256]{1,0:T(8,128)} %get-tuple-element.11), channel_id=1, source_target_pairs={{0,8},{8,0},{16,24},{24,16},{1,9},{9,1},{17,25},{25,17},{2,10},{10... | collective-permute-start | bytes 6291464 | tf_op jit(solution)/shard_map/ppermute | solution.py:104
  9.3 90.9 %collective-permute-start.2 = (f32[2048,256]{1,0:T(8,128)}, f32[2048,256]{1,0:T(8,128)}, u32[]{:S(2)}, u32[]{:S(2)}) collective-permute-start(f32[2048,256]{1,0:T(8,128)} %get-tuple-element.12), channel_id=1, source_target_pairs={{0,16},{8,24},{16,0},{24,8},{1,17},{9,25},{17,1},{25,9},{2,18},{10... | collective-permute-start | bytes 6291464 | tf_op jit(solution)/shard_map/ppermute | solution.py:104
  11.3 90.3 %collective-permute-start.3 = (f32[2048,256]{1,0:T(8,128)}, f32[2048,256]{1,0:T(8,128)}, u32[]{:S(2)}, u32[]{:S(2)}) collective-permute-start(f32[2048,256]{1,0:T(8,128)} %get-tuple-element.13), channel_id=1, source_target_pairs={{0,16},{8,24},{16,0},{24,8},{1,17},{9,25},{17,1},{25,9},{2,18},{10... | collective-permute-start | bytes 6291464 | tf_op jit(solution)/shard_map/ppermute | solution.py:104
  55.9 50.7 %copy-start.1 = (f32[2048,256]{1,0:T(8,128)}, f32[2048,256]{1,0:T(8,128)S(1)}, u32[]{:S(2)}) copy-start(f32[2048,256]{1,0:T(8,128)S(1)} %collective-permute-done) | copy-start | bytes 6291460
  106.7 46.2 %collective-permute-start.4 = (f32[2048,256]{1,0:T(8,128)S(1)}, f32[2048,256]{1,0:T(8,128)S(1)}, u32[]{:S(2)}, u32[]{:S(2)}) collective-permute-start(f32[2048,256]{1,0:T(8,128)S(1)} %get-tuple-element.14), channel_id=1, source_target_pairs={{0,16},{8,24},{16,0},{24,8},{1,17},{9,25},{17,1},{25,9},{2,18},{10... | collective-permute-start | bytes 6291464 | tf_op jit(solution)/shard_map/ppermute | solution.py:104
  108.5 45.6 %collective-permute-start.5 = (f32[2048,256]{1,0:T(8,128)S(1)}, f32[2048,256]{1,0:T(8,128)S(1)}, u32[]{:S(2)}, u32[]{:S(2)}) collective-permute-start(f32[2048,256]{1,0:T(8,128)S(1)} %get-tuple-element.15), channel_id=1, source_target_pairs={{0,8},{8,0},{16,24},{24,16},{1,9},{9,1},{17,25},{25,17},{2,10},{10... | collective-permute-start | bytes 6291464 | tf_op jit(solution)/shard_map/ppermute | solution.py:104
  159.9 1.8 copy-start
  163.6 1.5 collective-permute-start.6
  165.1 7.0 %collective-permute-start.7 = (f32[384,128]{1,0:T(8,128)S(1)}, f32[384,128]{1,0:T(8,128)S(1)}, u32[]{:S(2)}, u32[]{:S(2)}) collective-permute-start(f32[384,128]{1,0:T(8,128)S(1)} %fusion.16), channel_id=1, source_target_pairs={{0,2},{1,3},{2,0},{3,1},{4,6},{5,7},{6,4},{7,5},{8,10},{9,11},{10,... | collective-permute-start | bytes 589832 | tf_op jit(solution)/shard_map/ppermute | solution.py:24
  172.2 11.3 %collective-permute-start.8 = (f32[384,128]{1,0:T(8,128)S(1)}, f32[384,128]{1,0:T(8,128)S(1)}, u32[]{:S(2)}, u32[]{:S(2)}) collective-permute-start(f32[384,128]{1,0:T(8,128)S(1)} %add.114), channel_id=1, source_target_pairs={{0,4},{1,5},{2,6},{3,7},{4,0},{5,1},{6,2},{7,3},{8,12},{9,13},{10,... | collective-permute-start | bytes 589832 | tf_op jit(solution)/shard_map/ppermute | solution.py:24
  183.5 5.8 %collective-permute-start.9 = (f32[384,128]{1,0:T(8,128)S(1)}, f32[384,128]{1,0:T(8,128)S(1)}, u32[]{:S(2)}, u32[]{:S(2)}) collective-permute-start(f32[384,128]{1,0:T(8,128)S(1)} %add.115), channel_id=1, source_target_pairs={{0,8},{1,9},{2,10},{3,11},{4,12},{5,13},{6,14},{7,15},{8,0},{9,1},... | collective-permute-start | bytes 589832 | tf_op jit(solution)/shard_map/ppermute | solution.py:24
  189.3 5.7 %collective-permute-start.10 = (f32[384,128]{1,0:T(8,128)S(1)}, f32[384,128]{1,0:T(8,128)S(1)}, u32[]{:S(2)}, u32[]{:S(2)}) collective-permute-start(f32[384,128]{1,0:T(8,128)S(1)} %add.116), channel_id=1, source_target_pairs={{0,16},{1,17},{2,18},{3,19},{4,20},{5,21},{6,22},{7,23},{8,24},{9,... | collective-permute-start | bytes 589832 | tf_op jit(solution)/shard_map/ppermute | solution.py:24

commit v10 on v9

--- a/solution.py
+++ b/solution.py
@@ -120,17 +120,20 @@
         values = lax.dynamic_slice_in_dim(filtered[0], start, piece, axis=0)
         return values.astype(jnp.float32) * scale
 
-    sends = [part(2 * hi + 1 - low, 0) for hi in range(2)] + [part(2 * (1 - high) + lo, 1) for lo in range(2)]
-    sends = lax.optimization_barrier(sends)
-    got = [swap(sends[0], 1), swap(sends[1], 1), swap(sends[2], 2), swap(sends[3], 2)]
-    first = [part(2 * hi + low, 0) + got[hi] for hi in range(2)]
-    second = [part(2 * high + lo, 1) + got[2 + lo] for lo in range(2)]
-    send_first = jnp.where(high == 0, first[1], first[0])
-    send_second = jnp.where(low == 0, second[1], second[0])
+    forward_x = part(2 * (1 - high) + 1 - low, 0)
+    forward_y = part(2 * (1 - high) + 1 - low, 1)
+    forward_x, forward_y = lax.optimization_barrier((forward_x, forward_y))
+    got_forward_x, got_forward_y = swap(forward_x, 1), swap(forward_y, 2)
+    stay_x = part(2 * high + 1 - low, 0)
+    stay_y = part(2 * (1 - high) + low, 1)
+    stay_x, stay_y = lax.optimization_barrier((stay_x, stay_y))
+    got_stay_x, got_stay_y = swap(stay_x, 1), swap(stay_y, 2)
+    send_first = part(2 * (1 - high) + low, 0) + got_forward_x
+    send_second = part(2 * high + 1 - low, 1) + got_forward_y
     send_first, send_second = lax.optimization_barrier((send_first, send_second))
     got_first, got_second = swap(send_first, 2), swap(send_second, 1)
-    first = jnp.where(high == 0, first[0], first[1]) + got_first
-    second = jnp.where(low == 0, second[0], second[1]) + got_second
+    first = part(2 * high + low, 0) + got_stay_x + got_first
+    second = part(2 * high + low, 1) + got_stay_y + got_second
     return jnp.concatenate([first, second], axis=0)
 
 

time: 231 us -> 222 us (0.961)
  waiting for transfers between devices: 159 us -> 153 us
    ppermute x6, waiting for transfers between devices: 134 us -> 128 us  [swap(): return lax.ppermute(x, 'shift', [(i, i ^ bit) for i in range(size)])]
    select_n x1 -> x0, other arithmetic: 5.01 us -> none  [mix_rows(): send_second = jnp.where(low == 0, second[1], second[0])]
    add x1 -> x2, other arithmetic: 5.75 us -> 10.1 us  [the longest x1 5.34 us: mix_rows(): send_second = part(2 * high + 1 - low, 1) + got_forward_y]
  transfers between devices with their start and end apart: 11 -> 11, of which waited for: 10 -> 10; matrix products, arithmetic and copies ran while one was open for 0% -> 2% of each run, Pallas kernels for 0% -> 0%
where the time goes in v10:
time: 222 us
  waiting for transfers between devices  153 us (69%)
  Pallas kernels  29.5 us (13%)
  other arithmetic  15.9 us (7%)
  starting transfers between devices  13.6 us (6%)
  matrix products  9.07 us (4%)
    ppermute x6, waiting for transfers between devices, swap(): return lax.ppermute(x, 'shift', [(i, i ^ bit) for i in range(size)])  128 us
    pallas_call x1, Pallas kernels, factor(): pl.pallas_call(factor_kernel, out_shape=(jax.ShapeDtypeStruct((n, n), jnp...  29.5 us
    ppermute x5, waiting for transfers between devices, butterfly_sum(): x = x + lax.ppermute(x, axes, pairs)  24.8 us
    ppermute x6, starting transfers between devices, swap(): return lax.ppermute(x, 'shift', [(i, i ^ bit) for i in range(size)])  7.05 us
    ppermute x5, starting transfers between devices, butterfly_sum(): x = x + lax.ppermute(x, axes, pairs)  6.5 us
    dot_general x1, matrix products, dot_high(): jnp.dot(a, b, precision=lax.Precision.HIGH, preferred_element_type=jnp.fl...  5.42 us
    add x1, other arithmetic, mix_rows(): send_second = part(2 * high + 1 - low, 1) + got_forward_y  5.34 us
    mul x1, other arithmetic, part(): return values.astype(jnp.float32) * scale  5.05 us
  transfers between devices with their start and end apart: 11, of which 10 were waited for; matrix products, arithmetic and copies ran while one was open for 2% of the time, Pallas kernels for 0%

profile of v10, /device:TPU:0, one launch (start us, length us, event | category | flops | bytes accessed | tf_op | source)
XLA Modules:
  0.0 221.6 jit_solution(1062952615966482763)
XLA Ops:
  0.7 0.0 copy-start.1
  0.7 5.0 %convert_multiply_fusion.5 = (f32[2048,256]{1,0:T(8,128)S(1)}, f32[2048,256]{1,0:T(8,128)}, f32[2048,256]{1,0:T(8,128)}, f32[2048,256]{1,0:T(8,128)}) fusion(bf16[1,16384,256]{2,1,0:T(8,128)(2,1)} %param.2, s32[]{:T(128)S(6)} %select_n.39, f32[256]{0:T(256)} %bitcast.26, s32[]{:T(128)S(6)} %select_n.42, s32[]{:T(128)S(6)} %select_n.41, s32[]{:T(128)S(6)} %select_n.38), kind=kLoop, calls=%fused_computation.19 | loop fusion | flops 4194304 | bytes 12583952 | tf_op jit(solution)/shard_map/mul | solution.py:121
  5.7 2.9 %collective-permute-start.1 = (f32[2048,256]{1,0:T(8,128)}, f32[2048,256]{1,0:T(8,128)}, u32[]{:S(2)}, u32[]{:S(2)}) collective-permute-start(f32[2048,256]{1,0:T(8,128)} %get-tuple-element.11), channel_id=1, source_target_pairs={{0,8},{8,0},{16,24},{24,16},{1,9},{9,1},{17,25},{25,17},{2,10},{10... | collective-permute-start | bytes 6291464 | tf_op jit(solution)/shard_map/ppermute | solution.py:104
  8.7 1.5 collective-permute-start.2
  10.2 0.5 collective-permute-start
  10.7 0.0 collective-permute-start.4
  10.7 44.7 %collective-permute-done.1 = f32[2048,256]{1,0:T(8,128)} collective-permute-done((f32[2048,256]{1,0:T(8,128)}, f32[2048,256]{1,0:T(8,128)}, u32[]{:S(2)}, u32[]{:S(2)}) %collective-permute-start.1) | collective-permute-done | bytes 2097184 | tf_op jit(solution)/shard_map/ppermute | solution.py:104
  55.4 2.1 collective-permute-done.2
  57.5 0.0 copy-done.1
  57.5 5.3 %fusion.9 = (f32[2048,256]{1,0:T(8,128)}, f32[2048,256]{1,0:T(8,128)}) fusion(f32[2048,256]{1,0:T(8,128)} %collective-permute-done.2, bf16[1,16384,256]{2,1,0:T(8,128)(2,1)} %param.2, s32[]{:T(128)S(6)} %select_n.43, f32[256]{0:T(256)S(1)} %bitcast.27, f32[2048,256]{1,0:T(8,128)} %collective-permute-done.1, s32[]{:T(128)S(6)} %select_n.40), kind=kLoop, calls=%fused_computation.14 | loop fusion | flops 3145728 | bytes 10486792 | tf_op jit(solution)/shard_map/add | solution.py:132
  62.9 1.5 collective-permute-start.3
  64.4 0.5 collective-permute-start.5
  64.9 35.4 %collective-permute-done = f32[2048,256]{1,0:T(8,128)} collective-permute-done((f32[2048,256]{1,0:T(8,128)}, f32[2048,256]{1,0:T(8,128)}, u32[]{:S(2)}, u32[]{:S(2)}) %collective-permute-start) | collective-permute-done | bytes 2097184 | tf_op jit(solution)/shard_map/ppermute | solution.py:104
  100.4 2.1 collective-permute-done.4
  102.5 43.5 %collective-permute-done.3 = f32[2048,256]{1,0:T(8,128)} collective-permute-done((f32[2048,256]{1,0:T(8,128)}, f32[2048,256]{1,0:T(8,128)}, u32[]{:S(2)}, u32[]{:S(2)}) %collective-permute-start.3) | collective-permute-done | bytes 2097184 | tf_op jit(solution)/shard_map/ppermute | solution.py:104
  146.0 0.0 collective-permute-done.5
  146.0 4.7 %fusion.8 = (f32[2048,256]{1,0:T(8,128)S(1)}, f32[2048,256]{1,0:T(8,128)S(1)}) fusion(f32[2048,256]{1,0:T(8,128)} %collective-permute-done.5, f32[2048,256]{1,0:T(8,128)} %collective-permute-done.4, bf16[1,16384,256]{2,1,0:T(8,128)(2,1)} %param.2, s32[]{:T(128)S(6)} %select_n.44, f32[256]{0:T(256)S(1)} %bitcast.28, f32[2048,256]{1,0:T(8,128)} %collective-permute-done.3, ...), kind=kLoop, calls=%fused_computation.12 | loop fusion | flops 4194304 | bytes 14681096 | tf_op jit(solution)/shard_map/add | solution.py:136
  150.7 0.0 copy-start
  150.7 1.8 fusion.5
  152.5 0.0 copy-done
  152.6 1.8 fusion
  154.4 0.1 collective-permute-start.6
  154.5 1.4 collective-permute-done.6
  156.0 1.6 collective-permute-start.7
  157.6 5.4 %collective-permute-done.7 = f32[384,128]{1,0:T(8,128)S(1)} collective-permute-done((f32[384,128]{1,0:T(8,128)S(1)}, f32[384,128]{1,0:T(8,128)S(1)}, u32[]{:S(2)}, u32[]{:S(2)}) %collective-permute-start.7) | collective-permute-done | bytes 196640 | tf_op jit(solution)/shard_map/ppermute | solution.py:24
  163.0 2.7 %collective-permute-start.8 = (f32[384,128]{1,0:T(8,128)S(1)}, f32[384,128]{1,0:T(8,128)S(1)}, u32[]{:S(2)}, u32[]{:S(2)}) collective-permute-start(f32[384,128]{1,0:T(8,128)S(1)} %add.122), channel_id=1, source_target_pairs={{0,4},{1,5},{2,6},{3,7},{4,0},{5,1},{6,2},{7,3},{8,12},{9,13},{10,... | collective-permute-start | bytes 589832 | tf_op jit(solution)/shard_map/ppermute | solution.py:24
  165.7 8.6 %collective-permute-done.8 = f32[384,128]{1,0:T(8,128)S(1)} collective-permute-done((f32[384,128]{1,0:T(8,128)S(1)}, f32[384,128]{1,0:T(8,128)S(1)}, u32[]{:S(2)}, u32[]{:S(2)}) %collective-permute-start.8) | collective-permute-done | bytes 196640 | tf_op jit(solution)/shard_map/ppermute | solution.py:24
  174.3 0.6 collective-permute-start.9
  174.9 5.3 %collective-permute-done.9 = f32[384,128]{1,0:T(8,128)S(1)} collective-permute-done((f32[384,128]{1,0:T(8,128)S(1)}, f32[384,128]{1,0:T(8,128)S(1)}, u32[]{:S(2)}, u32[]{:S(2)}) %collective-permute-start.9) | collective-permute-done | bytes 196640 | tf_op jit(solution)/shard_map/ppermute | solution.py:24
  180.2 1.6 collective-permute-start.10
  181.8 4.2 %collective-permute-done.10 = f32[384,128]{1,0:T(8,128)S(1)} collective-permute-done((f32[384,128]{1,0:T(8,128)S(1)}, f32[384,128]{1,0:T(8,128)S(1)}, u32[]{:S(2)}, u32[]{:S(2)}) %collective-permute-start.10) | collective-permute-done | bytes 196640 | tf_op jit(solution)/shard_map/ppermute | solution.py:24
  185.9 0.7 add.125.gram_ref
  186.6 29.5 %shard_map.41 = (f32[256,256]{1,0:T(8,128)}, f32[256,256]{1,0:T(8,128)}) custom-call(f32[384,128]{1,0:T(8,128)} %add.125.gram_ref), custom_call_target="tpu_custom_call" | custom-call | tf_op jit(solution)/shard_map/pallas_call | solution.py:93
  216.1 5.4 %fusion.1 = f32[4096,256]{1,0:T(8,128)} fusion(f32[256,256]{1,0:T(8,128)} %get-tuple-element.16, f32[2048,256]{1,0:T(8,128)S(1)} %get-tuple-element.18, f32[2048,256]{1,0:T(8,128)} %copy-done), kind=kOutput, calls=%fused_computation.6 | convolution fusion | flops 1611661312 | bytes 8650752 | tf_op jit(solution)/shard_map/dot_general | solution.py:16
  (6 shorter events, 0.1 us)
Async XLA Ops:
  0.7 56.9 %copy-start.1 = (f32[1,256]{1,0:T(1,128)S(1)}, f32[1,256]{1,0:T(1,128)}, u32[]{:S(2)}) copy-start(f32[1,256]{1,0:T(1,128)} %param.3) | copy-start | bytes 3076
  5.7 49.7 %collective-permute-start.1 = (f32[2048,256]{1,0:T(8,128)}, f32[2048,256]{1,0:T(8,128)}, u32[]{:S(2)}, u32[]{:S(2)}) collective-permute-start(f32[2048,256]{1,0:T(8,128)} %get-tuple-element.11), channel_id=1, source_target_pairs={{0,8},{8,0},{16,24},{24,16},{1,9},{9,1},{17,25},{25,17},{2,10},{10... | collective-permute-start | bytes 6291464 | tf_op jit(solution)/shard_map/ppermute | solution.py:104
  8.7 48.9 %collective-permute-start.2 = (f32[2048,256]{1,0:T(8,128)}, f32[2048,256]{1,0:T(8,128)}, u32[]{:S(2)}, u32[]{:S(2)}) collective-permute-start(f32[2048,256]{1,0:T(8,128)} %get-tuple-element.12), channel_id=1, source_target_pairs={{0,16},{8,24},{16,0},{24,8},{1,17},{9,25},{17,1},{25,9},{2,18},{10... | collective-permute-start | bytes 6291464 | tf_op jit(solution)/shard_map/ppermute | solution.py:104
  10.2 90.2 %collective-permute-start = (f32[2048,256]{1,0:T(8,128)}, f32[2048,256]{1,0:T(8,128)}, u32[]{:S(2)}, u32[]{:S(2)}) collective-permute-start(f32[2048,256]{1,0:T(8,128)} %get-tuple-element.10), channel_id=1, source_target_pairs={{0,8},{8,0},{16,24},{24,16},{1,9},{9,1},{17,25},{25,17},{2,10},{10... | collective-permute-start | bytes 6291464 | tf_op jit(solution)/shard_map/ppermute | solution.py:104
  10.7 91.8 %collective-permute-start.4 = (f32[2048,256]{1,0:T(8,128)S(1)}, f32[2048,256]{1,0:T(8,128)}, u32[]{:S(2)}, u32[]{:S(2)}) collective-permute-start(f32[2048,256]{1,0:T(8,128)S(1)} %get-tuple-element.14), channel_id=1, source_target_pairs={{0,16},{8,24},{16,0},{24,8},{1,17},{9,25},{17,1},{25,9},{2,18},{10... | collective-permute-start | bytes 6291464 | tf_op jit(solution)/shard_map/ppermute | solution.py:104
  62.9 83.1 %collective-permute-start.3 = (f32[2048,256]{1,0:T(8,128)}, f32[2048,256]{1,0:T(8,128)}, u32[]{:S(2)}, u32[]{:S(2)}) collective-permute-start(f32[2048,256]{1,0:T(8,128)} %get-tuple-element.13), channel_id=1, source_target_pairs={{0,16},{8,24},{16,0},{24,8},{1,17},{9,25},{17,1},{25,9},{2,18},{10... | collective-permute-start | bytes 6291464 | tf_op jit(solution)/shard_map/ppermute | solution.py:104
  64.4 81.6 %collective-permute-start.5 = (f32[2048,256]{1,0:T(8,128)}, f32[2048,256]{1,0:T(8,128)}, u32[]{:S(2)}, u32[]{:S(2)}) collective-permute-start(f32[2048,256]{1,0:T(8,128)} %get-tuple-element.15), channel_id=1, source_target_pairs={{0,8},{8,0},{16,24},{24,16},{1,9},{9,1},{17,25},{25,17},{2,10},{10... | collective-permute-start | bytes 6291464 | tf_op jit(solution)/shard_map/ppermute | solution.py:104
  150.7 1.8 copy-start
  154.4 1.5 collective-permute-start.6
  156.0 7.0 %collective-permute-start.7 = (f32[384,128]{1,0:T(8,128)S(1)}, f32[384,128]{1,0:T(8,128)S(1)}, u32[]{:S(2)}, u32[]{:S(2)}) collective-permute-start(f32[384,128]{1,0:T(8,128)S(1)} %fusion.16), channel_id=1, source_target_pairs={{0,2},{1,3},{2,0},{3,1},{4,6},{5,7},{6,4},{7,5},{8,10},{9,11},{10,... | collective-permute-start | bytes 589832 | tf_op jit(solution)/shard_map/ppermute | solution.py:24
  163.0 11.3 %collective-permute-start.8 = (f32[384,128]{1,0:T(8,128)S(1)}, f32[384,128]{1,0:T(8,128)S(1)}, u32[]{:S(2)}, u32[]{:S(2)}) collective-permute-start(f32[384,128]{1,0:T(8,128)S(1)} %add.122), channel_id=1, source_target_pairs={{0,4},{1,5},{2,6},{3,7},{4,0},{5,1},{6,2},{7,3},{8,12},{9,13},{10,... | collective-permute-start | bytes 589832 | tf_op jit(solution)/shard_map/ppermute | solution.py:24
  174.3 5.8 %collective-permute-start.9 = (f32[384,128]{1,0:T(8,128)S(1)}, f32[384,128]{1,0:T(8,128)S(1)}, u32[]{:S(2)}, u32[]{:S(2)}) collective-permute-start(f32[384,128]{1,0:T(8,128)S(1)} %add.123), channel_id=1, source_target_pairs={{0,8},{1,9},{2,10},{3,11},{4,12},{5,13},{6,14},{7,15},{8,0},{9,1},... | collective-permute-start | bytes 589832 | tf_op jit(solution)/shard_map/ppermute | solution.py:24
  180.2 5.7 %collective-permute-start.10 = (f32[384,128]{1,0:T(8,128)S(1)}, f32[384,128]{1,0:T(8,128)S(1)}, u32[]{:S(2)}, u32[]{:S(2)}) collective-permute-start(f32[384,128]{1,0:T(8,128)S(1)} %add.124), channel_id=1, source_target_pairs={{0,16},{1,17},{2,18},{3,19},{4,20},{5,21},{6,22},{7,23},{8,24},{9,... | collective-permute-start | bytes 589832 | tf_op jit(solution)/shard_map/ppermute | solution.py:24

commit v11 on v10

--- a/solution.py
+++ b/solution.py
@@ -18,11 +18,25 @@
 
 def butterfly_sum(x, axes):
     size = lax.axis_size(axes)
+
+    def exchange(value, mask):
+        pairs = [(i, i ^ mask) for i in range(size)]
+        return lax.ppermute(value, axes, pairs)
+
+    bits = []
     bit = 1
     while bit < size:
-        pairs = [(i, i ^ bit) for i in range(size)]
-        x = x + lax.ppermute(x, axes, pairs)
+        bits.append(bit)
         bit *= 2
+    groups = [bits[:1]] + [bits[i:i + 2] for i in range(1, len(bits), 2)]
+    for group in groups:
+        if len(group) == 1:
+            x = x + exchange(x, group[0])
+        else:
+            near, far = group
+            own_pair = x + exchange(x, near)
+            other_pair = exchange(x, far) + exchange(x, near | far)
+            x = own_pair + other_pair
     return x
 
 

time: 222 us -> 224 us (level)
    ppermute x5 -> x7, starting transfers between devices: 6.5 us -> 8.08 us  [exchange(): return lax.ppermute(value, axes, pairs)]
    ppermute x5 -> x7, waiting for transfers between devices: 24.8 us -> 25.5 us  [exchange(): return lax.ppermute(value, axes, pairs)]
  transfers between devices with their start and end apart: 11 -> 13, of which waited for: 10 -> 11; matrix products, arithmetic and copies ran while one was open for 2% -> 2% of each run, Pallas kernels for 0% -> 0%
where the time goes in v11:
time: 224 us
  waiting for transfers between devices  153 us (68%)
  Pallas kernels  29.5 us (13%)
  other arithmetic  15.9 us (7%)
  starting transfers between devices  15.1 us (7%)
  matrix products  9.07 us (4%)
    ppermute x6, waiting for transfers between devices, swap(): return lax.ppermute(x, 'shift', [(i, i ^ bit) for i in range(size)])  128 us
    pallas_call x1, Pallas kernels, factor(): pl.pallas_call(factor_kernel, out_shape=(jax.ShapeDtypeStruct((n, n), jnp...  29.5 us
    ppermute x7, waiting for transfers between devices, exchange(): return lax.ppermute(value, axes, pairs)  25.5 us
    ppermute x7, starting transfers between devices, exchange(): return lax.ppermute(value, axes, pairs)  8.08 us
    ppermute x6, starting transfers between devices, swap(): return lax.ppermute(x, 'shift', [(i, i ^ bit) for i in range(size)])  7.05 us
    dot_general x1, matrix products, dot_high(): jnp.dot(a, b, precision=lax.Precision.HIGH, preferred_element_type=jnp.fl...  5.42 us
    add x1, other arithmetic, mix_rows(): send_second = part(2 * high + 1 - low, 1) + got_forward_y  5.34 us
    mul x1, other arithmetic, part(): return values.astype(jnp.float32) * scale  5.05 us
  transfers between devices with their start and end apart: 13, of which 11 were waited for; matrix products, arithmetic and copies ran while one was open for 2% of the time, Pallas kernels for 0%

profile of v11, /device:TPU:0, one launch (start us, length us, event | category | flops | bytes accessed | tf_op | source)
XLA Modules:
  0.0 223.7 jit_solution(1309996877000769235)
XLA Ops:
  0.7 0.0 copy-start.1
  0.7 5.0 %convert_multiply_fusion.5 = (f32[2048,256]{1,0:T(8,128)S(1)}, f32[2048,256]{1,0:T(8,128)}, f32[2048,256]{1,0:T(8,128)}, f32[2048,256]{1,0:T(8,128)}) fusion(bf16[1,16384,256]{2,1,0:T(8,128)(2,1)} %param.2, s32[]{:T(128)S(6)} %select_n.39, f32[256]{0:T(256)} %bitcast.26, s32[]{:T(128)S(6)} %select_n.42, s32[]{:T(128)S(6)} %select_n.41, s32[]{:T(128)S(6)} %select_n.38), kind=kLoop, calls=%fused_computation.19 | loop fusion | flops 4194304 | bytes 12583952 | tf_op jit(solution)/shard_map/mul | solution.py:135
  5.7 2.9 %collective-permute-start.1 = (f32[2048,256]{1,0:T(8,128)}, f32[2048,256]{1,0:T(8,128)}, u32[]{:S(2)}, u32[]{:S(2)}) collective-permute-start(f32[2048,256]{1,0:T(8,128)} %get-tuple-element.11), channel_id=1, source_target_pairs={{0,8},{8,0},{16,24},{24,16},{1,9},{9,1},{17,25},{25,17},{2,10},{10... | collective-permute-start | bytes 6291464 | tf_op jit(solution)/shard_map/ppermute | solution.py:118
  8.7 1.5 collective-permute-start.2
  10.2 0.5 collective-permute-start
  10.7 0.0 collective-permute-start.4
  10.7 44.7 %collective-permute-done.1 = f32[2048,256]{1,0:T(8,128)} collective-permute-done((f32[2048,256]{1,0:T(8,128)}, f32[2048,256]{1,0:T(8,128)}, u32[]{:S(2)}, u32[]{:S(2)}) %collective-permute-start.1) | collective-permute-done | bytes 2097184 | tf_op jit(solution)/shard_map/ppermute | solution.py:118
  55.4 2.1 collective-permute-done.2
  57.5 0.0 copy-done.1
  57.5 5.3 %fusion.9 = (f32[2048,256]{1,0:T(8,128)}, f32[2048,256]{1,0:T(8,128)}) fusion(f32[2048,256]{1,0:T(8,128)} %collective-permute-done.2, bf16[1,16384,256]{2,1,0:T(8,128)(2,1)} %param.2, s32[]{:T(128)S(6)} %select_n.43, f32[256]{0:T(256)S(1)} %bitcast.27, f32[2048,256]{1,0:T(8,128)} %collective-permute-done.1, s32[]{:T(128)S(6)} %select_n.40), kind=kLoop, calls=%fused_computation.14 | loop fusion | flops 3145728 | bytes 10486792 | tf_op jit(solution)/shard_map/add | solution.py:146
  62.9 1.5 collective-permute-start.3
  64.4 0.5 collective-permute-start.5
  64.9 35.4 %collective-permute-done = f32[2048,256]{1,0:T(8,128)} collective-permute-done((f32[2048,256]{1,0:T(8,128)}, f32[2048,256]{1,0:T(8,128)}, u32[]{:S(2)}, u32[]{:S(2)}) %collective-permute-start) | collective-permute-done | bytes 2097184 | tf_op jit(solution)/shard_map/ppermute | solution.py:118
  100.4 2.1 collective-permute-done.4
  102.5 43.5 %collective-permute-done.3 = f32[2048,256]{1,0:T(8,128)} collective-permute-done((f32[2048,256]{1,0:T(8,128)}, f32[2048,256]{1,0:T(8,128)}, u32[]{:S(2)}, u32[]{:S(2)}) %collective-permute-start.3) | collective-permute-done | bytes 2097184 | tf_op jit(solution)/shard_map/ppermute | solution.py:118
  146.0 0.0 collective-permute-done.5
  146.0 4.8 %fusion.8 = (f32[2048,256]{1,0:T(8,128)S(1)}, f32[2048,256]{1,0:T(8,128)S(1)}) fusion(f32[2048,256]{1,0:T(8,128)} %collective-permute-done.5, f32[2048,256]{1,0:T(8,128)} %collective-permute-done.4, bf16[1,16384,256]{2,1,0:T(8,128)(2,1)} %param.2, s32[]{:T(128)S(6)} %select_n.44, f32[256]{0:T(256)S(1)} %bitcast.28, f32[2048,256]{1,0:T(8,128)} %collective-permute-done.3, ...), kind=kLoop, calls=%fused_computation.12 | loop fusion | flops 4194304 | bytes 14681096 | tf_op jit(solution)/shard_map/add | solution.py:150
  150.7 0.0 copy-start
  150.7 1.8 fusion.5
  152.6 0.0 copy-done
  152.6 1.8 fusion
  154.5 0.1 collective-permute-start.6
  154.5 1.4 collective-permute-done.6
  156.0 3.7 %collective-permute-start.9 = (f32[384,128]{1,0:T(8,128)S(1)}, f32[384,128]{1,0:T(8,128)S(1)}, u32[]{:S(2)}, u32[]{:S(2)}) collective-permute-start(f32[384,128]{1,0:T(8,128)S(1)} %fusion.16), channel_id=1, source_target_pairs={{0,6},{1,7},{2,4},{3,5},{4,2},{5,3},{6,0},{7,1},{8,14},{9,15},{10,... | collective-permute-start | bytes 589832 | tf_op jit(solution)/shard_map/ppermute | solution.py:24
  159.7 0.0 collective-permute-start.8
  159.7 0.8 collective-permute-start.7
  160.4 5.3 %collective-permute-done.9 = f32[384,128]{1,0:T(8,128)S(1)} collective-permute-done((f32[384,128]{1,0:T(8,128)S(1)}, f32[384,128]{1,0:T(8,128)S(1)}, u32[]{:S(2)}, u32[]{:S(2)}) %collective-permute-start.9) | collective-permute-done | bytes 196640 | tf_op jit(solution)/shard_map/ppermute | solution.py:24
  165.7 10.9 %collective-permute-done.8 = f32[384,128]{1,0:T(8,128)S(1)} collective-permute-done((f32[384,128]{1,0:T(8,128)S(1)}, f32[384,128]{1,0:T(8,128)S(1)}, u32[]{:S(2)}, u32[]{:S(2)}) %collective-permute-start.8) | collective-permute-done | bytes 196640 | tf_op jit(solution)/shard_map/ppermute | solution.py:24
  176.7 0.0 collective-permute-done.7
  176.7 1.5 collective-permute-start.12
  178.2 0.5 collective-permute-start.11
  178.8 1.5 collective-permute-start.10
  180.3 5.3 %collective-permute-done.12 = f32[384,128]{1,0:T(8,128)S(1)} collective-permute-done((f32[384,128]{1,0:T(8,128)S(1)}, f32[384,128]{1,0:T(8,128)S(1)}, u32[]{:S(2)}, u32[]{:S(2)}) %collective-permute-start.12) | collective-permute-done | bytes 196640 | tf_op jit(solution)/shard_map/ppermute | solution.py:24
  185.6 2.4 %collective-permute-done.11 = f32[384,128]{1,0:T(8,128)S(1)} collective-permute-done((f32[384,128]{1,0:T(8,128)S(1)}, f32[384,128]{1,0:T(8,128)S(1)}, u32[]{:S(2)}, u32[]{:S(2)}) %collective-permute-start.11) | collective-permute-done | bytes 196640 | tf_op jit(solution)/shard_map/ppermute | solution.py:24
  188.0 0.1 collective-permute-done.10
  188.1 0.7 add_add_fusion.gram_ref
  188.8 29.5 %shard_map.41 = (f32[256,256]{1,0:T(8,128)}, f32[256,256]{1,0:T(8,128)}) custom-call(f32[384,128]{1,0:T(8,128)} %add_add_fusion.gram_ref), custom_call_target="tpu_custom_call" | custom-call | tf_op jit(solution)/shard_map/pallas_call | solution.py:107
  218.3 5.4 %fusion.1 = f32[4096,256]{1,0:T(8,128)} fusion(f32[256,256]{1,0:T(8,128)} %get-tuple-element.16, f32[2048,256]{1,0:T(8,128)S(1)} %get-tuple-element.18, f32[2048,256]{1,0:T(8,128)} %copy-done), kind=kOutput, calls=%fused_computation.6 | convolution fusion | flops 1611661312 | bytes 8650752 | tf_op jit(solution)/shard_map/dot_general | solution.py:16
  (4 shorter events, 0.1 us)
Async XLA Ops:
  0.7 56.9 %copy-start.1 = (f32[1,256]{1,0:T(1,128)S(1)}, f32[1,256]{1,0:T(1,128)}, u32[]{:S(2)}) copy-start(f32[1,256]{1,0:T(1,128)} %param.3) | copy-start | bytes 3076
  5.7 49.7 %collective-permute-start.1 = (f32[2048,256]{1,0:T(8,128)}, f32[2048,256]{1,0:T(8,128)}, u32[]{:S(2)}, u32[]{:S(2)}) collective-permute-start(f32[2048,256]{1,0:T(8,128)} %get-tuple-element.11), channel_id=1, source_target_pairs={{0,8},{8,0},{16,24},{24,16},{1,9},{9,1},{17,25},{25,17},{2,10},{10... | collective-permute-start | bytes 6291464 | tf_op jit(solution)/shard_map/ppermute | solution.py:118
  8.7 48.9 %collective-permute-start.2 = (f32[2048,256]{1,0:T(8,128)}, f32[2048,256]{1,0:T(8,128)}, u32[]{:S(2)}, u32[]{:S(2)}) collective-permute-start(f32[2048,256]{1,0:T(8,128)} %get-tuple-element.12), channel_id=1, source_target_pairs={{0,16},{8,24},{16,0},{24,8},{1,17},{9,25},{17,1},{25,9},{2,18},{10... | collective-permute-start | bytes 6291464 | tf_op jit(solution)/shard_map/ppermute | solution.py:118
  10.2 90.2 %collective-permute-start = (f32[2048,256]{1,0:T(8,128)}, f32[2048,256]{1,0:T(8,128)}, u32[]{:S(2)}, u32[]{:S(2)}) collective-permute-start(f32[2048,256]{1,0:T(8,128)} %get-tuple-element.10), channel_id=1, source_target_pairs={{0,8},{8,0},{16,24},{24,16},{1,9},{9,1},{17,25},{25,17},{2,10},{10... | collective-permute-start | bytes 6291464 | tf_op jit(solution)/shard_map/ppermute | solution.py:118
  10.7 91.8 %collective-permute-start.4 = (f32[2048,256]{1,0:T(8,128)S(1)}, f32[2048,256]{1,0:T(8,128)}, u32[]{:S(2)}, u32[]{:S(2)}) collective-permute-start(f32[2048,256]{1,0:T(8,128)S(1)} %get-tuple-element.14), channel_id=1, source_target_pairs={{0,16},{8,24},{16,0},{24,8},{1,17},{9,25},{17,1},{25,9},{2,18},{10... | collective-permute-start | bytes 6291464 | tf_op jit(solution)/shard_map/ppermute | solution.py:118
  62.9 83.1 %collective-permute-start.3 = (f32[2048,256]{1,0:T(8,128)}, f32[2048,256]{1,0:T(8,128)}, u32[]{:S(2)}, u32[]{:S(2)}) collective-permute-start(f32[2048,256]{1,0:T(8,128)} %get-tuple-element.13), channel_id=1, source_target_pairs={{0,16},{8,24},{16,0},{24,8},{1,17},{9,25},{17,1},{25,9},{2,18},{10... | collective-permute-start | bytes 6291464 | tf_op jit(solution)/shard_map/ppermute | solution.py:118
  64.4 81.6 %collective-permute-start.5 = (f32[2048,256]{1,0:T(8,128)}, f32[2048,256]{1,0:T(8,128)}, u32[]{:S(2)}, u32[]{:S(2)}) collective-permute-start(f32[2048,256]{1,0:T(8,128)} %get-tuple-element.15), channel_id=1, source_target_pairs={{0,8},{8,0},{16,24},{24,16},{1,9},{9,1},{17,25},{25,17},{2,10},{10... | collective-permute-start | bytes 6291464 | tf_op jit(solution)/shard_map/ppermute | solution.py:118
  150.7 1.8 copy-start
  154.5 1.5 collective-permute-start.6
  156.0 9.8 %collective-permute-start.9 = (f32[384,128]{1,0:T(8,128)S(1)}, f32[384,128]{1,0:T(8,128)S(1)}, u32[]{:S(2)}, u32[]{:S(2)}) collective-permute-start(f32[384,128]{1,0:T(8,128)S(1)} %fusion.16), channel_id=1, source_target_pairs={{0,6},{1,7},{2,4},{3,5},{4,2},{5,3},{6,0},{7,1},{8,14},{9,15},{10,... | collective-permute-start | bytes 589832 | tf_op jit(solution)/shard_map/ppermute | solution.py:24
  159.7 17.0 %collective-permute-start.8 = (f32[384,128]{1,0:T(8,128)S(1)}, f32[384,128]{1,0:T(8,128)S(1)}, u32[]{:S(2)}, u32[]{:S(2)}) collective-permute-start(f32[384,128]{1,0:T(8,128)S(1)} %fusion.16), channel_id=1, source_target_pairs={{0,4},{1,5},{2,6},{3,7},{4,0},{5,1},{6,2},{7,3},{8,12},{9,13},{10,... | collective-permute-start | bytes 589832 | tf_op jit(solution)/shard_map/ppermute | solution.py:24
  159.7 17.0 %collective-permute-start.7 = (f32[384,128]{1,0:T(8,128)S(1)}, f32[384,128]{1,0:T(8,128)S(1)}, u32[]{:S(2)}, u32[]{:S(2)}) collective-permute-start(f32[384,128]{1,0:T(8,128)S(1)} %fusion.16), channel_id=1, source_target_pairs={{0,2},{1,3},{2,0},{3,1},{4,6},{5,7},{6,4},{7,5},{8,10},{9,11},{10,... | collective-permute-start | bytes 589832 | tf_op jit(solution)/shard_map/ppermute | solution.py:24
  176.7 8.8 %collective-permute-start.12 = (f32[384,128]{1,0:T(8,128)S(1)}, f32[384,128]{1,0:T(8,128)S(1)}, u32[]{:S(2)}, u32[]{:S(2)}) collective-permute-start(f32[384,128]{1,0:T(8,128)S(1)} %add_add_fusion.1), channel_id=1, source_target_pairs={{0,24},{1,25},{2,26},{3,27},{4,28},{5,29},{6,30},{7,31},{8,16},{9,... | collective-permute-start | bytes 589832 | tf_op jit(solution)/shard_map/ppermute | solution.py:24
  178.2 9.7 %collective-permute-start.11 = (f32[384,128]{1,0:T(8,128)S(1)}, f32[384,128]{1,0:T(8,128)S(1)}, u32[]{:S(2)}, u32[]{:S(2)}) collective-permute-start(f32[384,128]{1,0:T(8,128)S(1)} %add_add_fusion.1), channel_id=1, source_target_pairs={{0,16},{1,17},{2,18},{3,19},{4,20},{5,21},{6,22},{7,23},{8,24},{9,... | collective-permute-start | bytes 589832 | tf_op jit(solution)/shard_map/ppermute | solution.py:24
  178.8 9.3 %collective-permute-start.10 = (f32[384,128]{1,0:T(8,128)S(1)}, f32[384,128]{1,0:T(8,128)S(1)}, u32[]{:S(2)}, u32[]{:S(2)}) collective-permute-start(f32[384,128]{1,0:T(8,128)S(1)} %add_add_fusion.1), channel_id=1, source_target_pairs={{0,8},{1,9},{2,10},{3,11},{4,12},{5,13},{6,14},{7,15},{8,0},{9,1},... | collective-permute-start | bytes 589832 | tf_op jit(solution)/shard_map/ppermute | solution.py:24

commit v12 on v10

--- a/solution.py
+++ b/solution.py
@@ -130,25 +130,38 @@
     got_stay_x, got_stay_y = swap(stay_x, 1), swap(stay_y, 2)
     send_first = part(2 * (1 - high) + low, 0) + got_forward_x
     send_second = part(2 * high + 1 - low, 1) + got_forward_y
+    quarter = piece // 2
     send_first, send_second = lax.optimization_barrier((send_first, send_second))
-    got_first, got_second = swap(send_first, 2), swap(send_second, 1)
-    first = part(2 * high + low, 0) + got_stay_x + got_first
-    second = part(2 * high + low, 1) + got_stay_y + got_second
-    return jnp.concatenate([first, second], axis=0)
+    got_pieces = []
+    for k in range(2):
+        rows_k = slice(k * quarter, (k + 1) * quarter)
+        got_pieces.append((swap(send_first[rows_k], 2), swap(send_second[rows_k], 1)))
+    own_first, own_second = part(2 * high + low, 0), part(2 * high + low, 1)
+    pieces = []
+    for k in range(2):
+        rows_k = slice(k * quarter, (k + 1) * quarter)
+        pieces.append((own_first[rows_k] + got_stay_x[rows_k] + got_pieces[k][0],
+                       own_second[rows_k] + got_stay_y[rows_k] + got_pieces[k][1]))
+    return [pieces[0][0], pieces[1][0], pieces[0][1], pieces[1][1]]
 
 
 def shards(filtered, weights):
     if lax.axis_size("shift") == 4:
-        mixed = mix_rows(filtered, weights)
+        row_pieces = mix_rows(filtered, weights)
     else:
         weighted = filtered[0].astype(jnp.float32) * weights[0][None, :]
-        mixed = lax.psum_scatter(weighted, "shift", scatter_dimension=0, tiled=True)
+        row_pieces = [lax.psum_scatter(weighted, "shift", scatter_dimension=0, tiled=True)]
+    mixed = jnp.concatenate(row_pieces, axis=0)
     devices_all = lax.axis_size(("shift", "rows"))
     total_rows = mixed.shape[0] * devices_all
     half = mixed.shape[1] // 2
-    top = cross_products(mixed[:, :half], mixed)
-    bottom = cross_products(mixed[:, half:], mixed[:, half:])
-    blocks = jnp.concatenate([top[:, :half], top[:, half:], bottom], axis=0) / total_rows
+    blocks = None
+    for rows_k in row_pieces:
+        top = cross_products(rows_k[:, :half], rows_k)
+        bottom = cross_products(rows_k[:, half:], rows_k[:, half:])
+        part_blocks = jnp.concatenate([top[:, :half], top[:, half:], bottom], axis=0)
+        blocks = part_blocks if blocks is None else blocks + part_blocks
+    blocks = blocks / total_rows
     upper, upper_inv = factor(butterfly_sum(blocks, ("shift", "rows")))
     basis = dot_high(mixed, upper_inv)
     return (basis, upper)

time: 222 us -> 222 us (level)
  starting transfers between devices: 13.6 us -> 18.8 us
  waiting for transfers between devices: 153 us -> 150 us
  other arithmetic: 15.9 us -> 13.4 us
    ppermute x6 -> x8, starting transfers between devices: 7.05 us -> 12.2 us  [swap(): return lax.ppermute(x, 'shift', [(i, i ^ bit) for i in range(size)])]
    ppermute x6 -> x8, waiting for transfers between devices: 128 us -> 125 us  [swap(): return lax.ppermute(x, 'shift', [(i, i ^ bit) for i in range(size)])]
    add x1 -> x2, other arithmetic: 4.75 us -> 2.36 us  [the longest x1 1.95 us: mix_rows(): own_first[rows_k] + got_stay_x[rows_k] + got_pieces[k][0]]
    dot_general x2 -> x8, matrix products: 3.65 us -> 4.7 us  [cross_products(): jnp.dot(left.T, right, precision=lax.Precision.HIGH, preferred_element_ty...]
  transfers between devices with their start and end apart: 11 -> 13, of which waited for: 10 -> 10; matrix products, arithmetic and copies ran while one was open for 2% -> 4% of each run, Pallas kernels for 0% -> 0%
where the time goes in v12:
time: 222 us
  waiting for transfers between devices  150 us (68%)
  Pallas kernels  29.5 us (13%)
  starting transfers between devices  18.8 us (8%)
  other arithmetic  13.4 us (6%)
  matrix products  9.79 us (4%)
    ppermute x8, waiting for transfers between devices, swap(): return lax.ppermute(x, 'shift', [(i, i ^ bit) for i in range(size)])  125 us
    pallas_call x1, Pallas kernels, factor(): pl.pallas_call(factor_kernel, out_shape=(jax.ShapeDtypeStruct((n, n), jnp...  29.5 us
    ppermute x5, waiting for transfers between devices, butterfly_sum(): x = x + lax.ppermute(x, axes, pairs)  24.7 us
    ppermute x8, starting transfers between devices, swap(): return lax.ppermute(x, 'shift', [(i, i ^ bit) for i in range(size)])  12.2 us
    mul x1, other arithmetic, part(): return values.astype(jnp.float32) * scale  6.9 us
    ppermute x5, starting transfers between devices, butterfly_sum(): x = x + lax.ppermute(x, axes, pairs)  6.64 us
    dot_general x1, matrix products, dot_high(): jnp.dot(a, b, precision=lax.Precision.HIGH, preferred_element_type=jnp.fl...  5.09 us
    dot_general x8, matrix products, cross_products(): jnp.dot(left.T, right, precision=lax.Precision.HIGH, preferred_element_ty...  4.7 us
  transfers between devices with their start and end apart: 13, of which 10 were waited for; matrix products, arithmetic and copies ran while one was open for 4% of the time, Pallas kernels for 0%

profile of v12, /device:TPU:0, one launch (start us, length us, event | category | flops | bytes accessed | tf_op | source)
XLA Modules:
  0.0 222.3 jit_solution(6433337681652049729)
XLA Ops:
  0.7 0.0 copy-start.3
  0.7 6.9 %convert_multiply_fusion = (f32[2048,256]{1,0:T(8,128)}, f32[2048,256]{1,0:T(8,128)}, f32[2048,256]{1,0:T(8,128)}, f32[2048,256]{1,0:T(8,128)}, f32[2048,256]{1,0:T(8,128)S(1)}, /*index=5*/f32[2048,256]{1,0:T(8,128)}) fusion(bf16[1,16384,256]{2,1,0:T(8,128)(2,1)} %param.2, s32[]{:T(128)S(6)} %select_n.44, f32[256]{0:T(256)} %bitcast.30, s32[]{:T(128)S(6)} %select_n.42, ...), kind=kLoop, calls=%fused_computation.8 | loop fusion | flops 6291456 | bytes 18875416 | tf_op jit(solution)/shard_map/mul | solution.py:121
  7.6 2.9 %collective-permute-start.1 = (f32[2048,256]{1,0:T(8,128)}, f32[2048,256]{1,0:T(8,128)}, u32[]{:S(2)}, u32[]{:S(2)}) collective-permute-start(f32[2048,256]{1,0:T(8,128)} %get-tuple-element.11), channel_id=1, source_target_pairs={{0,8},{8,0},{16,24},{24,16},{1,9},{9,1},{17,25},{25,17},{2,10},{10... | collective-permute-start | bytes 6291464 | tf_op jit(solution)/shard_map/ppermute | solution.py:104
  10.5 1.5 collective-permute-start.2
  12.1 0.5 collective-permute-start
  12.6 44.7 %collective-permute-done.1 = f32[2048,256]{1,0:T(8,128)} collective-permute-done((f32[2048,256]{1,0:T(8,128)}, f32[2048,256]{1,0:T(8,128)}, u32[]{:S(2)}, u32[]{:S(2)}) %collective-permute-start.1) | collective-permute-done | bytes 2097184 | tf_op jit(solution)/shard_map/ppermute | solution.py:104
  57.3 0.6 collective-permute-done.2
  57.9 0.0 copy-done.3
  57.9 3.3 %fusion.8 = (f32[2048,256]{1,0:T(8,128)S(1)}, f32[2048,256]{1,0:T(8,128)S(1)}) fusion(f32[2048,256]{1,0:T(8,128)} %collective-permute-done.2, bf16[1,16384,256]{2,1,0:T(8,128)(2,1)} %param.2, s32[]{:T(128)S(6)} %select_n.43, f32[256]{0:T(256)S(1)} %bitcast.31, f32[2048,256]{1,0:T(8,128)} %collective-permute-done.1, s32[]{:T(128)S(6)} %select_n.40), kind=kLoop, calls=%fused_computation.10 | loop fusion | flops 3145728 | bytes 10486792 | tf_op jit(solution)/shard_map/add | solution.py:132
  61.2 0.1 fusion.35
  61.4 1.6 collective-permute-start.4
  63.0 0.0 copy-start.2
  63.0 0.5 collective-permute-start.3
  63.5 1.5 collective-permute-start.5
  65.0 0.1 fusion.34
  65.1 1.5 collective-permute-start.7
  66.6 35.6 %collective-permute-done = f32[2048,256]{1,0:T(8,128)} collective-permute-done((f32[2048,256]{1,0:T(8,128)S(1)}, f32[2048,256]{1,0:T(8,128)}, u32[]{:S(2)}, u32[]{:S(2)}) %collective-permute-start) | collective-permute-done | bytes 2097184 | tf_op jit(solution)/shard_map/ppermute | solution.py:104
  102.3 2.1 collective-permute-start.6
  104.3 0.0 collective-permute-done.4
  104.3 5.7 %collective-permute-done.3 = f32[1024,256]{1,0:T(8,128)S(1)} collective-permute-done((f32[1024,256]{1,0:T(8,128)S(1)}, f32[1024,256]{1,0:T(8,128)S(1)}, u32[]{:S(2)}, u32[]{:S(2)}) %collective-permute-start.3) | collective-permute-done | bytes 1048608 | tf_op jit(solution)/shard_map/ppermute | solution.py:104
  110.0 0.0 copy-done.2
  110.0 1.9 fusion.12
  112.0 0.6 fusion.22
  112.6 0.0 copy-start.1
  112.6 0.6 fusion.26
  113.2 0.6 fusion.24
  113.8 0.6 fusion.28
  114.4 38.2 %collective-permute-done.5 = f32[2048,256]{1,0:T(8,128)S(1)} collective-permute-done((f32[2048,256]{1,0:T(8,128)}, f32[2048,256]{1,0:T(8,128)S(1)}, u32[]{:S(2)}, u32[]{:S(2)}) %collective-permute-start.5) | collective-permute-done | bytes 2097184 | tf_op jit(solution)/shard_map/ppermute | solution.py:104
  152.6 0.0 collective-permute-done.7
  152.6 0.0 collective-permute-done.6
  152.6 0.0 copy-done.1
  152.6 0.4 fusion.10
  153.0 0.0 copy-start
  153.0 0.6 fusion.14
  153.6 0.6 fusion.16
  154.2 0.6 fusion.18
  154.8 0.6 fusion.20
  155.4 0.0 copy-done
  155.5 0.1 collective-permute-start.8
  155.6 1.4 collective-permute-done.8
  157.0 1.6 collective-permute-start.9
  158.7 5.4 %collective-permute-done.9 = f32[384,128]{1,0:T(8,128)S(1)} collective-permute-done((f32[384,128]{1,0:T(8,128)S(1)}, f32[384,128]{1,0:T(8,128)S(1)}, u32[]{:S(2)}, u32[]{:S(2)}) %collective-permute-start.9) | collective-permute-done | bytes 196640 | tf_op jit(solution)/shard_map/ppermute | solution.py:24
  164.1 2.7 %collective-permute-start.10 = (f32[384,128]{1,0:T(8,128)S(1)}, f32[384,128]{1,0:T(8,128)S(1)}, u32[]{:S(2)}, u32[]{:S(2)}) collective-permute-start(f32[384,128]{1,0:T(8,128)S(1)} %add.150), channel_id=1, source_target_pairs={{0,4},{1,5},{2,6},{3,7},{4,0},{5,1},{6,2},{7,3},{8,12},{9,13},{10,... | collective-permute-start | bytes 589832 | tf_op jit(solution)/shard_map/ppermute | solution.py:24
  166.7 8.6 %collective-permute-done.10 = f32[384,128]{1,0:T(8,128)S(1)} collective-permute-done((f32[384,128]{1,0:T(8,128)S(1)}, f32[384,128]{1,0:T(8,128)S(1)}, u32[]{:S(2)}, u32[]{:S(2)}) %collective-permute-start.10) | collective-permute-done | bytes 196640 | tf_op jit(solution)/shard_map/ppermute | solution.py:24
  175.4 0.7 collective-permute-start.11
  176.1 5.1 %collective-permute-done.11 = f32[384,128]{1,0:T(8,128)S(1)} collective-permute-done((f32[384,128]{1,0:T(8,128)S(1)}, f32[384,128]{1,0:T(8,128)S(1)}, u32[]{:S(2)}, u32[]{:S(2)}) %collective-permute-start.11) | collective-permute-done | bytes 196640 | tf_op jit(solution)/shard_map/ppermute | solution.py:24
  181.2 1.6 collective-permute-start.12
  182.8 4.2 %collective-permute-done.12 = f32[384,128]{1,0:T(8,128)S(1)} collective-permute-done((f32[384,128]{1,0:T(8,128)S(1)}, f32[384,128]{1,0:T(8,128)S(1)}, u32[]{:S(2)}, u32[]{:S(2)}) %collective-permute-start.12) | collective-permute-done | bytes 196640 | tf_op jit(solution)/shard_map/ppermute | solution.py:24
  187.0 0.7 add.153.gram_ref
  187.7 29.5 %shard_map.41 = (f32[256,256]{1,0:T(8,128)}, f32[256,256]{1,0:T(8,128)}) custom-call(f32[384,128]{1,0:T(8,128)} %add.153.gram_ref), custom_call_target="tpu_custom_call" | custom-call | tf_op jit(solution)/shard_map/pallas_call | solution.py:93
  217.2 5.1 %fusion = f32[4096,256]{1,0:T(8,128)} fusion(f32[256,256]{1,0:T(8,128)} %get-tuple-element.16, f32[1024,256]{1,0:T(8,128)S(1)} %get-tuple-element.26, f32[1024,256]{1,0:T(8,128)} %copy-done, f32[1024,256]{1,0:T(8,128)S(1)} %get-tuple-element.28, f32[1024,256]{1,0:T(8,128)S(1)} %get-tuple-element.29), kind=kOutput, calls=%fused_computation | convolution fusion | flops 1613758464 | bytes 8650752 | tf_op jit(solution)/shard_map/dot_general | solution.py:16
  (7 shorter events, 0.2 us)
Async XLA Ops:
  0.7 57.3 %copy-start.3 = (f32[1,256]{1,0:T(1,128)S(1)}, f32[1,256]{1,0:T(1,128)}, u32[]{:S(2)}) copy-start(f32[1,256]{1,0:T(1,128)} %param.3) | copy-start | bytes 3076
  7.6 49.7 %collective-permute-start.1 = (f32[2048,256]{1,0:T(8,128)}, f32[2048,256]{1,0:T(8,128)}, u32[]{:S(2)}, u32[]{:S(2)}) collective-permute-start(f32[2048,256]{1,0:T(8,128)} %get-tuple-element.11), channel_id=1, source_target_pairs={{0,8},{8,0},{16,24},{24,16},{1,9},{9,1},{17,25},{25,17},{2,10},{10... | collective-permute-start | bytes 6291464 | tf_op jit(solution)/shard_map/ppermute | solution.py:104
  10.5 47.4 %collective-permute-start.2 = (f32[2048,256]{1,0:T(8,128)}, f32[2048,256]{1,0:T(8,128)}, u32[]{:S(2)}, u32[]{:S(2)}) collective-permute-start(f32[2048,256]{1,0:T(8,128)} %get-tuple-element.12), channel_id=1, source_target_pairs={{0,16},{8,24},{16,0},{24,8},{1,17},{9,25},{17,1},{25,9},{2,18},{10... | collective-permute-start | bytes 6291464 | tf_op jit(solution)/shard_map/ppermute | solution.py:104
  12.1 90.2 %collective-permute-start = (f32[2048,256]{1,0:T(8,128)S(1)}, f32[2048,256]{1,0:T(8,128)}, u32[]{:S(2)}, u32[]{:S(2)}) collective-permute-start(f32[2048,256]{1,0:T(8,128)S(1)} %get-tuple-element.10), channel_id=1, source_target_pairs={{0,8},{8,0},{16,24},{24,16},{1,9},{9,1},{17,25},{25,17},{2,10},{10... | collective-permute-start | bytes 6291464 | tf_op jit(solution)/shard_map/ppermute | solution.py:104
  61.4 42.9 %collective-permute-start.4 = (f32[1024,256]{1,0:T(8,128)S(1)}, f32[1024,256]{1,0:T(8,128)S(1)}, u32[]{:S(2)}, u32[]{:S(2)}) collective-permute-start(f32[1024,256]{1,0:T(8,128)S(1)} %get-tuple-element.32), channel_id=1, source_target_pairs={{0,16},{8,24},{16,0},{24,8},{1,17},{9,25},{17,1},{25,9},{2,18},{10... | collective-permute-start | bytes 3145736 | tf_op jit(solution)/shard_map/ppermute | solution.py:104
  63.0 47.0 %copy-start.2 = (f32[2048,256]{1,0:T(8,128)S(1)}, f32[2048,256]{1,0:T(8,128)}, u32[]{:S(2)}) copy-start(f32[2048,256]{1,0:T(8,128)} %get-tuple-element.23) | copy-start | bytes 6291460
  63.0 47.0 %collective-permute-start.3 = (f32[1024,256]{1,0:T(8,128)S(1)}, f32[1024,256]{1,0:T(8,128)S(1)}, u32[]{:S(2)}, u32[]{:S(2)}) collective-permute-start(f32[1024,256]{1,0:T(8,128)S(1)} %get-tuple-element.33), channel_id=1, source_target_pairs={{0,16},{8,24},{16,0},{24,8},{1,17},{9,25},{17,1},{25,9},{2,18},{10... | collective-permute-start | bytes 3145736 | tf_op jit(solution)/shard_map/ppermute | solution.py:104
  63.5 89.1 %collective-permute-start.5 = (f32[2048,256]{1,0:T(8,128)}, f32[2048,256]{1,0:T(8,128)S(1)}, u32[]{:S(2)}, u32[]{:S(2)}) collective-permute-start(f32[2048,256]{1,0:T(8,128)} %get-tuple-element.14), channel_id=1, source_target_pairs={{0,16},{8,24},{16,0},{24,8},{1,17},{9,25},{17,1},{25,9},{2,18},{10... | collective-permute-start | bytes 6291464 | tf_op jit(solution)/shard_map/ppermute | solution.py:104
  65.1 87.4 %collective-permute-start.7 = (f32[1024,256]{1,0:T(8,128)S(1)}, f32[1024,256]{1,0:T(8,128)S(1)}, u32[]{:S(2)}, u32[]{:S(2)}) collective-permute-start(f32[1024,256]{1,0:T(8,128)S(1)} %get-tuple-element.30), channel_id=1, source_target_pairs={{0,8},{8,0},{16,24},{24,16},{1,9},{9,1},{17,25},{25,17},{2,10},{10... | collective-permute-start | bytes 3145736 | tf_op jit(solution)/shard_map/ppermute | solution.py:104
  102.3 50.3 %collective-permute-start.6 = (f32[1024,256]{1,0:T(8,128)S(1)}, f32[1024,256]{1,0:T(8,128)S(1)}, u32[]{:S(2)}, u32[]{:S(2)}) collective-permute-start(f32[1024,256]{1,0:T(8,128)S(1)} %get-tuple-element.31), channel_id=1, source_target_pairs={{0,8},{8,0},{16,24},{24,16},{1,9},{9,1},{17,25},{25,17},{2,10},{10... | collective-permute-start | bytes 3145736 | tf_op jit(solution)/shard_map/ppermute | solution.py:104
  112.6 40.0 %copy-start.1 = (f32[2048,256]{1,0:T(8,128)S(1)}, f32[2048,256]{1,0:T(8,128)}, u32[]{:S(2)}) copy-start(f32[2048,256]{1,0:T(8,128)} %get-tuple-element.18) | copy-start | bytes 6291460
  153.0 2.4 %copy-start = (f32[1024,256]{1,0:T(8,128)}, f32[1024,256]{1,0:T(8,128)S(1)}, u32[]{:S(2)}) copy-start(f32[1024,256]{1,0:T(8,128)S(1)} %get-tuple-element.27) | copy-start | bytes 3145732
  155.5 1.5 collective-permute-start.8
  157.0 7.0 %collective-permute-start.9 = (f32[384,128]{1,0:T(8,128)S(1)}, f32[384,128]{1,0:T(8,128)S(1)}, u32[]{:S(2)}, u32[]{:S(2)}) collective-permute-start(f32[384,128]{1,0:T(8,128)S(1)} %add.149), channel_id=1, source_target_pairs={{0,2},{1,3},{2,0},{3,1},{4,6},{5,7},{6,4},{7,5},{8,10},{9,11},{10,... | collective-permute-start | bytes 589832 | tf_op jit(solution)/shard_map/ppermute | solution.py:24
  164.1 11.3 %collective-permute-start.10 = (f32[384,128]{1,0:T(8,128)S(1)}, f32[384,128]{1,0:T(8,128)S(1)}, u32[]{:S(2)}, u32[]{:S(2)}) collective-permute-start(f32[384,128]{1,0:T(8,128)S(1)} %add.150), channel_id=1, source_target_pairs={{0,4},{1,5},{2,6},{3,7},{4,0},{5,1},{6,2},{7,3},{8,12},{9,13},{10,... | collective-permute-start | bytes 589832 | tf_op jit(solution)/shard_map/ppermute | solution.py:24
  175.4 5.8 %collective-permute-start.11 = (f32[384,128]{1,0:T(8,128)S(1)}, f32[384,128]{1,0:T(8,128)S(1)}, u32[]{:S(2)}, u32[]{:S(2)}) collective-permute-start(f32[384,128]{1,0:T(8,128)S(1)} %add.151), channel_id=1, source_target_pairs={{0,8},{1,9},{2,10},{3,11},{4,12},{5,13},{6,14},{7,15},{8,0},{9,1},... | collective-permute-start | bytes 589832 | tf_op jit(solution)/shard_map/ppermute | solution.py:24
  181.2 5.7 %collective-permute-start.12 = (f32[384,128]{1,0:T(8,128)S(1)}, f32[384,128]{1,0:T(8,128)S(1)}, u32[]{:S(2)}, u32[]{:S(2)}) collective-permute-start(f32[384,128]{1,0:T(8,128)S(1)} %add.152), channel_id=1, source_target_pairs={{0,16},{1,17},{2,18},{3,19},{4,20},{5,21},{6,22},{7,23},{8,24},{9,... | collective-permute-start | bytes 589832 | tf_op jit(solution)/shard_map/ppermute | solution.py:24

commit v13 on v10

--- a/solution.py
+++ b/solution.py
@@ -9,7 +9,7 @@
 
 
 def cross_products(left, right):
-    return jnp.dot(left.T, right, precision=lax.Precision.HIGH, preferred_element_type=jnp.float32)
+    return jnp.dot(left.T, right, precision=lax.Precision.DEFAULT, preferred_element_type=jnp.float32)
 
 
 def dot_high(a, b):

time: 222 us -> 220 us (level)
  matrix products: 9.07 us -> 6.36 us
    dot_general x2, matrix products: 3.65 us -> 0.95 us  [cross_products(): jnp.dot(left.T, right, precision=lax.Precision.DEFAULT, preferred_element...]
where the time goes in v13:
time: 220 us
  waiting for transfers between devices  153 us (70%)
  Pallas kernels  29.4 us (13%)
  other arithmetic  15.9 us (7%)
  starting transfers between devices  13.6 us (6%)
  matrix products  6.36 us (3%)
    ppermute x6, waiting for transfers between devices, swap(): return lax.ppermute(x, 'shift', [(i, i ^ bit) for i in range(size)])  128 us
    pallas_call x1, Pallas kernels, factor(): pl.pallas_call(factor_kernel, out_shape=(jax.ShapeDtypeStruct((n, n), jnp...  29.4 us
    ppermute x5, waiting for transfers between devices, butterfly_sum(): x = x + lax.ppermute(x, axes, pairs)  24.8 us
    ppermute x6, starting transfers between devices, swap(): return lax.ppermute(x, 'shift', [(i, i ^ bit) for i in range(size)])  7.05 us
    ppermute x5, starting transfers between devices, butterfly_sum(): x = x + lax.ppermute(x, axes, pairs)  6.51 us
    dot_general x1, matrix products, dot_high(): jnp.dot(a, b, precision=lax.Precision.HIGH, preferred_element_type=jnp.fl...  5.41 us
    add x1, other arithmetic, mix_rows(): send_second = part(2 * high + 1 - low, 1) + got_forward_y  5.34 us
    mul x1, other arithmetic, part(): return values.astype(jnp.float32) * scale  5.05 us
  transfers between devices with their start and end apart: 11, of which 10 were waited for; matrix products, arithmetic and copies ran while one was open for 2% of the time, Pallas kernels for 0%

profile of v13, /device:TPU:0, one launch (start us, length us, event | category | flops | bytes accessed | tf_op | source)
XLA Modules:
  0.0 219.5 jit_solution(10463744484844552378)
XLA Ops:
  0.7 0.0 copy-start.1
  0.7 5.0 %convert_multiply_fusion.5 = (f32[2048,256]{1,0:T(8,128)S(1)}, f32[2048,256]{1,0:T(8,128)}, f32[2048,256]{1,0:T(8,128)}, f32[2048,256]{1,0:T(8,128)}) fusion(bf16[1,16384,256]{2,1,0:T(8,128)(2,1)} %param.2, s32[]{:T(128)S(6)} %select_n.39, f32[256]{0:T(256)} %bitcast.26, s32[]{:T(128)S(6)} %select_n.42, s32[]{:T(128)S(6)} %select_n.41, s32[]{:T(128)S(6)} %select_n.38), kind=kLoop, calls=%fused_computation.19 | loop fusion | flops 4194304 | bytes 12583952 | tf_op jit(solution)/shard_map/mul | solution.py:121
  5.7 2.9 %collective-permute-start.1 = (f32[2048,256]{1,0:T(8,128)}, f32[2048,256]{1,0:T(8,128)}, u32[]{:S(2)}, u32[]{:S(2)}) collective-permute-start(f32[2048,256]{1,0:T(8,128)} %get-tuple-element.11), channel_id=1, source_target_pairs={{0,8},{8,0},{16,24},{24,16},{1,9},{9,1},{17,25},{25,17},{2,10},{10... | collective-permute-start | bytes 6291464 | tf_op jit(solution)/shard_map/ppermute | solution.py:104
  8.7 1.5 collective-permute-start.2
  10.2 0.5 collective-permute-start
  10.7 0.0 collective-permute-start.4
  10.7 44.7 %collective-permute-done.1 = f32[2048,256]{1,0:T(8,128)} collective-permute-done((f32[2048,256]{1,0:T(8,128)}, f32[2048,256]{1,0:T(8,128)}, u32[]{:S(2)}, u32[]{:S(2)}) %collective-permute-start.1) | collective-permute-done | bytes 2097184 | tf_op jit(solution)/shard_map/ppermute | solution.py:104
  55.4 2.1 collective-permute-done.2
  57.5 0.0 copy-done.1
  57.5 5.3 %fusion.9 = (f32[2048,256]{1,0:T(8,128)}, f32[2048,256]{1,0:T(8,128)}) fusion(f32[2048,256]{1,0:T(8,128)} %collective-permute-done.2, bf16[1,16384,256]{2,1,0:T(8,128)(2,1)} %param.2, s32[]{:T(128)S(6)} %select_n.43, f32[256]{0:T(256)S(1)} %bitcast.27, f32[2048,256]{1,0:T(8,128)} %collective-permute-done.1, s32[]{:T(128)S(6)} %select_n.40), kind=kLoop, calls=%fused_computation.14 | loop fusion | flops 3145728 | bytes 10486792 | tf_op jit(solution)/shard_map/add | solution.py:132
  62.9 1.5 collective-permute-start.3
  64.4 0.5 collective-permute-start.5
  64.9 35.4 %collective-permute-done = f32[2048,256]{1,0:T(8,128)} collective-permute-done((f32[2048,256]{1,0:T(8,128)}, f32[2048,256]{1,0:T(8,128)}, u32[]{:S(2)}, u32[]{:S(2)}) %collective-permute-start) | collective-permute-done | bytes 2097184 | tf_op jit(solution)/shard_map/ppermute | solution.py:104
  100.4 2.1 collective-permute-done.4
  102.5 43.5 %collective-permute-done.3 = f32[2048,256]{1,0:T(8,128)} collective-permute-done((f32[2048,256]{1,0:T(8,128)}, f32[2048,256]{1,0:T(8,128)}, u32[]{:S(2)}, u32[]{:S(2)}) %collective-permute-start.3) | collective-permute-done | bytes 2097184 | tf_op jit(solution)/shard_map/ppermute | solution.py:104
  146.0 0.0 collective-permute-done.5
  146.0 4.7 %fusion.8 = (f32[2048,256]{1,0:T(8,128)S(1)}, f32[2048,256]{1,0:T(8,128)S(1)}) fusion(f32[2048,256]{1,0:T(8,128)} %collective-permute-done.5, f32[2048,256]{1,0:T(8,128)} %collective-permute-done.4, bf16[1,16384,256]{2,1,0:T(8,128)(2,1)} %param.2, s32[]{:T(128)S(6)} %select_n.44, f32[256]{0:T(256)S(1)} %bitcast.28, f32[2048,256]{1,0:T(8,128)} %collective-permute-done.3, ...), kind=kLoop, calls=%fused_computation.12 | loop fusion | flops 4194304 | bytes 14681096 | tf_op jit(solution)/shard_map/add | solution.py:136
  150.7 0.0 copy-start
  150.7 0.5 fusion.5
  151.2 0.9 copy-done
  152.1 0.5 fusion
  152.6 0.1 collective-permute-start.6
  152.7 1.4 collective-permute-done.6
  154.1 1.6 collective-permute-start.7
  155.8 5.4 %collective-permute-done.7 = f32[384,128]{1,0:T(8,128)S(1)} collective-permute-done((f32[384,128]{1,0:T(8,128)S(1)}, f32[384,128]{1,0:T(8,128)S(1)}, u32[]{:S(2)}, u32[]{:S(2)}) %collective-permute-start.7) | collective-permute-done | bytes 196640 | tf_op jit(solution)/shard_map/ppermute | solution.py:24
  161.2 2.7 %collective-permute-start.8 = (f32[384,128]{1,0:T(8,128)S(1)}, f32[384,128]{1,0:T(8,128)S(1)}, u32[]{:S(2)}, u32[]{:S(2)}) collective-permute-start(f32[384,128]{1,0:T(8,128)S(1)} %add.122), channel_id=1, source_target_pairs={{0,4},{1,5},{2,6},{3,7},{4,0},{5,1},{6,2},{7,3},{8,12},{9,13},{10,... | collective-permute-start | bytes 589832 | tf_op jit(solution)/shard_map/ppermute | solution.py:24
  163.8 8.6 %collective-permute-done.8 = f32[384,128]{1,0:T(8,128)S(1)} collective-permute-done((f32[384,128]{1,0:T(8,128)S(1)}, f32[384,128]{1,0:T(8,128)S(1)}, u32[]{:S(2)}, u32[]{:S(2)}) %collective-permute-start.8) | collective-permute-done | bytes 196640 | tf_op jit(solution)/shard_map/ppermute | solution.py:24
  172.5 0.5 collective-permute-start.9
  173.0 5.3 %collective-permute-done.9 = f32[384,128]{1,0:T(8,128)S(1)} collective-permute-done((f32[384,128]{1,0:T(8,128)S(1)}, f32[384,128]{1,0:T(8,128)S(1)}, u32[]{:S(2)}, u32[]{:S(2)}) %collective-permute-start.9) | collective-permute-done | bytes 196640 | tf_op jit(solution)/shard_map/ppermute | solution.py:24
  178.3 1.6 collective-permute-start.10
  179.9 4.1 %collective-permute-done.10 = f32[384,128]{1,0:T(8,128)S(1)} collective-permute-done((f32[384,128]{1,0:T(8,128)S(1)}, f32[384,128]{1,0:T(8,128)S(1)}, u32[]{:S(2)}, u32[]{:S(2)}) %collective-permute-start.10) | collective-permute-done | bytes 196640 | tf_op jit(solution)/shard_map/ppermute | solution.py:24
  184.0 0.7 add.125.gram_ref
  184.7 29.4 %shard_map.41 = (f32[256,256]{1,0:T(8,128)}, f32[256,256]{1,0:T(8,128)}) custom-call(f32[384,128]{1,0:T(8,128)} %add.125.gram_ref), custom_call_target="tpu_custom_call" | custom-call | tf_op jit(solution)/shard_map/pallas_call | solution.py:93
  214.1 5.4 %fusion.1 = f32[4096,256]{1,0:T(8,128)} fusion(f32[256,256]{1,0:T(8,128)} %get-tuple-element.16, f32[2048,256]{1,0:T(8,128)S(1)} %get-tuple-element.18, f32[2048,256]{1,0:T(8,128)} %copy-done), kind=kOutput, calls=%fused_computation.6 | convolution fusion | flops 1611661312 | bytes 8650752 | tf_op jit(solution)/shard_map/dot_general | solution.py:16
  (6 shorter events, 0.1 us)
Async XLA Ops:
  0.7 56.9 %copy-start.1 = (f32[1,256]{1,0:T(1,128)S(1)}, f32[1,256]{1,0:T(1,128)}, u32[]{:S(2)}) copy-start(f32[1,256]{1,0:T(1,128)} %param.3) | copy-start | bytes 3076
  5.7 49.7 %collective-permute-start.1 = (f32[2048,256]{1,0:T(8,128)}, f32[2048,256]{1,0:T(8,128)}, u32[]{:S(2)}, u32[]{:S(2)}) collective-permute-start(f32[2048,256]{1,0:T(8,128)} %get-tuple-element.11), channel_id=1, source_target_pairs={{0,8},{8,0},{16,24},{24,16},{1,9},{9,1},{17,25},{25,17},{2,10},{10... | collective-permute-start | bytes 6291464 | tf_op jit(solution)/shard_map/ppermute | solution.py:104
  8.7 48.9 %collective-permute-start.2 = (f32[2048,256]{1,0:T(8,128)}, f32[2048,256]{1,0:T(8,128)}, u32[]{:S(2)}, u32[]{:S(2)}) collective-permute-start(f32[2048,256]{1,0:T(8,128)} %get-tuple-element.12), channel_id=1, source_target_pairs={{0,16},{8,24},{16,0},{24,8},{1,17},{9,25},{17,1},{25,9},{2,18},{10... | collective-permute-start | bytes 6291464 | tf_op jit(solution)/shard_map/ppermute | solution.py:104
  10.2 90.2 %collective-permute-start = (f32[2048,256]{1,0:T(8,128)}, f32[2048,256]{1,0:T(8,128)}, u32[]{:S(2)}, u32[]{:S(2)}) collective-permute-start(f32[2048,256]{1,0:T(8,128)} %get-tuple-element.10), channel_id=1, source_target_pairs={{0,8},{8,0},{16,24},{24,16},{1,9},{9,1},{17,25},{25,17},{2,10},{10... | collective-permute-start | bytes 6291464 | tf_op jit(solution)/shard_map/ppermute | solution.py:104
  10.7 91.8 %collective-permute-start.4 = (f32[2048,256]{1,0:T(8,128)S(1)}, f32[2048,256]{1,0:T(8,128)}, u32[]{:S(2)}, u32[]{:S(2)}) collective-permute-start(f32[2048,256]{1,0:T(8,128)S(1)} %get-tuple-element.14), channel_id=1, source_target_pairs={{0,16},{8,24},{16,0},{24,8},{1,17},{9,25},{17,1},{25,9},{2,18},{10... | collective-permute-start | bytes 6291464 | tf_op jit(solution)/shard_map/ppermute | solution.py:104
  62.9 83.1 %collective-permute-start.3 = (f32[2048,256]{1,0:T(8,128)}, f32[2048,256]{1,0:T(8,128)}, u32[]{:S(2)}, u32[]{:S(2)}) collective-permute-start(f32[2048,256]{1,0:T(8,128)} %get-tuple-element.13), channel_id=1, source_target_pairs={{0,16},{8,24},{16,0},{24,8},{1,17},{9,25},{17,1},{25,9},{2,18},{10... | collective-permute-start | bytes 6291464 | tf_op jit(solution)/shard_map/ppermute | solution.py:104
  64.4 81.6 %collective-permute-start.5 = (f32[2048,256]{1,0:T(8,128)}, f32[2048,256]{1,0:T(8,128)}, u32[]{:S(2)}, u32[]{:S(2)}) collective-permute-start(f32[2048,256]{1,0:T(8,128)} %get-tuple-element.15), channel_id=1, source_target_pairs={{0,8},{8,0},{16,24},{24,16},{1,9},{9,1},{17,25},{25,17},{2,10},{10... | collective-permute-start | bytes 6291464 | tf_op jit(solution)/shard_map/ppermute | solution.py:104
  150.7 1.3 copy-start
  152.6 1.5 collective-permute-start.6
  154.1 7.0 %collective-permute-start.7 = (f32[384,128]{1,0:T(8,128)S(1)}, f32[384,128]{1,0:T(8,128)S(1)}, u32[]{:S(2)}, u32[]{:S(2)}) collective-permute-start(f32[384,128]{1,0:T(8,128)S(1)} %fusion.16), channel_id=1, source_target_pairs={{0,2},{1,3},{2,0},{3,1},{4,6},{5,7},{6,4},{7,5},{8,10},{9,11},{10,... | collective-permute-start | bytes 589832 | tf_op jit(solution)/shard_map/ppermute | solution.py:24
  161.2 11.3 %collective-permute-start.8 = (f32[384,128]{1,0:T(8,128)S(1)}, f32[384,128]{1,0:T(8,128)S(1)}, u32[]{:S(2)}, u32[]{:S(2)}) collective-permute-start(f32[384,128]{1,0:T(8,128)S(1)} %add.122), channel_id=1, source_target_pairs={{0,4},{1,5},{2,6},{3,7},{4,0},{5,1},{6,2},{7,3},{8,12},{9,13},{10,... | collective-permute-start | bytes 589832 | tf_op jit(solution)/shard_map/ppermute | solution.py:24
  172.5 5.8 %collective-permute-start.9 = (f32[384,128]{1,0:T(8,128)S(1)}, f32[384,128]{1,0:T(8,128)S(1)}, u32[]{:S(2)}, u32[]{:S(2)}) collective-permute-start(f32[384,128]{1,0:T(8,128)S(1)} %add.123), channel_id=1, source_target_pairs={{0,8},{1,9},{2,10},{3,11},{4,12},{5,13},{6,14},{7,15},{8,0},{9,1},... | collective-permute-start | bytes 589832 | tf_op jit(solution)/shard_map/ppermute | solution.py:24
  178.3 5.7 %collective-permute-start.10 = (f32[384,128]{1,0:T(8,128)S(1)}, f32[384,128]{1,0:T(8,128)S(1)}, u32[]{:S(2)}, u32[]{:S(2)}) collective-permute-start(f32[384,128]{1,0:T(8,128)S(1)} %add.124), channel_id=1, source_target_pairs={{0,16},{1,17},{2,18},{3,19},{4,20},{5,21},{6,22},{7,23},{8,24},{9,... | collective-permute-start | bytes 589832 | tf_op jit(solution)/shard_map/ppermute | solution.py:24

commit v14 on v10

--- a/solution.py
+++ b/solution.py
@@ -69,9 +69,15 @@
 def factor_kernel(gram_ref, r_ref, rinv_ref, work):
     h = gram_ref.shape[1]
     g = gram_ref[...]
-    r11, l11i = factor_half(g[:h], work)
+    packed = g[:h]
+    rows = lax.broadcasted_iota(jnp.int32, (h, h), 0)
+    cols = lax.broadcasted_iota(jnp.int32, (h, h), 1)
+    flipped = packed.T
+    g11 = jnp.where(rows <= cols, packed, flipped)
+    g22 = jnp.where(rows < cols, flipped, jnp.where(rows > cols, packed, g[2 * h:2 * h + 1]))
+    r11, l11i = factor_half(g11, work)
     r12 = dot(l11i, g[h:2 * h])
-    schur = g[2 * h:] - dot(r12.T, r12)
+    schur = g22 - dot(r12.T, r12)
     r22, l22i = factor_half(schur, work)
     r11i = l11i.T
     r22i = l22i.T
@@ -148,7 +154,11 @@
     half = mixed.shape[1] // 2
     top = cross_products(mixed[:, :half], mixed)
     bottom = cross_products(mixed[:, half:], mixed[:, half:])
-    blocks = jnp.concatenate([top[:, :half], top[:, half:], bottom], axis=0) / total_rows
+    rows = lax.broadcasted_iota(jnp.int32, (half, half), 0)
+    cols = lax.broadcasted_iota(jnp.int32, (half, half), 1)
+    packed = jnp.where(rows <= cols, top[:, :half], bottom.T)
+    diagonal = jnp.where(rows[:8] == 0, jnp.sum(jnp.where(rows == cols, bottom, 0.0), axis=0, keepdims=True), 0.0)
+    blocks = jnp.concatenate([packed, top[:, half:], diagonal], axis=0) / total_rows
     upper, upper_inv = factor(butterfly_sum(blocks, ("shift", "rows")))
     basis = dot_high(mixed, upper_inv)
     return (basis, upper)

time: 222 us -> 216 us (0.973)
  waiting for transfers between devices: 153 us -> 147 us
    ppermute x5, waiting for transfers between devices: 24.8 us -> 19.4 us  [butterfly_sum(): x = x + lax.ppermute(x, axes, pairs)]
where the time goes in v14:
time: 216 us
  waiting for transfers between devices  147 us (68%)
  Pallas kernels  29.6 us (14%)
  other arithmetic  15.9 us (7%)
  starting transfers between devices  13.5 us (6%)
  matrix products  9.15 us (4%)
    ppermute x6, waiting for transfers between devices, swap(): return lax.ppermute(x, 'shift', [(i, i ^ bit) for i in range(size)])  128 us
    pallas_call x1, Pallas kernels, factor(): pl.pallas_call(factor_kernel, out_shape=(jax.ShapeDtypeStruct((n, n), jnp...  29.6 us
    ppermute x5, waiting for transfers between devices, butterfly_sum(): x = x + lax.ppermute(x, axes, pairs)  19.4 us
    ppermute x6, starting transfers between devices, swap(): return lax.ppermute(x, 'shift', [(i, i ^ bit) for i in range(size)])  7.05 us
    ppermute x5, starting transfers between devices, butterfly_sum(): x = x + lax.ppermute(x, axes, pairs)  6.5 us
    dot_general x1, matrix products, dot_high(): jnp.dot(a, b, precision=lax.Precision.HIGH, preferred_element_type=jnp.fl...  5.42 us
    add x1, other arithmetic, mix_rows(): send_second = part(2 * high + 1 - low, 1) + got_forward_y  5.34 us
    mul x1, other arithmetic, part(): return values.astype(jnp.float32) * scale  5.03 us
  transfers between devices with their start and end apart: 11, of which 10 were waited for; matrix products, arithmetic and copies ran while one was open for 2% of the time, Pallas kernels for 0%

profile of v14, /device:TPU:0, one launch (start us, length us, event | category | flops | bytes accessed | tf_op | source)
XLA Modules:
  0.0 216.2 jit_solution(6818902639910635132)
XLA Ops:
  0.7 0.0 copy-start.1
  0.7 5.0 %convert_multiply_fusion.5 = (f32[2048,256]{1,0:T(8,128)S(1)}, f32[2048,256]{1,0:T(8,128)}, f32[2048,256]{1,0:T(8,128)}, f32[2048,256]{1,0:T(8,128)}) fusion(bf16[1,16384,256]{2,1,0:T(8,128)(2,1)} %param.2, s32[]{:T(128)S(6)} %select_n.51, f32[256]{0:T(256)} %bitcast.28, s32[]{:T(128)S(6)} %select_n.54, s32[]{:T(128)S(6)} %select_n.53, s32[]{:T(128)S(6)} %select_n.50), kind=kLoop, calls=%fused_computation.19 | loop fusion | flops 4194304 | bytes 12583952 | tf_op jit(solution)/shard_map/mul | solution.py:127
  5.7 2.9 %collective-permute-start.1 = (f32[2048,256]{1,0:T(8,128)}, f32[2048,256]{1,0:T(8,128)}, u32[]{:S(2)}, u32[]{:S(2)}) collective-permute-start(f32[2048,256]{1,0:T(8,128)} %get-tuple-element.11), channel_id=1, source_target_pairs={{0,8},{8,0},{16,24},{24,16},{1,9},{9,1},{17,25},{25,17},{2,10},{10... | collective-permute-start | bytes 6291464 | tf_op jit(solution)/shard_map/ppermute | solution.py:110
  8.7 1.5 collective-permute-start.2
  10.2 0.5 collective-permute-start
  10.7 0.0 collective-permute-start.4
  10.7 44.7 %collective-permute-done.1 = f32[2048,256]{1,0:T(8,128)} collective-permute-done((f32[2048,256]{1,0:T(8,128)}, f32[2048,256]{1,0:T(8,128)}, u32[]{:S(2)}, u32[]{:S(2)}) %collective-permute-start.1) | collective-permute-done | bytes 2097184 | tf_op jit(solution)/shard_map/ppermute | solution.py:110
  55.4 2.1 collective-permute-done.2
  57.5 0.0 copy-done.1
  57.5 5.3 %fusion.9 = (f32[2048,256]{1,0:T(8,128)}, f32[2048,256]{1,0:T(8,128)}) fusion(f32[2048,256]{1,0:T(8,128)} %collective-permute-done.2, bf16[1,16384,256]{2,1,0:T(8,128)(2,1)} %param.2, s32[]{:T(128)S(6)} %select_n.55, f32[256]{0:T(256)S(1)} %bitcast.29, f32[2048,256]{1,0:T(8,128)} %collective-permute-done.1, s32[]{:T(128)S(6)} %select_n.52), kind=kLoop, calls=%fused_computation.14 | loop fusion | flops 3145728 | bytes 10486792 | tf_op jit(solution)/shard_map/add | solution.py:138
  62.9 1.5 collective-permute-start.3
  64.4 0.5 collective-permute-start.5
  64.9 35.4 %collective-permute-done = f32[2048,256]{1,0:T(8,128)} collective-permute-done((f32[2048,256]{1,0:T(8,128)}, f32[2048,256]{1,0:T(8,128)}, u32[]{:S(2)}, u32[]{:S(2)}) %collective-permute-start) | collective-permute-done | bytes 2097184 | tf_op jit(solution)/shard_map/ppermute | solution.py:110
  100.4 2.1 collective-permute-done.4
  102.5 43.5 %collective-permute-done.3 = f32[2048,256]{1,0:T(8,128)} collective-permute-done((f32[2048,256]{1,0:T(8,128)}, f32[2048,256]{1,0:T(8,128)}, u32[]{:S(2)}, u32[]{:S(2)}) %collective-permute-start.3) | collective-permute-done | bytes 2097184 | tf_op jit(solution)/shard_map/ppermute | solution.py:110
  146.0 0.0 collective-permute-done.5
  146.0 4.7 %fusion.8 = (f32[2048,256]{1,0:T(8,128)S(1)}, f32[2048,256]{1,0:T(8,128)S(1)}) fusion(f32[2048,256]{1,0:T(8,128)} %collective-permute-done.5, f32[2048,256]{1,0:T(8,128)} %collective-permute-done.4, bf16[1,16384,256]{2,1,0:T(8,128)(2,1)} %param.2, s32[]{:T(128)S(6)} %select_n.56, f32[256]{0:T(256)S(1)} %bitcast.30, f32[2048,256]{1,0:T(8,128)} %collective-permute-done.3, ...), kind=kLoop, calls=%fused_computation.12 | loop fusion | flops 4194304 | bytes 14681096 | tf_op jit(solution)/shard_map/add | solution.py:142
  150.7 0.0 copy-start
  150.7 1.9 select_reduce_fusion
  152.6 0.0 copy-done
  152.6 1.8 fusion
  154.5 0.1 collective-permute-start.6
  154.6 1.3 collective-permute-done.6
  156.0 1.6 collective-permute-start.7
  157.6 4.1 %collective-permute-done.7 = f32[264,128]{1,0:T(8,128)S(1)} collective-permute-done((f32[264,128]{1,0:T(8,128)S(1)}, f32[264,128]{1,0:T(8,128)S(1)}, u32[]{:S(2)}, u32[]{:S(2)}) %collective-permute-start.7) | collective-permute-done | bytes 135200 | tf_op jit(solution)/shard_map/ppermute | solution.py:24
  161.7 2.7 %collective-permute-start.8 = (f32[264,128]{1,0:T(8,128)S(1)}, f32[264,128]{1,0:T(8,128)S(1)}, u32[]{:S(2)}, u32[]{:S(2)}) collective-permute-start(f32[264,128]{1,0:T(8,128)S(1)} %add.122), channel_id=1, source_target_pairs={{0,4},{1,5},{2,6},{3,7},{4,0},{5,1},{6,2},{7,3},{8,12},{9,13},{10,... | collective-permute-start | bytes 405512 | tf_op jit(solution)/shard_map/ppermute | solution.py:24
  164.3 6.0 %collective-permute-done.8 = f32[264,128]{1,0:T(8,128)S(1)} collective-permute-done((f32[264,128]{1,0:T(8,128)S(1)}, f32[264,128]{1,0:T(8,128)S(1)}, u32[]{:S(2)}, u32[]{:S(2)}) %collective-permute-start.8) | collective-permute-done | bytes 135200 | tf_op jit(solution)/shard_map/ppermute | solution.py:24
  170.4 0.5 collective-permute-start.9
  170.9 4.5 %collective-permute-done.9 = f32[264,128]{1,0:T(8,128)S(1)} collective-permute-done((f32[264,128]{1,0:T(8,128)S(1)}, f32[264,128]{1,0:T(8,128)S(1)}, u32[]{:S(2)}, u32[]{:S(2)}) %collective-permute-start.9) | collective-permute-done | bytes 135200 | tf_op jit(solution)/shard_map/ppermute | solution.py:24
  175.5 1.6 collective-permute-start.10
  177.1 3.5 %collective-permute-done.10 = f32[264,128]{1,0:T(8,128)S(1)} collective-permute-done((f32[264,128]{1,0:T(8,128)S(1)}, f32[264,128]{1,0:T(8,128)S(1)}, u32[]{:S(2)}, u32[]{:S(2)}) %collective-permute-start.10) | collective-permute-done | bytes 135200 | tf_op jit(solution)/shard_map/ppermute | solution.py:24
  180.6 0.7 add.125.gram_ref
  181.2 29.6 %shard_map.41 = (f32[256,256]{1,0:T(8,128)}, f32[256,256]{1,0:T(8,128)}) custom-call(f32[264,128]{1,0:T(8,128)} %add.125.gram_ref), custom_call_target="tpu_custom_call" | custom-call | tf_op jit(solution)/shard_map/pallas_call | solution.py:99
  210.8 5.4 %fusion.1 = f32[4096,256]{1,0:T(8,128)} fusion(f32[256,256]{1,0:T(8,128)} %get-tuple-element.16, f32[2048,256]{1,0:T(8,128)S(1)} %get-tuple-element.18, f32[2048,256]{1,0:T(8,128)} %copy-done), kind=kOutput, calls=%fused_computation.6 | convolution fusion | flops 1611661312 | bytes 8650752 | tf_op jit(solution)/shard_map/dot_general | solution.py:16
  (7 shorter events, 0.1 us)
Async XLA Ops:
  0.7 56.9 %copy-start.1 = (f32[1,256]{1,0:T(1,128)S(1)}, f32[1,256]{1,0:T(1,128)}, u32[]{:S(2)}) copy-start(f32[1,256]{1,0:T(1,128)} %param.3) | copy-start | bytes 3076
  5.7 49.7 %collective-permute-start.1 = (f32[2048,256]{1,0:T(8,128)}, f32[2048,256]{1,0:T(8,128)}, u32[]{:S(2)}, u32[]{:S(2)}) collective-permute-start(f32[2048,256]{1,0:T(8,128)} %get-tuple-element.11), channel_id=1, source_target_pairs={{0,8},{8,0},{16,24},{24,16},{1,9},{9,1},{17,25},{25,17},{2,10},{10... | collective-permute-start | bytes 6291464 | tf_op jit(solution)/shard_map/ppermute | solution.py:110
  8.7 48.9 %collective-permute-start.2 = (f32[2048,256]{1,0:T(8,128)}, f32[2048,256]{1,0:T(8,128)}, u32[]{:S(2)}, u32[]{:S(2)}) collective-permute-start(f32[2048,256]{1,0:T(8,128)} %get-tuple-element.12), channel_id=1, source_target_pairs={{0,16},{8,24},{16,0},{24,8},{1,17},{9,25},{17,1},{25,9},{2,18},{10... | collective-permute-start | bytes 6291464 | tf_op jit(solution)/shard_map/ppermute | solution.py:110
  10.2 90.2 %collective-permute-start = (f32[2048,256]{1,0:T(8,128)}, f32[2048,256]{1,0:T(8,128)}, u32[]{:S(2)}, u32[]{:S(2)}) collective-permute-start(f32[2048,256]{1,0:T(8,128)} %get-tuple-element.10), channel_id=1, source_target_pairs={{0,8},{8,0},{16,24},{24,16},{1,9},{9,1},{17,25},{25,17},{2,10},{10... | collective-permute-start | bytes 6291464 | tf_op jit(solution)/shard_map/ppermute | solution.py:110
  10.7 91.8 %collective-permute-start.4 = (f32[2048,256]{1,0:T(8,128)S(1)}, f32[2048,256]{1,0:T(8,128)}, u32[]{:S(2)}, u32[]{:S(2)}) collective-permute-start(f32[2048,256]{1,0:T(8,128)S(1)} %get-tuple-element.14), channel_id=1, source_target_pairs={{0,16},{8,24},{16,0},{24,8},{1,17},{9,25},{17,1},{25,9},{2,18},{10... | collective-permute-start | bytes 6291464 | tf_op jit(solution)/shard_map/ppermute | solution.py:110
  62.9 83.1 %collective-permute-start.3 = (f32[2048,256]{1,0:T(8,128)}, f32[2048,256]{1,0:T(8,128)}, u32[]{:S(2)}, u32[]{:S(2)}) collective-permute-start(f32[2048,256]{1,0:T(8,128)} %get-tuple-element.13), channel_id=1, source_target_pairs={{0,16},{8,24},{16,0},{24,8},{1,17},{9,25},{17,1},{25,9},{2,18},{10... | collective-permute-start | bytes 6291464 | tf_op jit(solution)/shard_map/ppermute | solution.py:110
  64.4 81.6 %collective-permute-start.5 = (f32[2048,256]{1,0:T(8,128)}, f32[2048,256]{1,0:T(8,128)}, u32[]{:S(2)}, u32[]{:S(2)}) collective-permute-start(f32[2048,256]{1,0:T(8,128)} %get-tuple-element.15), channel_id=1, source_target_pairs={{0,8},{8,0},{16,24},{24,16},{1,9},{9,1},{17,25},{25,17},{2,10},{10... | collective-permute-start | bytes 6291464 | tf_op jit(solution)/shard_map/ppermute | solution.py:110
  150.7 1.9 copy-start
  154.5 1.4 collective-permute-start.6
  156.0 5.7 %collective-permute-start.7 = (f32[264,128]{1,0:T(8,128)S(1)}, f32[264,128]{1,0:T(8,128)S(1)}, u32[]{:S(2)}, u32[]{:S(2)}) collective-permute-start(f32[264,128]{1,0:T(8,128)S(1)} %fusion.17), channel_id=1, source_target_pairs={{0,2},{1,3},{2,0},{3,1},{4,6},{5,7},{6,4},{7,5},{8,10},{9,11},{10,... | collective-permute-start | bytes 405512 | tf_op jit(solution)/shard_map/ppermute | solution.py:24
  161.7 8.7 %collective-permute-start.8 = (f32[264,128]{1,0:T(8,128)S(1)}, f32[264,128]{1,0:T(8,128)S(1)}, u32[]{:S(2)}, u32[]{:S(2)}) collective-permute-start(f32[264,128]{1,0:T(8,128)S(1)} %add.122), channel_id=1, source_target_pairs={{0,4},{1,5},{2,6},{3,7},{4,0},{5,1},{6,2},{7,3},{8,12},{9,13},{10,... | collective-permute-start | bytes 405512 | tf_op jit(solution)/shard_map/ppermute | solution.py:24
  170.4 5.1 %collective-permute-start.9 = (f32[264,128]{1,0:T(8,128)S(1)}, f32[264,128]{1,0:T(8,128)S(1)}, u32[]{:S(2)}, u32[]{:S(2)}) collective-permute-start(f32[264,128]{1,0:T(8,128)S(1)} %add.123), channel_id=1, source_target_pairs={{0,8},{1,9},{2,10},{3,11},{4,12},{5,13},{6,14},{7,15},{8,0},{9,1},... | collective-permute-start | bytes 405512 | tf_op jit(solution)/shard_map/ppermute | solution.py:24
  175.5 5.1 %collective-permute-start.10 = (f32[264,128]{1,0:T(8,128)S(1)}, f32[264,128]{1,0:T(8,128)S(1)}, u32[]{:S(2)}, u32[]{:S(2)}) collective-permute-start(f32[264,128]{1,0:T(8,128)S(1)} %add.124), channel_id=1, source_target_pairs={{0,16},{1,17},{2,18},{3,19},{4,20},{5,21},{6,22},{7,23},{8,24},{9,... | collective-permute-start | bytes 405512 | tf_op jit(solution)/shard_map/ppermute | solution.py:24

commit v15 on v14

--- a/solution.py
+++ b/solution.py
@@ -62,7 +62,7 @@
     upper = jnp.concatenate([r11 + r12, pltpu.roll(r22, m, 1)], axis=0)
     first = jnp.concatenate([l11i, zeros], axis=0)
     second = jnp.concatenate([zeros, l22i_high], axis=0)
-    inverse = first + second - dot(dot(second, r12_full.T), first)
+    inverse = first + second - dot(second, dot(r12_full.T, first))
     return upper, inverse
 
 
@@ -78,10 +78,11 @@
     r11, l11i = factor_half(g11, work)
     r12 = dot(l11i, g[h:2 * h])
     schur = g22 - dot(r12.T, r12)
+    r11i = l11i.T
+    head = dot(r11i, r12)
     r22, l22i = factor_half(schur, work)
-    r11i = l11i.T
     r22i = l22i.T
-    rinv12 = -dot(dot(r11i, r12), r22i)
+    rinv12 = -dot(head, r22i)
     zero = jnp.zeros((h, h), jnp.float32)
     r_ref[:h, :h] = r11
     r_ref[:h, h:] = r12

time: 216 us -> 216 us (level)
  no operation moved by 1% of the time
where the time goes in v15:
time: 216 us
  waiting for transfers between devices  147 us (68%)
  Pallas kernels  29.2 us (14%)
  other arithmetic  15.9 us (7%)
  starting transfers between devices  13.5 us (6%)
  matrix products  9.15 us (4%)
    ppermute x6, waiting for transfers between devices, swap(): return lax.ppermute(x, 'shift', [(i, i ^ bit) for i in range(size)])  128 us
    pallas_call x1, Pallas kernels, factor(): pl.pallas_call(factor_kernel, out_shape=(jax.ShapeDtypeStruct((n, n), jnp...  29.2 us
    ppermute x5, waiting for transfers between devices, butterfly_sum(): x = x + lax.ppermute(x, axes, pairs)  19.4 us
    ppermute x6, starting transfers between devices, swap(): return lax.ppermute(x, 'shift', [(i, i ^ bit) for i in range(size)])  7.05 us
    ppermute x5, starting transfers between devices, butterfly_sum(): x = x + lax.ppermute(x, axes, pairs)  6.5 us
    dot_general x1, matrix products, dot_high(): jnp.dot(a, b, precision=lax.Precision.HIGH, preferred_element_type=jnp.fl...  5.42 us
    add x1, other arithmetic, mix_rows(): send_second = part(2 * high + 1 - low, 1) + got_forward_y  5.34 us
    mul x1, other arithmetic, part(): return values.astype(jnp.float32) * scale  5.03 us
  transfers between devices with their start and end apart: 11, of which 10 were waited for; matrix products, arithmetic and copies ran while one was open for 2% of the time, Pallas kernels for 0%

profile of v15, /device:TPU:0, one launch (start us, length us, event | category | flops | bytes accessed | tf_op | source)
XLA Modules:
  0.0 215.8 jit_solution(13920798152407634545)
XLA Ops:
  0.7 0.0 copy-start.1
  0.7 5.0 %convert_multiply_fusion.5 = (f32[2048,256]{1,0:T(8,128)S(1)}, f32[2048,256]{1,0:T(8,128)}, f32[2048,256]{1,0:T(8,128)}, f32[2048,256]{1,0:T(8,128)}) fusion(bf16[1,16384,256]{2,1,0:T(8,128)(2,1)} %param.2, s32[]{:T(128)S(6)} %select_n.51, f32[256]{0:T(256)} %bitcast.28, s32[]{:T(128)S(6)} %select_n.54, s32[]{:T(128)S(6)} %select_n.53, s32[]{:T(128)S(6)} %select_n.50), kind=kLoop, calls=%fused_computation.19 | loop fusion | flops 4194304 | bytes 12583952 | tf_op jit(solution)/shard_map/mul | solution.py:128
  5.7 2.9 %collective-permute-start.1 = (f32[2048,256]{1,0:T(8,128)}, f32[2048,256]{1,0:T(8,128)}, u32[]{:S(2)}, u32[]{:S(2)}) collective-permute-start(f32[2048,256]{1,0:T(8,128)} %get-tuple-element.11), channel_id=1, source_target_pairs={{0,8},{8,0},{16,24},{24,16},{1,9},{9,1},{17,25},{25,17},{2,10},{10... | collective-permute-start | bytes 6291464 | tf_op jit(solution)/shard_map/ppermute | solution.py:111
  8.7 1.5 collective-permute-start.2
  10.2 0.5 collective-permute-start
  10.7 0.0 collective-permute-start.4
  10.7 44.7 %collective-permute-done.1 = f32[2048,256]{1,0:T(8,128)} collective-permute-done((f32[2048,256]{1,0:T(8,128)}, f32[2048,256]{1,0:T(8,128)}, u32[]{:S(2)}, u32[]{:S(2)}) %collective-permute-start.1) | collective-permute-done | bytes 2097184 | tf_op jit(solution)/shard_map/ppermute | solution.py:111
  55.4 2.1 collective-permute-done.2
  57.5 0.0 copy-done.1
  57.5 5.3 %fusion.9 = (f32[2048,256]{1,0:T(8,128)}, f32[2048,256]{1,0:T(8,128)}) fusion(f32[2048,256]{1,0:T(8,128)} %collective-permute-done.2, bf16[1,16384,256]{2,1,0:T(8,128)(2,1)} %param.2, s32[]{:T(128)S(6)} %select_n.55, f32[256]{0:T(256)S(1)} %bitcast.29, f32[2048,256]{1,0:T(8,128)} %collective-permute-done.1, s32[]{:T(128)S(6)} %select_n.52), kind=kLoop, calls=%fused_computation.14 | loop fusion | flops 3145728 | bytes 10486792 | tf_op jit(solution)/shard_map/add | solution.py:139
  62.9 1.5 collective-permute-start.3
  64.4 0.5 collective-permute-start.5
  64.9 35.4 %collective-permute-done = f32[2048,256]{1,0:T(8,128)} collective-permute-done((f32[2048,256]{1,0:T(8,128)}, f32[2048,256]{1,0:T(8,128)}, u32[]{:S(2)}, u32[]{:S(2)}) %collective-permute-start) | collective-permute-done | bytes 2097184 | tf_op jit(solution)/shard_map/ppermute | solution.py:111
  100.4 2.1 collective-permute-done.4
  102.5 43.5 %collective-permute-done.3 = f32[2048,256]{1,0:T(8,128)} collective-permute-done((f32[2048,256]{1,0:T(8,128)}, f32[2048,256]{1,0:T(8,128)}, u32[]{:S(2)}, u32[]{:S(2)}) %collective-permute-start.3) | collective-permute-done | bytes 2097184 | tf_op jit(solution)/shard_map/ppermute | solution.py:111
  146.0 0.0 collective-permute-done.5
  146.0 4.7 %fusion.8 = (f32[2048,256]{1,0:T(8,128)S(1)}, f32[2048,256]{1,0:T(8,128)S(1)}) fusion(f32[2048,256]{1,0:T(8,128)} %collective-permute-done.5, f32[2048,256]{1,0:T(8,128)} %collective-permute-done.4, bf16[1,16384,256]{2,1,0:T(8,128)(2,1)} %param.2, s32[]{:T(128)S(6)} %select_n.56, f32[256]{0:T(256)S(1)} %bitcast.30, f32[2048,256]{1,0:T(8,128)} %collective-permute-done.3, ...), kind=kLoop, calls=%fused_computation.12 | loop fusion | flops 4194304 | bytes 14681096 | tf_op jit(solution)/shard_map/add | solution.py:143
  150.7 0.0 copy-start
  150.7 1.9 select_reduce_fusion
  152.6 0.0 copy-done
  152.6 1.8 fusion
  154.5 0.1 collective-permute-start.6
  154.6 1.3 collective-permute-done.6
  156.0 1.6 collective-permute-start.7
  157.6 4.1 %collective-permute-done.7 = f32[264,128]{1,0:T(8,128)S(1)} collective-permute-done((f32[264,128]{1,0:T(8,128)S(1)}, f32[264,128]{1,0:T(8,128)S(1)}, u32[]{:S(2)}, u32[]{:S(2)}) %collective-permute-start.7) | collective-permute-done | bytes 135200 | tf_op jit(solution)/shard_map/ppermute | solution.py:24
  161.7 2.7 %collective-permute-start.8 = (f32[264,128]{1,0:T(8,128)S(1)}, f32[264,128]{1,0:T(8,128)S(1)}, u32[]{:S(2)}, u32[]{:S(2)}) collective-permute-start(f32[264,128]{1,0:T(8,128)S(1)} %add.122), channel_id=1, source_target_pairs={{0,4},{1,5},{2,6},{3,7},{4,0},{5,1},{6,2},{7,3},{8,12},{9,13},{10,... | collective-permute-start | bytes 405512 | tf_op jit(solution)/shard_map/ppermute | solution.py:24
  164.3 6.0 %collective-permute-done.8 = f32[264,128]{1,0:T(8,128)S(1)} collective-permute-done((f32[264,128]{1,0:T(8,128)S(1)}, f32[264,128]{1,0:T(8,128)S(1)}, u32[]{:S(2)}, u32[]{:S(2)}) %collective-permute-start.8) | collective-permute-done | bytes 135200 | tf_op jit(solution)/shard_map/ppermute | solution.py:24
  170.4 0.5 collective-permute-start.9
  170.9 4.5 %collective-permute-done.9 = f32[264,128]{1,0:T(8,128)S(1)} collective-permute-done((f32[264,128]{1,0:T(8,128)S(1)}, f32[264,128]{1,0:T(8,128)S(1)}, u32[]{:S(2)}, u32[]{:S(2)}) %collective-permute-start.9) | collective-permute-done | bytes 135200 | tf_op jit(solution)/shard_map/ppermute | solution.py:24
  175.5 1.6 collective-permute-start.10
  177.1 3.5 %collective-permute-done.10 = f32[264,128]{1,0:T(8,128)S(1)} collective-permute-done((f32[264,128]{1,0:T(8,128)S(1)}, f32[264,128]{1,0:T(8,128)S(1)}, u32[]{:S(2)}, u32[]{:S(2)}) %collective-permute-start.10) | collective-permute-done | bytes 135200 | tf_op jit(solution)/shard_map/ppermute | solution.py:24
  180.6 0.7 add.125.gram_ref
  181.2 29.2 %shard_map.41 = (f32[256,256]{1,0:T(8,128)}, f32[256,256]{1,0:T(8,128)}) custom-call(f32[264,128]{1,0:T(8,128)} %add.125.gram_ref), custom_call_target="tpu_custom_call" | custom-call | tf_op jit(solution)/shard_map/pallas_call | solution.py:100
  210.4 5.4 %fusion.1 = f32[4096,256]{1,0:T(8,128)} fusion(f32[256,256]{1,0:T(8,128)} %get-tuple-element.16, f32[2048,256]{1,0:T(8,128)S(1)} %get-tuple-element.18, f32[2048,256]{1,0:T(8,128)} %copy-done), kind=kOutput, calls=%fused_computation.6 | convolution fusion | flops 1611661312 | bytes 8650752 | tf_op jit(solution)/shard_map/dot_general | solution.py:16
  (7 shorter events, 0.1 us)
Async XLA Ops:
  0.7 56.9 %copy-start.1 = (f32[1,256]{1,0:T(1,128)S(1)}, f32[1,256]{1,0:T(1,128)}, u32[]{:S(2)}) copy-start(f32[1,256]{1,0:T(1,128)} %param.3) | copy-start | bytes 3076
  5.7 49.7 %collective-permute-start.1 = (f32[2048,256]{1,0:T(8,128)}, f32[2048,256]{1,0:T(8,128)}, u32[]{:S(2)}, u32[]{:S(2)}) collective-permute-start(f32[2048,256]{1,0:T(8,128)} %get-tuple-element.11), channel_id=1, source_target_pairs={{0,8},{8,0},{16,24},{24,16},{1,9},{9,1},{17,25},{25,17},{2,10},{10... | collective-permute-start | bytes 6291464 | tf_op jit(solution)/shard_map/ppermute | solution.py:111
  8.7 48.9 %collective-permute-start.2 = (f32[2048,256]{1,0:T(8,128)}, f32[2048,256]{1,0:T(8,128)}, u32[]{:S(2)}, u32[]{:S(2)}) collective-permute-start(f32[2048,256]{1,0:T(8,128)} %get-tuple-element.12), channel_id=1, source_target_pairs={{0,16},{8,24},{16,0},{24,8},{1,17},{9,25},{17,1},{25,9},{2,18},{10... | collective-permute-start | bytes 6291464 | tf_op jit(solution)/shard_map/ppermute | solution.py:111
  10.2 90.2 %collective-permute-start = (f32[2048,256]{1,0:T(8,128)}, f32[2048,256]{1,0:T(8,128)}, u32[]{:S(2)}, u32[]{:S(2)}) collective-permute-start(f32[2048,256]{1,0:T(8,128)} %get-tuple-element.10), channel_id=1, source_target_pairs={{0,8},{8,0},{16,24},{24,16},{1,9},{9,1},{17,25},{25,17},{2,10},{10... | collective-permute-start | bytes 6291464 | tf_op jit(solution)/shard_map/ppermute | solution.py:111
  10.7 91.8 %collective-permute-start.4 = (f32[2048,256]{1,0:T(8,128)S(1)}, f32[2048,256]{1,0:T(8,128)}, u32[]{:S(2)}, u32[]{:S(2)}) collective-permute-start(f32[2048,256]{1,0:T(8,128)S(1)} %get-tuple-element.14), channel_id=1, source_target_pairs={{0,16},{8,24},{16,0},{24,8},{1,17},{9,25},{17,1},{25,9},{2,18},{10... | collective-permute-start | bytes 6291464 | tf_op jit(solution)/shard_map/ppermute | solution.py:111
  62.9 83.1 %collective-permute-start.3 = (f32[2048,256]{1,0:T(8,128)}, f32[2048,256]{1,0:T(8,128)}, u32[]{:S(2)}, u32[]{:S(2)}) collective-permute-start(f32[2048,256]{1,0:T(8,128)} %get-tuple-element.13), channel_id=1, source_target_pairs={{0,16},{8,24},{16,0},{24,8},{1,17},{9,25},{17,1},{25,9},{2,18},{10... | collective-permute-start | bytes 6291464 | tf_op jit(solution)/shard_map/ppermute | solution.py:111
  64.4 81.6 %collective-permute-start.5 = (f32[2048,256]{1,0:T(8,128)}, f32[2048,256]{1,0:T(8,128)}, u32[]{:S(2)}, u32[]{:S(2)}) collective-permute-start(f32[2048,256]{1,0:T(8,128)} %get-tuple-element.15), channel_id=1, source_target_pairs={{0,8},{8,0},{16,24},{24,16},{1,9},{9,1},{17,25},{25,17},{2,10},{10... | collective-permute-start | bytes 6291464 | tf_op jit(solution)/shard_map/ppermute | solution.py:111
  150.7 1.9 copy-start
  154.5 1.4 collective-permute-start.6
  156.0 5.7 %collective-permute-start.7 = (f32[264,128]{1,0:T(8,128)S(1)}, f32[264,128]{1,0:T(8,128)S(1)}, u32[]{:S(2)}, u32[]{:S(2)}) collective-permute-start(f32[264,128]{1,0:T(8,128)S(1)} %fusion.17), channel_id=1, source_target_pairs={{0,2},{1,3},{2,0},{3,1},{4,6},{5,7},{6,4},{7,5},{8,10},{9,11},{10,... | collective-permute-start | bytes 405512 | tf_op jit(solution)/shard_map/ppermute | solution.py:24
  161.7 8.7 %collective-permute-start.8 = (f32[264,128]{1,0:T(8,128)S(1)}, f32[264,128]{1,0:T(8,128)S(1)}, u32[]{:S(2)}, u32[]{:S(2)}) collective-permute-start(f32[264,128]{1,0:T(8,128)S(1)} %add.122), channel_id=1, source_target_pairs={{0,4},{1,5},{2,6},{3,7},{4,0},{5,1},{6,2},{7,3},{8,12},{9,13},{10,... | collective-permute-start | bytes 405512 | tf_op jit(solution)/shard_map/ppermute | solution.py:24
  170.4 5.1 %collective-permute-start.9 = (f32[264,128]{1,0:T(8,128)S(1)}, f32[264,128]{1,0:T(8,128)S(1)}, u32[]{:S(2)}, u32[]{:S(2)}) collective-permute-start(f32[264,128]{1,0:T(8,128)S(1)} %add.123), channel_id=1, source_target_pairs={{0,8},{1,9},{2,10},{3,11},{4,12},{5,13},{6,14},{7,15},{8,0},{9,1},... | collective-permute-start | bytes 405512 | tf_op jit(solution)/shard_map/ppermute | solution.py:24
  175.5 5.1 %collective-permute-start.10 = (f32[264,128]{1,0:T(8,128)S(1)}, f32[264,128]{1,0:T(8,128)S(1)}, u32[]{:S(2)}, u32[]{:S(2)}) collective-permute-start(f32[264,128]{1,0:T(8,128)S(1)} %add.124), channel_id=1, source_target_pairs={{0,16},{1,17},{2,18},{3,19},{4,20},{5,21},{6,22},{7,23},{8,24},{9,... | collective-permute-start | bytes 405512 | tf_op jit(solution)/shard_map/ppermute | solution.py:24

commit v16 on v15

--- a/solution.py
+++ b/solution.py
@@ -39,7 +39,7 @@
     row_index = lax.broadcasted_iota(jnp.int32, (m, 1), 0)
     for j in range(m):
         row = current[j:j + 1, :]
-        scale = 1.0 / jnp.sqrt(row[:, j:j + 1])
+        scale = lax.rsqrt(row[:, j:j + 1])
         scaled = row * scale
         coef = jnp.where(row_index > j, current[:, j:j + 1] * scale, 0.0)
         current = jnp.where(row_index == j, scaled, current - coef * scaled)

time: 216 us -> 213 us (0.986)
  Pallas kernels: 29.2 us -> 25.7 us
    pallas_call x1, Pallas kernels: 29.2 us -> 25.7 us  [factor(): pl.pallas_call(factor_kernel, out_shape=(jax.ShapeDtypeStruct((n, n), jnp...]
  transfers between devices with their start and end apart: 11 -> 11, of which waited for: 10 -> 10; matrix products, arithmetic and copies ran while one was open for 2% -> 3% of each run, Pallas kernels for 0% -> 0%
where the time goes in v16:
time: 213 us; the launch traced here: 212 us
  waiting for transfers between devices  147 us (69%)
  Pallas kernels  25.7 us (12%)
  other arithmetic  15.9 us (7%)
  starting transfers between devices  13.5 us (6%)
  matrix products  9.15 us (4%)
    ppermute x6, waiting for transfers between devices, swap(): return lax.ppermute(x, 'shift', [(i, i ^ bit) for i in range(size)])  128 us
    pallas_call x1, Pallas kernels, factor(): pl.pallas_call(factor_kernel, out_shape=(jax.ShapeDtypeStruct((n, n), jnp...  25.7 us
    ppermute x5, waiting for transfers between devices, butterfly_sum(): x = x + lax.ppermute(x, axes, pairs)  19.4 us
    ppermute x6, starting transfers between devices, swap(): return lax.ppermute(x, 'shift', [(i, i ^ bit) for i in range(size)])  7.05 us
    ppermute x5, starting transfers between devices, butterfly_sum(): x = x + lax.ppermute(x, axes, pairs)  6.5 us
    dot_general x1, matrix products, dot_high(): jnp.dot(a, b, precision=lax.Precision.HIGH, preferred_element_type=jnp.fl...  5.41 us
    add x1, other arithmetic, mix_rows(): send_second = part(2 * high + 1 - low, 1) + got_forward_y  5.34 us
    mul x1, other arithmetic, part(): return values.astype(jnp.float32) * scale  5.03 us
  transfers between devices with their start and end apart: 11, of which 10 were waited for; matrix products, arithmetic and copies ran while one was open for 3% of the time, Pallas kernels for 0%

profile of v16, /device:TPU:0, one launch (start us, length us, event | category | flops | bytes accessed | tf_op | source)
XLA Modules:
  0.0 212.4 jit_solution(13409643169705045606)
XLA Ops:
  0.7 0.0 copy-start.1
  0.7 5.0 %convert_multiply_fusion.5 = (f32[2048,256]{1,0:T(8,128)S(1)}, f32[2048,256]{1,0:T(8,128)}, f32[2048,256]{1,0:T(8,128)}, f32[2048,256]{1,0:T(8,128)}) fusion(bf16[1,16384,256]{2,1,0:T(8,128)(2,1)} %param.2, s32[]{:T(128)S(6)} %select_n.51, f32[256]{0:T(256)} %bitcast.28, s32[]{:T(128)S(6)} %select_n.54, s32[]{:T(128)S(6)} %select_n.53, s32[]{:T(128)S(6)} %select_n.50), kind=kLoop, calls=%fused_computation.19 | loop fusion | flops 4194304 | bytes 12583952 | tf_op jit(solution)/shard_map/mul | solution.py:128
  5.7 2.9 %collective-permute-start.1 = (f32[2048,256]{1,0:T(8,128)}, f32[2048,256]{1,0:T(8,128)}, u32[]{:S(2)}, u32[]{:S(2)}) collective-permute-start(f32[2048,256]{1,0:T(8,128)} %get-tuple-element.11), channel_id=1, source_target_pairs={{0,8},{8,0},{16,24},{24,16},{1,9},{9,1},{17,25},{25,17},{2,10},{10... | collective-permute-start | bytes 6291464 | tf_op jit(solution)/shard_map/ppermute | solution.py:111
  8.7 1.5 collective-permute-start.2
  10.2 0.5 collective-permute-start
  10.7 0.0 collective-permute-start.4
  10.7 44.7 %collective-permute-done.1 = f32[2048,256]{1,0:T(8,128)} collective-permute-done((f32[2048,256]{1,0:T(8,128)}, f32[2048,256]{1,0:T(8,128)}, u32[]{:S(2)}, u32[]{:S(2)}) %collective-permute-start.1) | collective-permute-done | bytes 2097184 | tf_op jit(solution)/shard_map/ppermute | solution.py:111
  55.4 2.1 collective-permute-done.2
  57.5 0.0 copy-done.1
  57.5 5.3 %fusion.9 = (f32[2048,256]{1,0:T(8,128)}, f32[2048,256]{1,0:T(8,128)}) fusion(f32[2048,256]{1,0:T(8,128)} %collective-permute-done.2, bf16[1,16384,256]{2,1,0:T(8,128)(2,1)} %param.2, s32[]{:T(128)S(6)} %select_n.55, f32[256]{0:T(256)S(1)} %bitcast.29, f32[2048,256]{1,0:T(8,128)} %collective-permute-done.1, s32[]{:T(128)S(6)} %select_n.52), kind=kLoop, calls=%fused_computation.14 | loop fusion | flops 3145728 | bytes 10486792 | tf_op jit(solution)/shard_map/add | solution.py:139
  62.9 1.5 collective-permute-start.3
  64.4 0.5 collective-permute-start.5
  64.9 35.4 %collective-permute-done = f32[2048,256]{1,0:T(8,128)} collective-permute-done((f32[2048,256]{1,0:T(8,128)}, f32[2048,256]{1,0:T(8,128)}, u32[]{:S(2)}, u32[]{:S(2)}) %collective-permute-start) | collective-permute-done | bytes 2097184 | tf_op jit(solution)/shard_map/ppermute | solution.py:111
  100.4 2.1 collective-permute-done.4
  102.5 43.5 %collective-permute-done.3 = f32[2048,256]{1,0:T(8,128)} collective-permute-done((f32[2048,256]{1,0:T(8,128)}, f32[2048,256]{1,0:T(8,128)}, u32[]{:S(2)}, u32[]{:S(2)}) %collective-permute-start.3) | collective-permute-done | bytes 2097184 | tf_op jit(solution)/shard_map/ppermute | solution.py:111
  146.0 0.0 collective-permute-done.5
  146.0 4.7 %fusion.8 = (f32[2048,256]{1,0:T(8,128)S(1)}, f32[2048,256]{1,0:T(8,128)S(1)}) fusion(f32[2048,256]{1,0:T(8,128)} %collective-permute-done.5, f32[2048,256]{1,0:T(8,128)} %collective-permute-done.4, bf16[1,16384,256]{2,1,0:T(8,128)(2,1)} %param.2, s32[]{:T(128)S(6)} %select_n.56, f32[256]{0:T(256)S(1)} %bitcast.30, f32[2048,256]{1,0:T(8,128)} %collective-permute-done.3, ...), kind=kLoop, calls=%fused_computation.12 | loop fusion | flops 4194304 | bytes 14681096 | tf_op jit(solution)/shard_map/add | solution.py:143
  150.7 0.0 copy-start
  150.7 1.9 select_reduce_fusion
  152.6 0.0 copy-done
  152.6 1.8 fusion
  154.5 0.1 collective-permute-start.6
  154.6 1.3 collective-permute-done.6
  156.0 1.6 collective-permute-start.7
  157.6 4.1 %collective-permute-done.7 = f32[264,128]{1,0:T(8,128)S(1)} collective-permute-done((f32[264,128]{1,0:T(8,128)S(1)}, f32[264,128]{1,0:T(8,128)S(1)}, u32[]{:S(2)}, u32[]{:S(2)}) %collective-permute-start.7) | collective-permute-done | bytes 135200 | tf_op jit(solution)/shard_map/ppermute | solution.py:24
  161.7 2.7 %collective-permute-start.8 = (f32[264,128]{1,0:T(8,128)S(1)}, f32[264,128]{1,0:T(8,128)S(1)}, u32[]{:S(2)}, u32[]{:S(2)}) collective-permute-start(f32[264,128]{1,0:T(8,128)S(1)} %add.122), channel_id=1, source_target_pairs={{0,4},{1,5},{2,6},{3,7},{4,0},{5,1},{6,2},{7,3},{8,12},{9,13},{10,... | collective-permute-start | bytes 405512 | tf_op jit(solution)/shard_map/ppermute | solution.py:24
  164.3 6.0 %collective-permute-done.8 = f32[264,128]{1,0:T(8,128)S(1)} collective-permute-done((f32[264,128]{1,0:T(8,128)S(1)}, f32[264,128]{1,0:T(8,128)S(1)}, u32[]{:S(2)}, u32[]{:S(2)}) %collective-permute-start.8) | collective-permute-done | bytes 135200 | tf_op jit(solution)/shard_map/ppermute | solution.py:24
  170.4 0.5 collective-permute-start.9
  170.9 4.5 %collective-permute-done.9 = f32[264,128]{1,0:T(8,128)S(1)} collective-permute-done((f32[264,128]{1,0:T(8,128)S(1)}, f32[264,128]{1,0:T(8,128)S(1)}, u32[]{:S(2)}, u32[]{:S(2)}) %collective-permute-start.9) | collective-permute-done | bytes 135200 | tf_op jit(solution)/shard_map/ppermute | solution.py:24
  175.5 1.6 collective-permute-start.10
  177.1 3.5 %collective-permute-done.10 = f32[264,128]{1,0:T(8,128)S(1)} collective-permute-done((f32[264,128]{1,0:T(8,128)S(1)}, f32[264,128]{1,0:T(8,128)S(1)}, u32[]{:S(2)}, u32[]{:S(2)}) %collective-permute-start.10) | collective-permute-done | bytes 135200 | tf_op jit(solution)/shard_map/ppermute | solution.py:24
  180.6 0.7 add.125.gram_ref
  181.2 25.7 %shard_map.41 = (f32[256,256]{1,0:T(8,128)}, f32[256,256]{1,0:T(8,128)}) custom-call(f32[264,128]{1,0:T(8,128)} %add.125.gram_ref), custom_call_target="tpu_custom_call" | custom-call | tf_op jit(solution)/shard_map/pallas_call | solution.py:100
  207.0 5.4 %fusion.1 = f32[4096,256]{1,0:T(8,128)} fusion(f32[256,256]{1,0:T(8,128)} %get-tuple-element.16, f32[2048,256]{1,0:T(8,128)S(1)} %get-tuple-element.18, f32[2048,256]{1,0:T(8,128)} %copy-done), kind=kOutput, calls=%fused_computation.6 | convolution fusion | flops 1611661312 | bytes 8650752 | tf_op jit(solution)/shard_map/dot_general | solution.py:16
  (7 shorter events, 0.1 us)
Async XLA Ops:
  0.7 56.9 %copy-start.1 = (f32[1,256]{1,0:T(1,128)S(1)}, f32[1,256]{1,0:T(1,128)}, u32[]{:S(2)}) copy-start(f32[1,256]{1,0:T(1,128)} %param.3) | copy-start | bytes 3076
  5.7 49.7 %collective-permute-start.1 = (f32[2048,256]{1,0:T(8,128)}, f32[2048,256]{1,0:T(8,128)}, u32[]{:S(2)}, u32[]{:S(2)}) collective-permute-start(f32[2048,256]{1,0:T(8,128)} %get-tuple-element.11), channel_id=1, source_target_pairs={{0,8},{8,0},{16,24},{24,16},{1,9},{9,1},{17,25},{25,17},{2,10},{10... | collective-permute-start | bytes 6291464 | tf_op jit(solution)/shard_map/ppermute | solution.py:111
  8.7 48.9 %collective-permute-start.2 = (f32[2048,256]{1,0:T(8,128)}, f32[2048,256]{1,0:T(8,128)}, u32[]{:S(2)}, u32[]{:S(2)}) collective-permute-start(f32[2048,256]{1,0:T(8,128)} %get-tuple-element.12), channel_id=1, source_target_pairs={{0,16},{8,24},{16,0},{24,8},{1,17},{9,25},{17,1},{25,9},{2,18},{10... | collective-permute-start | bytes 6291464 | tf_op jit(solution)/shard_map/ppermute | solution.py:111
  10.2 90.2 %collective-permute-start = (f32[2048,256]{1,0:T(8,128)}, f32[2048,256]{1,0:T(8,128)}, u32[]{:S(2)}, u32[]{:S(2)}) collective-permute-start(f32[2048,256]{1,0:T(8,128)} %get-tuple-element.10), channel_id=1, source_target_pairs={{0,8},{8,0},{16,24},{24,16},{1,9},{9,1},{17,25},{25,17},{2,10},{10... | collective-permute-start | bytes 6291464 | tf_op jit(solution)/shard_map/ppermute | solution.py:111
  10.7 91.8 %collective-permute-start.4 = (f32[2048,256]{1,0:T(8,128)S(1)}, f32[2048,256]{1,0:T(8,128)}, u32[]{:S(2)}, u32[]{:S(2)}) collective-permute-start(f32[2048,256]{1,0:T(8,128)S(1)} %get-tuple-element.14), channel_id=1, source_target_pairs={{0,16},{8,24},{16,0},{24,8},{1,17},{9,25},{17,1},{25,9},{2,18},{10... | collective-permute-start | bytes 6291464 | tf_op jit(solution)/shard_map/ppermute | solution.py:111
  62.9 83.1 %collective-permute-start.3 = (f32[2048,256]{1,0:T(8,128)}, f32[2048,256]{1,0:T(8,128)}, u32[]{:S(2)}, u32[]{:S(2)}) collective-permute-start(f32[2048,256]{1,0:T(8,128)} %get-tuple-element.13), channel_id=1, source_target_pairs={{0,16},{8,24},{16,0},{24,8},{1,17},{9,25},{17,1},{25,9},{2,18},{10... | collective-permute-start | bytes 6291464 | tf_op jit(solution)/shard_map/ppermute | solution.py:111
  64.4 81.6 %collective-permute-start.5 = (f32[2048,256]{1,0:T(8,128)}, f32[2048,256]{1,0:T(8,128)}, u32[]{:S(2)}, u32[]{:S(2)}) collective-permute-start(f32[2048,256]{1,0:T(8,128)} %get-tuple-element.15), channel_id=1, source_target_pairs={{0,8},{8,0},{16,24},{24,16},{1,9},{9,1},{17,25},{25,17},{2,10},{10... | collective-permute-start | bytes 6291464 | tf_op jit(solution)/shard_map/ppermute | solution.py:111
  150.7 1.9 copy-start
  154.5 1.4 collective-permute-start.6
  156.0 5.7 %collective-permute-start.7 = (f32[264,128]{1,0:T(8,128)S(1)}, f32[264,128]{1,0:T(8,128)S(1)}, u32[]{:S(2)}, u32[]{:S(2)}) collective-permute-start(f32[264,128]{1,0:T(8,128)S(1)} %fusion.17), channel_id=1, source_target_pairs={{0,2},{1,3},{2,0},{3,1},{4,6},{5,7},{6,4},{7,5},{8,10},{9,11},{10,... | collective-permute-start | bytes 405512 | tf_op jit(solution)/shard_map/ppermute | solution.py:24
  161.7 8.7 %collective-permute-start.8 = (f32[264,128]{1,0:T(8,128)S(1)}, f32[264,128]{1,0:T(8,128)S(1)}, u32[]{:S(2)}, u32[]{:S(2)}) collective-permute-start(f32[264,128]{1,0:T(8,128)S(1)} %add.122), channel_id=1, source_target_pairs={{0,4},{1,5},{2,6},{3,7},{4,0},{5,1},{6,2},{7,3},{8,12},{9,13},{10,... | collective-permute-start | bytes 405512 | tf_op jit(solution)/shard_map/ppermute | solution.py:24
  170.4 5.1 %collective-permute-start.9 = (f32[264,128]{1,0:T(8,128)S(1)}, f32[264,128]{1,0:T(8,128)S(1)}, u32[]{:S(2)}, u32[]{:S(2)}) collective-permute-start(f32[264,128]{1,0:T(8,128)S(1)} %add.123), channel_id=1, source_target_pairs={{0,8},{1,9},{2,10},{3,11},{4,12},{5,13},{6,14},{7,15},{8,0},{9,1},... | collective-permute-start | bytes 405512 | tf_op jit(solution)/shard_map/ppermute | solution.py:24
  175.5 5.1 %collective-permute-start.10 = (f32[264,128]{1,0:T(8,128)S(1)}, f32[264,128]{1,0:T(8,128)S(1)}, u32[]{:S(2)}, u32[]{:S(2)}) collective-permute-start(f32[264,128]{1,0:T(8,128)S(1)} %add.124), channel_id=1, source_target_pairs={{0,16},{1,17},{2,18},{3,19},{4,20},{5,21},{6,22},{7,23},{8,24},{9,... | collective-permute-start | bytes 405512 | tf_op jit(solution)/shard_map/ppermute | solution.py:24
